TPU v7x, 1024 devices: a whole 4x8x16 slice. The times are simulated.
1024 devices in a mesh: blk: 64 (over z, y_lo, core), head: 16 (over y_hi, x).
Axes of the slice: x: 4, y: 8 (y_hi: 4, y_lo: 2; y = y_hi * 2 + y_lo), z: 16, core: 2. Of those that a mesh axis runs over, the one named last changes fastest.
Arguments:
- queries: bfloat16 [65536, 4096], P(('blk', 'head')), may hold values from -60 to 60
- keys: bfloat16 [65536, 4096], P(('blk', 'head')), may hold values from -6.5 to 6.5
- values: bfloat16 [65536, 4096], P(('blk', 'head')), may hold values from -6 to 6
- block_lists: int32 [256, 3], P('blk'), may hold values from 0 to 255, as said below
- block_counts: int32 [256], P('blk'), may hold values from 1 to 3, as said below
Outputs:
- attended: bfloat16 [65536, 4096], P(('blk', 'head'))
Inputs may be any that keep to these rules, and one draw needn't show every extreme that they name: `block_lists`: row q holds distinct block indices among q - 2 to q, none below 0, starting with q itself; only its first block_counts[q] entries are used, and the rest repeat q. block_counts[q] is at most min(q + 1, 3); the last block's count is 3.
All inputs are finite; a program needn't handle non-finite values.
Results may differ from a plain program's by a relative error of at most 0.0037.
Values may be sent and summed in bfloat16 or wider, within the bound.
No kernel may reach another device: no remote copies, remote signals or barrier semaphores. Data moves between devices by JAX's collectives and lax.ppermute only.
A program may use at most 32 MiB of HBM per device.

v0:
```python
import jax
import jax.numpy as jnp
from jax import lax
from jax.sharding import PartitionSpec as P

HEADS = 32
HDIM = 128
BLOCK = 256
CYCLE = 3


def from_behind(value, axis, steps):
    count = lax.axis_size(axis)
    initial, last = (max(0, -steps), min(count, count - steps))
    return lax.ppermute(value, axis, [(source, source + steps) for source in range(initial, last)])


def body(queries, keys, values, block_lists, block_counts):
    local_heads = HEADS // lax.axis_size("head")
    scale = 1.0 / HDIM**0.5
    qmine = lax.all_to_all(queries, "head", split_axis=1, concat_axis=0, tiled=True)
    kmine, vmine = (
        lax.all_to_all(keys, "head", split_axis=1, concat_axis=0, tiled=True),
        lax.all_to_all(values, "head", split_axis=1, concat_axis=0, tiled=True),
    )
    rows = qmine.shape[0]
    owned_blocks = rows // BLOCK
    reach = CYCLE - 1
    mine = jnp.stack((kmine, vmine))
    before = from_behind(mine, "blk", 1)[:, rows - reach * BLOCK :]
    extended = jnp.concatenate((before, mine), axis=1)
    own = lax.axis_index("blk")
    entry = jnp.arange(CYCLE, dtype=jnp.int32)
    frame_pos = jnp.arange(BLOCK, dtype=jnp.int32)
    causal = frame_pos[None, :] <= frame_pos[:, None]
    outputs = []
    for local in range(owned_blocks):
        target = own * owned_blocks + local
        list_row = block_lists[local]
        count = block_counts[local]
        used = entry < count
        parts_mask = []
        for place in range(CYCLE):
            distance = reach - place
            wanted = jnp.any(used & (list_row == target - distance))
            if distance == 0:
                parts_mask.append(causal & wanted)
            else:
                parts_mask.append(jnp.broadcast_to(wanted, (BLOCK, BLOCK)))
        mask = jnp.concatenate(parts_mask, axis=1)
        span = extended[:, local * BLOCK : (local + CYCLE) * BLOCK]
        qsplit = qmine[local * BLOCK : (local + 1) * BLOCK].reshape(BLOCK, local_heads, HDIM)
        ksplit = span[0].reshape(CYCLE * BLOCK, local_heads, HDIM)
        vsplit = span[1].reshape(CYCLE * BLOCK, local_heads, HDIM)
        scores = (
            jnp.einsum("qhd,khd->hqk", qsplit, ksplit, preferred_element_type=jnp.float32) * scale
        )
        scores = jnp.where(mask[None], scores, -1e30)
        top = jnp.max(scores, axis=-1, keepdims=True)
        weights = jnp.where(mask[None], jnp.exp(scores - top), 0.0)
        total = jnp.sum(weights, axis=-1)
        rounded = weights.astype(jnp.bfloat16)
        summed = jnp.einsum("hqk,khd->qhd", rounded, vsplit, preferred_element_type=jnp.float32)
        result = summed / jnp.transpose(total)[:, :, None]
        outputs.append(result.reshape(BLOCK, local_heads * HDIM).astype(jnp.bfloat16))
    joined = jnp.concatenate(outputs, axis=0)
    return lax.all_to_all(joined, "head", split_axis=0, concat_axis=1, tiled=True)


def solution(mesh):
    return jax.shard_map(
        body,
        mesh=mesh,
        in_specs=(
            P(("blk", "head"), None),
            P(("blk", "head"), None),
            P(("blk", "head"), None),
            P("blk", None),
            P("blk"),
        ),
        out_specs=P(("blk", "head"), None),
        check_vma=False,
    )
```

profile of v0, /device:TPU:448, one launch (start us, length us, event | category | flops | bytes accessed | tf_op | source)
XLA Modules:
  0.0 125.5 jit_solution(5856260717055279714)
XLA Ops:
  0.0 2.0 %copy.145 = bf16[8,16,8,256]{3,2,0,1:T(8,128)(2,1)} copy(bf16[8,16,8,256]{3,2,1,0:T(8,128)(2,1)} %bitcast.160) | data formatting | bytes 1048576 | tf_op jit(solution)/shard_map/all_to_all | solution.py:23
  2.0 9.8 %all-to-all-start = ((bf16[64,16,256]{2,0,1:T(8,128)(2,1)}), bf16[64,16,256]{2,0,1:T(8,128)(2,1)S(1)}, u32[]{:S(2)}, u32[]{:S(2)}) async-start(bf16[64,16,256]{2,0,1:T(8,128)(2,1)} %bitcast.142), calls=%async_computation | async-start | bytes 1048576 | tf_op jit(solution)/shard_map/all_to_all | solution.py:23
  11.8 0.8 copy.144
  12.7 0.9 copy.143
  14.2 3.4 %fusion.46 = (pred[]{:T(512)}, pred[]{:T(512)}, pred[]{:T(512)}, pred[]{:T(512)}, pred[]{:T(512)}, /*index=5*/pred[]{:T(512)}, pred[]{:T(512)}, pred[]{:T(512)},...) fusion(s32[]{:T(128)S(6)} %sub.21, s32[]{:T(128)} %bitcast.5, s32[4,3]{1,0:T(4,128)S(1)} %copy-done.9, s32[]{:T(128)S(6)} %mul.24, ...), kind=kLoop, calls=%fused_computation.76 | loop fusion | flops 108 | bytes 100 | tf_op jit(solution)/shard_map/reduce_or | solution.py:45
  20.1 9.7 %all-to-all-done = bf16[64,16,256]{2,0,1:T(8,128)(2,1)S(1)} async-done(((bf16[64,16,256]{2,0,1:T(8,128)(2,1)}), bf16[64,16,256]{2,0,1:T(8,128)(2,1)S(1)}, u32[]{:S(2)}, u32[]{:S(2)}) %all-to-all-start) | async-done | bytes 524320 | tf_op jit(solution)/shard_map/all_to_all | solution.py:23
  29.8 4.3 %all-to-all-start.1 = ((bf16[64,16,256]{2,0,1:T(8,128)(2,1)}), bf16[64,16,256]{2,0,1:T(8,128)(2,1)S(1)}, u32[]{:S(2)}, u32[]{:S(2)}) async-start(bf16[64,16,256]{2,0,1:T(8,128)(2,1)} %bitcast.141), calls=%async_computation.1 | async-start | bytes 1048576 | tf_op jit(solution)/shard_map/all_to_all | solution.py:24
  34.8 0.7 broadcast_in_dim.99
  35.5 1.4 %fusion.22 = (pred[256,256]{0,1:T(8,128)(4,1)S(1)}, pred[256,256]{0,1:T(8,128)(4,1)S(1)}) fusion(pred[]{:T(512)} %get-tuple-element.35, pred[]{:T(512)} %get-tuple-element.16), kind=kLoop, calls=%fused_computation.45 | loop fusion | flops 196608 | bytes 131074 | tf_op jit(solution)/shard_map/and | solution.py:47
  36.9 1.3 %fusion.20 = (pred[256,256]{0,1:T(8,128)(4,1)S(1)}, pred[256,256]{0,1:T(8,128)(4,1)S(1)}) fusion(pred[]{:T(512)} %get-tuple-element.31, pred[]{:T(512)} %get-tuple-element.33), kind=kLoop, calls=%fused_computation.43 | loop fusion | flops 196608 | bytes 131074 | tf_op jit(solution)/shard_map/and | solution.py:47
  38.1 0.9 pad_add_fusion
  39.0 0.9 pad_add_fusion.1
  39.9 0.8 pad_add_fusion.2
  40.7 10.0 %all-to-all-done.1 = bf16[64,16,256]{2,0,1:T(8,128)(2,1)S(1)} async-done(((bf16[64,16,256]{2,0,1:T(8,128)(2,1)}), bf16[64,16,256]{2,0,1:T(8,128)(2,1)S(1)}, u32[]{:S(2)}, u32[]{:S(2)}) %all-to-all-start.1) | async-done | bytes 524320 | tf_op jit(solution)/shard_map/all_to_all | solution.py:24
  50.7 4.3 %all-to-all-start.2 = ((bf16[64,16,256]{2,0,1:T(8,128)(2,1)}), bf16[64,16,256]{2,0,1:T(8,128)(2,1)S(1)}, u32[]{:S(2)}, u32[]{:S(2)}) async-start(bf16[64,16,256]{2,0,1:T(8,128)(2,1)} %bitcast.140), calls=%async_computation.2 | async-start | bytes 1048576 | tf_op jit(solution)/shard_map/all_to_all | solution.py:21
  55.6 0.7 broadcast_in_dim.102
  56.3 0.9 pad_add_fusion.3
  57.2 1.1 pad_maximum_fusion
  58.3 1.9 %collective-permute-start = (bf16[2,1024,256]{2,1,0:T(8,128)(2,1)}, bf16[2,1024,256]{2,1,0:T(8,128)(2,1)}, u32[]{:S(2)}, u32[]{:S(2)}) collective-permute-start(bf16[2,1024,256]{2,1,0:T(8,128)(2,1)} %pad_maximum_fusion), channel_id=1, source_target_pairs={{0,16},{16,32},{32,48},{48,64},{64,80},{80,96},{96,112},{112,128},... | collective-permute-start | bytes 3145736 | tf_op jit(solution)/shard_map/ppermute | solution.py:15
  60.2 0.8 fusion.66
  61.0 0.8 fusion.67
  61.8 10.6 %all-to-all-done.2 = bf16[64,16,256]{2,0,1:T(8,128)(2,1)S(1)} async-done(((bf16[64,16,256]{2,0,1:T(8,128)(2,1)}), bf16[64,16,256]{2,0,1:T(8,128)(2,1)S(1)}, u32[]{:S(2)}, u32[]{:S(2)}) %all-to-all-start.2) | async-done | bytes 524320 | tf_op jit(solution)/shard_map/all_to_all | solution.py:21
  72.4 0.8 fusion.65
  73.4 1.3 %multiply_select_fusion.1 = f32[2,256,768]{1,2,0:T(8,128)S(1)} fusion(bf16[768,2,128]{0,2,1:T(8,128)(2,1)S(1)} %bitcast.154, pred[256,768]{0,1:T(8,128)(4,1)} %pad_add_fusion.2, bf16[256,2,128]{2,1,0:T(2,128)(2,1)S(1)} %reshape.80), kind=kOutput, calls=%fused_computation.14 | convolution fusion | flops 101449728 | bytes 2293760 | tf_op jit(solution)/shard_map/qhd,khd->hqk/dot_general | solution.py:56
  74.7 1.9 %fusion.72 = f32[2,256]{1,0:T(2,128)S(1)} fusion(bf16[768,2,128]{0,2,1:T(8,128)(2,1)S(1)} %bitcast.155, pred[256,768]{0,1:T(8,128)(4,1)} %pad_add_fusion.2, bf16[256,2,128]{2,1,0:T(2,128)(2,1)S(1)} %reshape.80), kind=kOutput, calls=%fused_computation.105 | convolution fusion | flops 102630144 | bytes 722944 | tf_op jit(solution)/shard_map/sub | solution.py:60
  76.7 1.6 %reshape.78 = bf16[256,2,128]{2,1,0:T(2,128)(2,1)} reshape(bf16[4,64,256]{2,1,0:T(8,128)(2,1)} %get-tuple-element.21) | data formatting | bytes 262144 | tf_op jit(solution)/shard_map/reshape | solution.py:52
  78.3 1.6 %reshape.79 = bf16[256,2,128]{2,1,0:T(2,128)(2,1)} reshape(bf16[4,64,256]{2,1,0:T(8,128)(2,1)} %get-tuple-element.24) | data formatting | bytes 262144 | tf_op jit(solution)/shard_map/reshape | solution.py:52
  79.8 1.2 copy.89
  81.0 1.5 %fusion.13 = bf16[256,2,128]{0,2,1:T(8,128)(2,1)S(1)} fusion(bf16[768,2,128]{0,2,1:T(8,128)(2,1)S(1)} %bitcast.164, f32[2,256,768]{1,2,0:T(8,128)S(1)} %multiply_select_fusion.1, pred[256,768]{0,1:T(8,128)(4,1)} %pad_add_fusion.2, f32[256,2]{0,1:T(2,128)S(1)} %bitcast.173), kind=kOutput, calls=%fused_computation.26 | convolution fusion | flops 101975296 | bytes 2295808 | tf_op jit(solution)/shard_map/hqk,khd->qhd/dot_general | solution.py:63
  82.5 0.8 copy.99
  83.3 1.2 copy.91
  84.4 0.9 reshape.81
  85.4 0.9 copy.95
  86.3 0.9 fusion.69
  87.7 1.6 %fusion.12 = bf16[256,2,128]{0,2,1:T(8,128)(2,1)S(1)} fusion(bf16[768,2,128]{0,2,1:T(8,128)(2,1)} %bitcast.163, f32[2,256,768]{1,2,0:T(8,128)S(1)} %multiply_select_fusion, pred[256,768]{0,1:T(8,128)(4,1)S(1)} %copy-done.2, f32[256,2]{0,1:T(2,128)S(1)} %bitcast.174), kind=kOutput, calls=%fused_computation.25 | convolution fusion | flops 101975296 | bytes 2295808 | tf_op jit(solution)/shard_map/hqk,khd->qhd/dot_general | solution.py:63
  89.2 0.8 copy.100
  90.0 1.1 slice.104
  91.2 0.9 fusion.64
  92.7 0.9 fusion.78
  93.6 0.9 copy.81
  94.5 1.5 %bitcast_select_fusion = f32[2,256,768]{1,2,0:T(8,128)S(1)} fusion(bf16[768,2,128]{0,2,1:T(8,128)(2,1)} %bitcast.158, pred[256,768]{0,1:T(8,128)(4,1)} %pad_add_fusion.1, bf16[256,2,128]{2,1,0:T(2,128)(2,1)} %reshape.79), kind=kOutput, calls=%fused_computation.9 | convolution fusion | flops 101449728 | bytes 2293760 | tf_op jit(solution)/shard_map/qhd,khd->hqk/dot_general | solution.py:56
  96.0 2.1 %fusion.75 = f32[2,256]{1,0:T(2,128)S(1)} fusion(bf16[768,2,128]{0,2,1:T(8,128)(2,1)} %bitcast.159, pred[256,768]{0,1:T(8,128)(4,1)} %pad_add_fusion.1, bf16[256,2,128]{2,1,0:T(2,128)(2,1)} %reshape.79), kind=kOutput, calls=%fused_computation.106 | convolution fusion | flops 102630144 | bytes 722944 | tf_op jit(solution)/shard_map/sub | solution.py:60
  98.1 1.9 %copy.74 = bf16[1,768,256]{1,2,0:T(8,128)(2,1)} copy(bf16[1,768,256]{2,1,0:T(8,128)(2,1)} %get-tuple-element.20) | data formatting | bytes 786432 | tf_op jit(solution)/shard_map/slice | solution.py:54
  100.0 2.3 %fusion.15 = bf16[256,2,128]{0,2,1:T(8,128)(2,1)} fusion(bf16[768,2,128]{0,2,1:T(8,128)(2,1)} %bitcast.165, f32[2,256,768]{1,2,0:T(8,128)S(1)} %bitcast_select_fusion.1, pred[256,768]{0,1:T(8,128)(4,1)} %pad_add_fusion, f32[256,2]{0,1:T(2,128)S(1)} %bitcast.172), kind=kOutput, calls=%fused_computation.28 | convolution fusion | flops 101975296 | bytes 2295808 | tf_op jit(solution)/shard_map/hqk,khd->qhd/dot_general | solution.py:63
  102.3 1.0 copy.97
  103.5 1.5 %fusion.14 = bf16[256,2,128]{0,2,1:T(8,128)(2,1)S(1)} fusion(bf16[768,2,128]{0,2,1:T(8,128)(2,1)S(1)} %bitcast.166, f32[2,256,768]{1,2,0:T(8,128)S(1)} %bitcast_select_fusion, pred[256,768]{0,1:T(8,128)(4,1)} %pad_add_fusion.1, f32[256,2]{0,1:T(2,128)S(1)} %bitcast.171), kind=kOutput, calls=%fused_computation.27 | convolution fusion | flops 101975296 | bytes 2295808 | tf_op jit(solution)/shard_map/hqk,khd->qhd/dot_general | solution.py:63
  105.2 19.5 %all_to_all.67 = bf16[16,64,256]{2,1,0:T(8,128)(2,1)S(1)} all-to-all(bf16[16,64,256]{2,1,0:T(8,128)(2,1)S(1)} %bitcast.150), channel_id=1, replica_groups=mesh['blk'=64,'head'=16] {'head'}, dimensions={0} | all-to-all | bytes 1048576 | tf_op jit(solution)/shard_map/all_to_all | solution.py:67
  124.7 0.8 copy.115
  (41 shorter events, 6.0 us)
Async XLA Ops:
  0.0 11.8 %copy-start.4 = (bf16[64,4096]{1,0:T(8,128)(2,1)S(1)}, bf16[64,4096]{1,0:T(8,128)(2,1)}, u32[]{:S(2)}) copy-start(bf16[64,4096]{1,0:T(8,128)(2,1)} %param.7) | copy-start | bytes 1572868
  0.0 12.6 %copy-start.5 = (bf16[64,4096]{1,0:T(8,128)(2,1)S(1)}, bf16[64,4096]{1,0:T(8,128)(2,1)}, u32[]{:S(2)}) copy-start(bf16[64,4096]{1,0:T(8,128)(2,1)} %param.5) | copy-start | bytes 1572868
  2.0 11.5 %copy-start.8 = (s32[4]{0:T(128)S(1)}, s32[4]{0:T(128)}, u32[]{:S(2)}) copy-start(s32[4]{0:T(128)} %param.9) | copy-start | bytes 52
  2.0 12.2 %copy-start.9 = (s32[4,3]{1,0:T(4,128)S(1)}, s32[4,3]{1,0:T(4,128)}, u32[]{:S(2)}) copy-start(s32[4,3]{1,0:T(4,128)} %param.8) | copy-start | bytes 148
  2.0 27.8 %all-to-all-start = ((bf16[64,16,256]{2,0,1:T(8,128)(2,1)}), bf16[64,16,256]{2,0,1:T(8,128)(2,1)S(1)}, u32[]{:S(2)}, u32[]{:S(2)}) async-start(bf16[64,16,256]{2,0,1:T(8,128)(2,1)} %bitcast.142), calls=%async_computation | async-start | bytes 1048576 | tf_op jit(solution)/shard_map/all_to_all | solution.py:23
  29.8 20.9 %all-to-all-start.1 = ((bf16[64,16,256]{2,0,1:T(8,128)(2,1)}), bf16[64,16,256]{2,0,1:T(8,128)(2,1)S(1)}, u32[]{:S(2)}, u32[]{:S(2)}) async-start(bf16[64,16,256]{2,0,1:T(8,128)(2,1)} %bitcast.141), calls=%async_computation.1 | async-start | bytes 1048576 | tf_op jit(solution)/shard_map/all_to_all | solution.py:24
  50.7 21.7 %all-to-all-start.2 = ((bf16[64,16,256]{2,0,1:T(8,128)(2,1)}), bf16[64,16,256]{2,0,1:T(8,128)(2,1)S(1)}, u32[]{:S(2)}, u32[]{:S(2)}) async-start(bf16[64,16,256]{2,0,1:T(8,128)(2,1)} %bitcast.140), calls=%async_computation.2 | async-start | bytes 1048576 | tf_op jit(solution)/shard_map/all_to_all | solution.py:21
  58.3 31.7 %collective-permute-start = (bf16[2,1024,256]{2,1,0:T(8,128)(2,1)}, bf16[2,1024,256]{2,1,0:T(8,128)(2,1)}, u32[]{:S(2)}, u32[]{:S(2)}) collective-permute-start(bf16[2,1024,256]{2,1,0:T(8,128)(2,1)} %pad_maximum_fusion), channel_id=1, source_target_pairs={{0,16},{16,32},{32,48},{48,64},{64,80},{80,96},{96,112},{112,128},... | collective-permute-start | bytes 3145736 | tf_op jit(solution)/shard_map/ppermute | solution.py:15
  82.5 3.8 %copy-start.1 = (pred[256,768]{0,1:T(8,128)(4,1)S(1)}, pred[256,768]{0,1:T(8,128)(4,1)}, u32[]{:S(2)}) copy-start(pred[256,768]{0,1:T(8,128)(4,1)} %pad_add_fusion.3) | copy-start | bytes 589828
  86.3 0.9 copy-start.2
  91.2 1.1 copy-start
  91.2 1.1 copy-start.3
  103.5 1.7 %copy-start.6 = (bf16[256,256]{1,0:T(8,128)(2,1)S(1)}, bf16[256,256]{1,0:T(8,128)(2,1)}, u32[]{:S(2)}) copy-start(bf16[256,256]{1,0:T(8,128)(2,1)} %copy.99) | copy-start | bytes 393220
  103.5 1.7 %copy-start.7 = (bf16[256,256]{1,0:T(8,128)(2,1)S(1)}, bf16[256,256]{1,0:T(8,128)(2,1)}, u32[]{:S(2)}) copy-start(bf16[256,256]{1,0:T(8,128)(2,1)} %copy.100) | copy-start | bytes 393220
where the time goes:
time: 127 us; the launch traced here: 126 us
  waiting for transfers between devices  30.3 us (24%)
  local copies, waits for them, and re-layouts  27.9 us (22%)
  starting transfers between devices  20.4 us (16%)
  blocking collectives  19.5 us (15%)
  matrix products  16.4 us (13%)
  other arithmetic  10.7 us (8%)
    all_to_all x1, blocking collectives, body(): lax.all_to_all(joined, 'head', split_axis=0, concat_axis=1, tiled=True)  19.5 us
    all_to_all x1, waiting for transfers between devices, body(): lax.all_to_all(queries, 'head', split_axis=1, concat_axis=0, tiled=True)  10.6 us
    all_to_all x1, waiting for transfers between devices, body(): lax.all_to_all(values, 'head', split_axis=1, concat_axis=0, tiled=True)  10 us
    all_to_all x1, starting transfers between devices, body(): lax.all_to_all(keys, 'head', split_axis=1, concat_axis=0, tiled=True)  9.8 us
    all_to_all x1, waiting for transfers between devices, body(): lax.all_to_all(keys, 'head', split_axis=1, concat_axis=0, tiled=True)  9.68 us
    dot_general x4, matrix products, body(): jnp.einsum('hqk,khd->qhd', rounded, vsplit, preferred_element_type=jnp.fl...  6.86 us
    sub x4, matrix products, body(): weights = jnp.where(mask[None], jnp.exp(scores - top), 0.0)  5.81 us
    broadcast_in_dim x8, local copies, waits for them, and re-layouts, body(): parts_mask.append(jnp.broadcast_to(wanted, (BLOCK, BLOCK)))  5.05 us
  transfers between devices with their start and end apart: 4, of which 3 were waited for; matrix products, arithmetic and copies ran while one was open for 30% of the time, Pallas kernels for 0%

commit v1 on v0

v1 whole, which is shorter than its diff:
```python
import jax
import jax.numpy as jnp
from jax import lax
from jax.experimental import pallas as pl
from jax.experimental.pallas import tpu as pltpu
from jax.sharding import PartitionSpec as P

HEADS = 32
HDIM = 128
BLOCK = 256
CYCLE = 3


def from_behind(value, axis, steps):
    count = lax.axis_size(axis)
    initial, last = (max(0, -steps), min(count, count - steps))
    return lax.ppermute(value, axis, [(source, source + steps) for source in range(initial, last)])


def attention_kernel(flags_ref, qkv_ref, before_ref, out_ref):
    rows = qkv_ref.shape[1]
    owned_blocks = rows // BLOCK
    local_heads = qkv_ref.shape[2] // HDIM
    reach = CYCLE - 1
    scale = 1.0 / HDIM**0.5
    row_pos = lax.broadcasted_iota(jnp.int32, (BLOCK, BLOCK), 0)
    col_pos = lax.broadcasted_iota(jnp.int32, (BLOCK, BLOCK), 1)
    causal = col_pos <= row_pos
    for local in range(owned_blocks):
        wanted = [flags_ref[local, place] != 0 for place in range(CYCLE)]
        masks = []
        for place in range(CYCLE):
            if place == reach:
                masks.append(causal & wanted[place])
            else:
                masks.append(jnp.broadcast_to(wanted[place], (BLOCK, BLOCK)))
        for head in range(local_heads):
            cols = slice(head * HDIM, (head + 1) * HDIM)
            q = qkv_ref[0, local * BLOCK : (local + 1) * BLOCK, cols]
            parts = []
            for place in range(CYCLE):
                source = local - (reach - place)
                if source >= 0:
                    k = qkv_ref[1, source * BLOCK : (source + 1) * BLOCK, cols]
                    v = qkv_ref[2, source * BLOCK : (source + 1) * BLOCK, cols]
                else:
                    start = (source + reach) * BLOCK
                    k = before_ref[0, start : start + BLOCK, cols]
                    v = before_ref[1, start : start + BLOCK, cols]
                s = lax.dot_general(q, k, (((1,), (1,)), ((), ())), preferred_element_type=jnp.float32) * scale
                s = jnp.where(masks[place], s, -1e30)
                parts.append((s, v))
            top = jnp.max(parts[0][0], axis=1, keepdims=True)
            for s, _ in parts[1:]:
                top = jnp.maximum(top, jnp.max(s, axis=1, keepdims=True))
            total = None
            summed = None
            for place, (s, v) in enumerate(parts):
                w = jnp.where(masks[place], jnp.exp(s - top), 0.0)
                t = jnp.sum(w, axis=1, keepdims=True)
                o = jnp.dot(w.astype(jnp.bfloat16), v, preferred_element_type=jnp.float32)
                total = t if total is None else total + t
                summed = o if summed is None else summed + o
            out_ref[local * BLOCK : (local + 1) * BLOCK, cols] = (summed / total).astype(out_ref.dtype)


def body(queries, keys, values, block_lists, block_counts):
    qkv = jnp.stack((queries, keys, values))
    mine = lax.all_to_all(qkv, "head", split_axis=2, concat_axis=1, tiled=True)
    rows = mine.shape[1]
    owned_blocks = rows // BLOCK
    reach = CYCLE - 1
    before = from_behind(mine[1:, rows - reach * BLOCK :], "blk", 1)
    own = lax.axis_index("blk")
    target = own * owned_blocks + jnp.arange(owned_blocks, dtype=jnp.int32)
    distance = reach - jnp.arange(CYCLE, dtype=jnp.int32)
    used = jnp.arange(CYCLE, dtype=jnp.int32)[None, :] < block_counts[:, None]
    hits = used[:, None, :] & (block_lists[:, None, :] == (target[:, None] - distance[None, :])[:, :, None])
    flags = jnp.any(hits, axis=2).astype(jnp.int32)
    joined = pl.pallas_call(
        attention_kernel,
        out_shape=jax.ShapeDtypeStruct((rows, mine.shape[2]), queries.dtype),
        in_specs=[
            pl.BlockSpec(memory_space=pltpu.SMEM),
            pl.BlockSpec(memory_space=pltpu.VMEM),
            pl.BlockSpec(memory_space=pltpu.VMEM),
        ],
        out_specs=pl.BlockSpec(memory_space=pltpu.VMEM),
    )(flags, mine, before)
    return lax.all_to_all(joined, "head", split_axis=0, concat_axis=1, tiled=True)


def solution(mesh):
    return jax.shard_map(
        body,
        mesh=mesh,
        in_specs=(
            P(("blk", "head"), None),
            P(("blk", "head"), None),
            P(("blk", "head"), None),
            P("blk", None),
            P("blk"),
        ),
        out_specs=P(("blk", "head"), None),
        check_vma=False,
    )
```

time: 127 us -> 115 us (0.906)
  the two profiles are of different devices: /device:TPU:448 before, /device:TPU:256 now
where the time goes in v1:
time: 115 us; the launch traced here: 114 us
  waiting for transfers between devices  51.5 us (45%)
  local copies, waits for them, and re-layouts  23.9 us (21%)
  blocking collectives  18.7 us (16%)
  starting transfers between devices  11.6 us (10%)
  Pallas kernels  5.75 us (5%)
  other arithmetic  2.48 us (2%)
    all_to_all x1, waiting for transfers between devices, body(): mine = lax.all_to_all(qkv, 'head', split_axis=2, concat_axis=1, tiled=True)  41.9 us
    all_to_all x1, blocking collectives, body(): lax.all_to_all(joined, 'head', split_axis=0, concat_axis=1, tiled=True)  18.7 us
    unnamed x10, local copies, waits for them, and re-layouts  12.8 us
    all_to_all x1, starting transfers between devices, body(): mine = lax.all_to_all(qkv, 'head', split_axis=2, concat_axis=1, tiled=True)  9.67 us
    ppermute x1, waiting for transfers between devices, from_behind(): lax.ppermute(value, axis, [(source, source + steps) for source in range(i...  9.61 us
    pallas_call x1, Pallas kernels, body(): pl.pallas_call(attention_kernel, out_shape=jax.ShapeDtypeStruct((rows, mi...  5.75 us
    all_to_all x1, local copies, waits for them, and re-layouts, body(): mine = lax.all_to_all(qkv, 'head', split_axis=2, concat_axis=1, tiled=True)  5.44 us
    another operation x1, local copies, waits for them, and re-layouts, body(): qkv = jnp.stack((queries, keys, values))  4.74 us
  transfers between devices with their start and end apart: 2, of which 2 were waited for; matrix products, arithmetic and copies ran while one was open for 1% of the time, Pallas kernels for 0%

profile of v1, /device:TPU:256, one launch (start us, length us, event | category | flops | bytes accessed | tf_op | source)
XLA Modules:
  0.0 114.1 jit_solution(10555835483402602160)
XLA Ops:
  0.0 1.5 %pad_maximum_fusion = bf16[3,64,4096]{2,1,0:T(8,128)(2,1)S(1)} fusion(bf16[1,64,4096]{2,1,0:T(8,128)(2,1)} %bitcast.19, bf16[1,64,4096]{2,1,0:T(8,128)(2,1)} %bitcast.20, bf16[1,64,4096]{2,1,0:T(8,128)(2,1)} %bitcast.21), kind=kLoop, calls=%fused_computation | loop fusion | flops 1572864 | bytes 3145728 | tf_op jit(solution)/shard_map/stack | solution.py:68
  1.5 4.7 %copy.17 = bf16[3,64,4096]{1,0,2:T(4,128)(2,1)} copy(bf16[3,64,4096]{2,1,0:T(8,128)(2,1)S(1)} %pad_maximum_fusion) | data formatting | bytes 3145728 | tf_op jit(solution)/shard_map/stack | solution.py:68
  6.3 7.2 %reshape.56 = bf16[16,2,24576]{2,1,0:T(2,128)(2,1)} reshape(bf16[4096,3,64]{2,1,0:T(4,128)(2,1)} %bitcast.13) | data formatting | bytes 3145728
  13.5 9.7 %all-to-all-start = ((bf16[16,2,24576]{2,1,0:T(2,128)(2,1)}), bf16[16,2,24576]{2,1,0:T(2,128)(2,1)S(1)}, u32[]{:S(2)}, u32[]{:S(2)}) async-start(bf16[16,2,24576]{2,1,0:T(2,128)(2,1)} %reshape.56), calls=%async_computation | async-start | bytes 3145728 | tf_op jit(solution)/shard_map/all_to_all | solution.py:69
  23.2 41.9 %all-to-all-done = bf16[16,2,24576]{2,1,0:T(2,128)(2,1)S(1)} async-done(((bf16[16,2,24576]{2,1,0:T(2,128)(2,1)}), bf16[16,2,24576]{2,1,0:T(2,128)(2,1)S(1)}, u32[]{:S(2)}, u32[]{:S(2)}) %all-to-all-start) | async-done | bytes 1572896 | tf_op jit(solution)/shard_map/all_to_all | solution.py:69
  65.1 4.7 %reshape.57 = bf16[4096,3,64]{2,1,0:T(4,128)(2,1)} reshape(bf16[16,2,24576]{2,1,0:T(2,128)(2,1)S(1)} %all-to-all-done) | data formatting | bytes 3145728
  69.9 0.0 copy-start.3
  69.9 0.0 copy-start.2
  69.9 5.4 %copy.18 = bf16[3,64,16,256]{3,1,2,0:T(8,128)(2,1)S(1)} copy(bf16[3,64,16,256]{1,0,3,2:T(4,128)(2,1)} %bitcast.14) | data formatting | bytes 3145728 | tf_op jit(solution)/shard_map/all_to_all | solution.py:69
  75.3 0.0 copy-start
  75.4 1.9 %collective-permute-start = (bf16[2,512,256]{2,1,0:T(8,128)(2,1)S(1)}, bf16[2,512,256]{2,1,0:T(8,128)(2,1)S(1)}, u32[]{:S(2)}, u32[]{:S(2)}) collective-permute-start(bf16[2,512,256]{2,1,0:T(8,128)(2,1)S(1)} %slice.4), channel_id=1, source_target_pairs={{0,16},{16,32},{32,48},{48,64},{64,80},{80,96},{96,112},{112,128},... | collective-permute-start | bytes 1572872 | tf_op jit(solution)/shard_map/ppermute | solution.py:17
  77.3 0.0 copy-done.3
  77.3 0.1 iota_compare_fusion
  77.4 0.1 broadcast_subtract_fusion
  77.5 0.0 copy-done.2
  77.5 0.2 and_reduce_fusion
  77.7 0.1 copy.16
  77.8 0.6 convert_element_type.3.flags_ref
  78.4 9.6 %collective-permute-done.before_ref = bf16[2,512,256]{2,1,0:T(8,128)(2,1)S(1)} collective-permute-done((bf16[2,512,256]{2,1,0:T(8,128)(2,1)S(1)}, bf16[2,512,256]{2,1,0:T(8,128)(2,1)S(1)}, u32[]{:S(2)}, u32[]{:S(2)}) %collective-permute-start) | collective-permute-done | bytes 524320 | tf_op jit(solution)/shard_map/ppermute | solution.py:17
  88.0 0.0 copy-done
  88.0 0.0 copy-start.1
  88.0 0.8 copy-done.1
  88.8 5.7 %shard_map.55 = bf16[1024,256]{1,0:T(8,128)(2,1)} custom-call(s32[4,3]{1,0:T(4,128)} %convert_element_type.3.flags_ref, bf16[3,1024,256]{2,1,0:T(8,128)(2,1)} %bitcast.16, bf16[2,512,256]{2,1,0:T(8,128)(2,1)} %copy-done.1), custom_call_target="tpu_custom_call" | custom-call | tf_op jit(solution)/shard_map/pallas_call | solution.py:80
  94.5 18.7 %all_to_all.37 = bf16[16,64,256]{2,1,0:T(8,128)(2,1)S(1)} all-to-all(bf16[16,64,256]{2,1,0:T(8,128)(2,1)} %bitcast.18), channel_id=1, replica_groups=mesh['blk'=64,'head'=16] {'head'}, dimensions={0} | all-to-all | bytes 1048576 | tf_op jit(solution)/shard_map/all_to_all | solution.py:90
  113.3 0.8 copy.20
  (3 shorter events, 0.0 us)
Async XLA Ops:
  13.5 51.6 %all-to-all-start = ((bf16[16,2,24576]{2,1,0:T(2,128)(2,1)}), bf16[16,2,24576]{2,1,0:T(2,128)(2,1)S(1)}, u32[]{:S(2)}, u32[]{:S(2)}) async-start(bf16[16,2,24576]{2,1,0:T(2,128)(2,1)} %reshape.56), calls=%async_computation | async-start | bytes 3145728 | tf_op jit(solution)/shard_map/all_to_all | solution.py:69
  69.9 7.4 %copy-start.3 = (s32[4]{0:T(128)S(1)}, s32[4]{0:T(128)}, u32[]{:S(2)}) copy-start(s32[4]{0:T(128)} %param.9) | copy-start | bytes 52
  69.9 7.6 %copy-start.2 = (s32[4,3]{1,0:T(4,128)S(1)}, s32[4,3]{1,0:T(4,128)}, u32[]{:S(2)}) copy-start(s32[4,3]{1,0:T(4,128)} %param.8) | copy-start | bytes 148
  75.3 12.7 %copy-start = (bf16[3,64,16,256]{3,1,2,0:T(8,128)(2,1)}, bf16[3,64,16,256]{3,1,2,0:T(8,128)(2,1)S(1)}, u32[]{:S(2)}) copy-start(bf16[3,64,16,256]{3,1,2,0:T(8,128)(2,1)S(1)} %copy.18) | copy-start | bytes 4718596
  75.4 12.6 %collective-permute-start = (bf16[2,512,256]{2,1,0:T(8,128)(2,1)S(1)}, bf16[2,512,256]{2,1,0:T(8,128)(2,1)S(1)}, u32[]{:S(2)}, u32[]{:S(2)}) collective-permute-start(bf16[2,512,256]{2,1,0:T(8,128)(2,1)S(1)} %slice.4), channel_id=1, source_target_pairs={{0,16},{16,32},{32,48},{48,64},{64,80},{80,96},{96,112},{112,128},... | collective-permute-start | bytes 1572872 | tf_op jit(solution)/shard_map/ppermute | solution.py:17
  88.0 0.8 copy-start.1

commit v2 on v1

--- a/solution.py
+++ b/solution.py
@@ -17,10 +17,11 @@
     return lax.ppermute(value, axis, [(source, source + steps) for source in range(initial, last)])
 
 
-def attention_kernel(flags_ref, qkv_ref, before_ref, out_ref):
-    rows = qkv_ref.shape[1]
-    owned_blocks = rows // BLOCK
-    local_heads = qkv_ref.shape[2] // HDIM
+def attention_kernel(flags_ref, q_ref, kv_ref, before_ref, out_ref):
+    peers, chunk, width = q_ref.shape
+    per_block = BLOCK // chunk
+    owned_blocks = peers // per_block
+    local_heads = width // HDIM
     reach = CYCLE - 1
     scale = 1.0 / HDIM**0.5
     row_pos = lax.broadcasted_iota(jnp.int32, (BLOCK, BLOCK), 0)
@@ -34,19 +35,21 @@
                 masks.append(causal & wanted[place])
             else:
                 masks.append(jnp.broadcast_to(wanted[place], (BLOCK, BLOCK)))
+        rows = slice(local * per_block, (local + 1) * per_block)
         for head in range(local_heads):
             cols = slice(head * HDIM, (head + 1) * HDIM)
-            q = qkv_ref[0, local * BLOCK : (local + 1) * BLOCK, cols]
+            q = q_ref[rows, :, cols].reshape(BLOCK, HDIM)
             parts = []
             for place in range(CYCLE):
                 source = local - (reach - place)
                 if source >= 0:
-                    k = qkv_ref[1, source * BLOCK : (source + 1) * BLOCK, cols]
-                    v = qkv_ref[2, source * BLOCK : (source + 1) * BLOCK, cols]
+                    src = slice(source * per_block, (source + 1) * per_block)
+                    k = kv_ref[src, 0, :, cols].reshape(BLOCK, HDIM)
+                    v = kv_ref[src, 1, :, cols].reshape(BLOCK, HDIM)
                 else:
-                    start = (source + reach) * BLOCK
-                    k = before_ref[0, start : start + BLOCK, cols]
-                    v = before_ref[1, start : start + BLOCK, cols]
+                    src = slice((source + reach) * per_block, (source + reach + 1) * per_block)
+                    k = before_ref[src, 0, :, cols].reshape(BLOCK, HDIM)
+                    v = before_ref[src, 1, :, cols].reshape(BLOCK, HDIM)
                 s = lax.dot_general(q, k, (((1,), (1,)), ((), ())), preferred_element_type=jnp.float32) * scale
                 s = jnp.where(masks[place], s, -1e30)
                 parts.append((s, v))
@@ -61,16 +64,22 @@
                 o = jnp.dot(w.astype(jnp.bfloat16), v, preferred_element_type=jnp.float32)
                 total = t if total is None else total + t
                 summed = o if summed is None else summed + o
-            out_ref[local * BLOCK : (local + 1) * BLOCK, cols] = (summed / total).astype(out_ref.dtype)
+            result = (summed / total).astype(out_ref.dtype)
+            out_ref[rows, :, cols] = result.reshape(per_block, chunk, HDIM)
 
 
 def body(queries, keys, values, block_lists, block_counts):
-    qkv = jnp.stack((queries, keys, values))
-    mine = lax.all_to_all(qkv, "head", split_axis=2, concat_axis=1, tiled=True)
-    rows = mine.shape[1]
-    owned_blocks = rows // BLOCK
+    peers = lax.axis_size("head")
+    chunk, width = queries.shape
+    cols = width // peers
+    per_block = BLOCK // chunk
+    owned_blocks = peers // per_block
     reach = CYCLE - 1
-    before = from_behind(mine[1:, rows - reach * BLOCK :], "blk", 1)
+    kv_out = jnp.stack((keys, values)).reshape(2, chunk, peers, cols).transpose(2, 0, 1, 3)
+    kv = lax.all_to_all(kv_out, "head", split_axis=0, concat_axis=0, tiled=True)
+    before = from_behind(kv[peers - reach * per_block :], "blk", 1)
+    q_out = queries.reshape(chunk, peers, cols).transpose(1, 0, 2)
+    q = lax.all_to_all(q_out, "head", split_axis=0, concat_axis=0, tiled=True)
     own = lax.axis_index("blk")
     target = own * owned_blocks + jnp.arange(owned_blocks, dtype=jnp.int32)
     distance = reach - jnp.arange(CYCLE, dtype=jnp.int32)
@@ -79,15 +88,17 @@
     flags = jnp.any(hits, axis=2).astype(jnp.int32)
     joined = pl.pallas_call(
         attention_kernel,
-        out_shape=jax.ShapeDtypeStruct((rows, mine.shape[2]), queries.dtype),
+        out_shape=jax.ShapeDtypeStruct(q.shape, queries.dtype),
         in_specs=[
             pl.BlockSpec(memory_space=pltpu.SMEM),
             pl.BlockSpec(memory_space=pltpu.VMEM),
             pl.BlockSpec(memory_space=pltpu.VMEM),
+            pl.BlockSpec(memory_space=pltpu.VMEM),
         ],
         out_specs=pl.BlockSpec(memory_space=pltpu.VMEM),
-    )(flags, mine, before)
-    return lax.all_to_all(joined, "head", split_axis=0, concat_axis=1, tiled=True)
+    )(flags, q, kv, before)
+    back = lax.all_to_all(joined, "head", split_axis=0, concat_axis=0, tiled=True)
+    return back.transpose(1, 0, 2).reshape(chunk, width)
 
 
 def solution(mesh):

time: 115 us -> 99 us (0.86)
  the two profiles are of different devices: /device:TPU:256 before, /device:TPU:520 now
where the time goes in v2:
time: 99 us; the launch traced here: 98.4 us
  waiting for transfers between devices  42.7 us (43%)
  starting transfers between devices  21 us (21%)
  blocking collectives  20.9 us (21%)
  local copies, waits for them, and re-layouts  5.88 us (6%)
  Pallas kernels  5.76 us (6%)
  other arithmetic  2.03 us (2%)
    all_to_all x1, waiting for transfers between devices, body(): kv = lax.all_to_all(kv_out, 'head', split_axis=0, concat_axis=0, tiled=True)  22.1 us
    all_to_all x1, blocking collectives, body(): lax.all_to_all(joined, 'head', split_axis=0, concat_axis=0, tiled=True)  20.9 us
    all_to_all x1, waiting for transfers between devices, body(): q = lax.all_to_all(q_out, 'head', split_axis=0, concat_axis=0, tiled=True)  20.6 us
    all_to_all x1, starting transfers between devices, body(): q = lax.all_to_all(q_out, 'head', split_axis=0, concat_axis=0, tiled=True)  10.2 us
    all_to_all x1, starting transfers between devices, body(): kv = lax.all_to_all(kv_out, 'head', split_axis=0, concat_axis=0, tiled=True)  8.9 us
    pallas_call x1, Pallas kernels, body(): pl.pallas_call(attention_kernel, out_shape=jax.ShapeDtypeStruct(q.shape,...  5.76 us
    unnamed x16, local copies, waits for them, and re-layouts  3.75 us
  transfers between devices with their start and end apart: 3, of which 2 were waited for; matrix products, arithmetic and copies ran while one was open for 2% of the time, Pallas kernels for 0%

profile of v2, /device:TPU:520, one launch (start us, length us, event | category | flops | bytes accessed | tf_op | source)
XLA Modules:
  0.0 98.4 jit_solution(3448722615296024456)
XLA Ops:
  0.0 1.1 %copy.17 = bf16[8,8,16,256]{3,2,1,0:T(8,128)(2,1)S(1)} copy(bf16[8,8,16,256]{3,1,2,0:T(8,128)(2,1)} %bitcast.21) | data formatting | bytes 1048576
  1.1 0.0 copy-start.2
  1.2 0.2 copy.12
  1.3 0.9 copy-done.2
  2.2 0.1 copy.18
  2.3 0.2 copy.13
  2.5 1.1 %maximum_bitcast_fusion = bf16[16,2,64,256]{3,2,1,0:T(8,128)(2,1)} fusion(bf16[1,64,16,256]{3,1,0,2:T(8,128)(2,1)S(1)} %copy.13, bf16[1,64,16,256]{3,1,0,2:T(8,128)(2,1)S(1)} %copy.12), kind=kLoop, calls=%fused_computation | loop fusion | flops 524288 | bytes 2097152 | tf_op jit(solution)/shard_map/transpose | solution.py:78
  3.5 0.0 copy-start.3
  3.5 8.9 %all-to-all-start.1 = ((bf16[16,2,64,256]{3,2,1,0:T(8,128)(2,1)}), bf16[16,2,64,256]{3,2,1,0:T(8,128)(2,1)S(1)}, u32[]{:S(2)}, u32[]{:S(2)}) async-start(bf16[16,2,64,256]{3,2,1,0:T(8,128)(2,1)} %maximum_bitcast_fusion), calls=%async_computation.1 | async-start | bytes 2097152 | tf_op jit(solution)/shard_map/all_to_all | solution.py:79
  12.4 0.0 copy-done.3
  12.4 0.8 copy.20
  13.3 22.1 %all-to-all-done.1.kv_ref = bf16[16,2,64,256]{3,2,1,0:T(8,128)(2,1)S(1)} async-done(((bf16[16,2,64,256]{3,2,1,0:T(8,128)(2,1)}), bf16[16,2,64,256]{3,2,1,0:T(8,128)(2,1)S(1)}, u32[]{:S(2)}, u32[]{:S(2)}) %all-to-all-start.1) | async-done | bytes 1048608 | tf_op jit(solution)/shard_map/all_to_all | solution.py:79
  35.4 0.0 copy-start
  35.4 10.2 %all-to-all-start = ((bf16[16,64,256]{2,1,0:T(8,128)(2,1)}), bf16[16,64,256]{2,1,0:T(8,128)(2,1)S(1)}, u32[]{:S(2)}, u32[]{:S(2)}) async-start(bf16[16,64,256]{2,1,0:T(8,128)(2,1)} %bitcast.17), calls=%async_computation | async-start | bytes 1048576 | tf_op jit(solution)/shard_map/all_to_all | solution.py:82
  45.7 0.0 copy-start.6
  45.7 0.0 copy-done
  45.7 0.0 copy-start.5
  45.8 1.9 %collective-permute-start = (bf16[8,2,64,256]{3,2,1,0:T(8,128)(2,1)S(1)}, bf16[8,2,64,256]{3,2,1,0:T(8,128)(2,1)S(1)}, u32[]{:S(2)}, u32[]{:S(2)}) collective-permute-start(bf16[8,2,64,256]{3,2,1,0:T(8,128)(2,1)S(1)} %slice.4), channel_id=1, source_target_pairs={{0,16},{16,32},{32,48},{48,64},{64,80},{80,96},{96,112},{112,128},... | collective-permute-start | bytes 1572872 | tf_op jit(solution)/shard_map/ppermute | solution.py:17
  47.7 0.0 copy-done.6
  47.7 0.1 iota_compare_fusion
  47.8 0.1 broadcast_subtract_fusion
  47.8 0.0 copy-done.5
  47.8 0.2 and_reduce_fusion
  48.1 0.1 copy.10
  48.2 0.6 convert_element_type.3.flags_ref
  48.8 20.6 %all-to-all-done.q_ref = bf16[16,64,256]{2,1,0:T(8,128)(2,1)S(1)} async-done(((bf16[16,64,256]{2,1,0:T(8,128)(2,1)}), bf16[16,64,256]{2,1,0:T(8,128)(2,1)S(1)}, u32[]{:S(2)}, u32[]{:S(2)}) %all-to-all-start) | async-done | bytes 524320 | tf_op jit(solution)/shard_map/all_to_all | solution.py:82
  69.3 0.0 copy-start.1
  69.3 0.0 collective-permute-done.before_ref
  69.3 0.8 copy-done.1
  70.1 0.0 copy-start.4
  70.1 0.8 copy-done.4
  71.0 5.8 %shard_map.55 = bf16[16,64,256]{2,1,0:T(8,128)(2,1)} custom-call(s32[4,3]{1,0:T(4,128)} %convert_element_type.3.flags_ref, bf16[16,64,256]{2,1,0:T(8,128)(2,1)} %copy-done.1, bf16[16,2,64,256]{3,2,1,0:T(8,128)(2,1)} %copy-done, bf16[8,2,64,256]{3,2,1,0:T(8,128)(2,1)} %copy-done.4), custom_call_target="tpu_custom_call" | custom-call | tf_op jit(solution)/shard_map/pallas_call | solution.py:89
  76.7 20.9 %all_to_all.15 = bf16[16,64,256]{2,1,0:T(8,128)(2,1)S(1)} all-to-all(bf16[16,64,256]{2,1,0:T(8,128)(2,1)} %shard_map.55), channel_id=1, replica_groups=mesh['blk'=64,'head'=16] {'head'}, dimensions={0} | all-to-all | bytes 1048576 | tf_op jit(solution)/shard_map/all_to_all | solution.py:100
  97.6 0.8 copy.16
  (3 shorter events, 0.0 us)
Async XLA Ops:
  1.1 1.0 %copy-start.2 = (bf16[64,4096]{1,0:T(8,128)(2,1)S(1)}, bf16[64,4096]{1,0:T(8,128)(2,1)}, u32[]{:S(2)}) copy-start(bf16[64,4096]{1,0:T(8,128)(2,1)} %param.7) | copy-start | bytes 1572868
  3.5 8.9 %copy-start.3 = (bf16[64,4096]{1,0:T(8,128)(2,1)S(1)}, bf16[64,4096]{1,0:T(8,128)(2,1)}, u32[]{:S(2)}) copy-start(bf16[64,4096]{1,0:T(8,128)(2,1)} %param.5) | copy-start | bytes 1572868
  3.5 31.9 %all-to-all-start.1 = ((bf16[16,2,64,256]{3,2,1,0:T(8,128)(2,1)}), bf16[16,2,64,256]{3,2,1,0:T(8,128)(2,1)S(1)}, u32[]{:S(2)}, u32[]{:S(2)}) async-start(bf16[16,2,64,256]{3,2,1,0:T(8,128)(2,1)} %maximum_bitcast_fusion), calls=%async_computation.1 | async-start | bytes 2097152 | tf_op jit(solution)/shard_map/all_to_all | solution.py:79
  35.4 10.3 %copy-start = (bf16[16,2,64,256]{3,2,1,0:T(8,128)(2,1)}, bf16[16,2,64,256]{3,2,1,0:T(8,128)(2,1)S(1)}, u32[]{:S(2)}) copy-start(bf16[16,2,64,256]{3,2,1,0:T(8,128)(2,1)S(1)} %all-to-all-done.1.kv_ref) | copy-start | bytes 3145732
  35.4 33.9 %all-to-all-start = ((bf16[16,64,256]{2,1,0:T(8,128)(2,1)}), bf16[16,64,256]{2,1,0:T(8,128)(2,1)S(1)}, u32[]{:S(2)}, u32[]{:S(2)}) async-start(bf16[16,64,256]{2,1,0:T(8,128)(2,1)} %bitcast.17), calls=%async_computation | async-start | bytes 1048576 | tf_op jit(solution)/shard_map/all_to_all | solution.py:82
  45.7 2.0 %copy-start.6 = (s32[4]{0:T(128)S(1)}, s32[4]{0:T(128)}, u32[]{:S(2)}) copy-start(s32[4]{0:T(128)} %param.9) | copy-start | bytes 52
  45.7 2.1 %copy-start.5 = (s32[4,3]{1,0:T(4,128)S(1)}, s32[4,3]{1,0:T(4,128)}, u32[]{:S(2)}) copy-start(s32[4,3]{1,0:T(4,128)} %param.8) | copy-start | bytes 148
  45.8 23.6 %collective-permute-start = (bf16[8,2,64,256]{3,2,1,0:T(8,128)(2,1)S(1)}, bf16[8,2,64,256]{3,2,1,0:T(8,128)(2,1)S(1)}, u32[]{:S(2)}, u32[]{:S(2)}) collective-permute-start(bf16[8,2,64,256]{3,2,1,0:T(8,128)(2,1)S(1)} %slice.4), channel_id=1, source_target_pairs={{0,16},{16,32},{32,48},{48,64},{64,80},{80,96},{96,112},{112,128},... | collective-permute-start | bytes 1572872 | tf_op jit(solution)/shard_map/ppermute | solution.py:17
  69.3 0.8 copy-start.1
  70.1 0.8 copy-start.4

commit v3 on v2

--- a/solution.py
+++ b/solution.py
@@ -1,3 +1,5 @@
+import functools
+
 import jax
 import jax.numpy as jnp
 from jax import lax
@@ -17,17 +19,24 @@
     return lax.ppermute(value, axis, [(source, source + steps) for source in range(initial, last)])
 
 
-def attention_kernel(flags_ref, q_ref, kv_ref, before_ref, out_ref):
-    peers, chunk, width = q_ref.shape
+def attention_kernel(blocks, has_before, has_prior, flags_ref, qkv_ref, *refs):
+    before_ref = refs[0] if has_before else None
+    out_ref = refs[-1]
+    peers, _, chunk, width = qkv_ref.shape
     per_block = BLOCK // chunk
-    owned_blocks = peers // per_block
     local_heads = width // HDIM
     reach = CYCLE - 1
     scale = 1.0 / HDIM**0.5
     row_pos = lax.broadcasted_iota(jnp.int32, (BLOCK, BLOCK), 0)
     col_pos = lax.broadcasted_iota(jnp.int32, (BLOCK, BLOCK), 1)
     causal = col_pos <= row_pos
-    for local in range(owned_blocks):
+    if has_prior:
+        prior_ref = refs[-2]
+        for local in range(peers // per_block):
+            if local not in blocks:
+                rows = slice(local * per_block, (local + 1) * per_block)
+                out_ref[rows] = prior_ref[rows]
+    for local in blocks:
         wanted = [flags_ref[local, place] != 0 for place in range(CYCLE)]
         masks = []
         for place in range(CYCLE):
@@ -38,14 +47,14 @@
         rows = slice(local * per_block, (local + 1) * per_block)
         for head in range(local_heads):
             cols = slice(head * HDIM, (head + 1) * HDIM)
-            q = q_ref[rows, :, cols].reshape(BLOCK, HDIM)
+            q = qkv_ref[rows, 0, :, cols].reshape(BLOCK, HDIM)
             parts = []
             for place in range(CYCLE):
                 source = local - (reach - place)
                 if source >= 0:
                     src = slice(source * per_block, (source + 1) * per_block)
-                    k = kv_ref[src, 0, :, cols].reshape(BLOCK, HDIM)
-                    v = kv_ref[src, 1, :, cols].reshape(BLOCK, HDIM)
+                    k = qkv_ref[src, 1, :, cols].reshape(BLOCK, HDIM)
+                    v = qkv_ref[src, 2, :, cols].reshape(BLOCK, HDIM)
                 else:
                     src = slice((source + reach) * per_block, (source + reach + 1) * per_block)
                     k = before_ref[src, 0, :, cols].reshape(BLOCK, HDIM)
@@ -68,6 +77,18 @@
             out_ref[rows, :, cols] = result.reshape(per_block, chunk, HDIM)
 
 
+def attend(blocks, flags, qkv, before, prior):
+    vmem = pl.BlockSpec(memory_space=pltpu.VMEM)
+    extra = tuple(x for x in (before, prior) if x is not None)
+    peers, _, chunk, width = qkv.shape
+    return pl.pallas_call(
+        functools.partial(attention_kernel, blocks, before is not None, prior is not None),
+        out_shape=jax.ShapeDtypeStruct((peers, chunk, width), qkv.dtype),
+        in_specs=[pl.BlockSpec(memory_space=pltpu.SMEM)] + [vmem] * (1 + len(extra)),
+        out_specs=vmem,
+    )(flags, qkv, *extra)
+
+
 def body(queries, keys, values, block_lists, block_counts):
     peers = lax.axis_size("head")
     chunk, width = queries.shape
@@ -75,28 +96,19 @@
     per_block = BLOCK // chunk
     owned_blocks = peers // per_block
     reach = CYCLE - 1
-    kv_out = jnp.stack((keys, values)).reshape(2, chunk, peers, cols).transpose(2, 0, 1, 3)
-    kv = lax.all_to_all(kv_out, "head", split_axis=0, concat_axis=0, tiled=True)
-    before = from_behind(kv[peers - reach * per_block :], "blk", 1)
-    q_out = queries.reshape(chunk, peers, cols).transpose(1, 0, 2)
-    q = lax.all_to_all(q_out, "head", split_axis=0, concat_axis=0, tiled=True)
+    qkv_out = jnp.stack((queries, keys, values)).reshape(3, chunk, peers, cols).transpose(2, 0, 1, 3)
+    qkv = lax.all_to_all(qkv_out, "head", split_axis=0, concat_axis=0, tiled=True)
+    before = from_behind(qkv[peers - reach * per_block :, 1:], "blk", 1)
     own = lax.axis_index("blk")
     target = own * owned_blocks + jnp.arange(owned_blocks, dtype=jnp.int32)
     distance = reach - jnp.arange(CYCLE, dtype=jnp.int32)
     used = jnp.arange(CYCLE, dtype=jnp.int32)[None, :] < block_counts[:, None]
     hits = used[:, None, :] & (block_lists[:, None, :] == (target[:, None] - distance[None, :])[:, :, None])
     flags = jnp.any(hits, axis=2).astype(jnp.int32)
-    joined = pl.pallas_call(
-        attention_kernel,
-        out_shape=jax.ShapeDtypeStruct(q.shape, queries.dtype),
-        in_specs=[
-            pl.BlockSpec(memory_space=pltpu.SMEM),
-            pl.BlockSpec(memory_space=pltpu.VMEM),
-            pl.BlockSpec(memory_space=pltpu.VMEM),
-            pl.BlockSpec(memory_space=pltpu.VMEM),
-        ],
-        out_specs=pl.BlockSpec(memory_space=pltpu.VMEM),
-    )(flags, q, kv, before)
+    late = tuple(range(min(reach, owned_blocks)))
+    early = tuple(range(len(late), owned_blocks))
+    joined = attend(early, flags, qkv, None, None) if early else None
+    joined = attend(late, flags, qkv, before, joined)
     back = lax.all_to_all(joined, "head", split_axis=0, concat_axis=0, tiled=True)
     return back.transpose(1, 0, 2).reshape(chunk, width)
 

time: 99 us -> 93.4 us (0.943)
  the two profiles are of different devices: /device:TPU:520 before, /device:TPU:256 now
where the time goes in v3:
time: 93.4 us; the launch traced here: 92.9 us
  waiting for transfers between devices  47.5 us (51%)
  blocking collectives  18.7 us (20%)
  starting transfers between devices  11.7 us (13%)
  Pallas kernels  8.33 us (9%)
  local copies, waits for them, and re-layouts  4.26 us (5%)
  other arithmetic  2.28 us (2%)
    all_to_all x1, waiting for transfers between devices, body(): lax.all_to_all(qkv_out, 'head', split_axis=0, concat_axis=0, tiled=True)  41.9 us
    all_to_all x1, blocking collectives, body(): lax.all_to_all(joined, 'head', split_axis=0, concat_axis=0, tiled=True)  18.7 us
    all_to_all x1, starting transfers between devices, body(): lax.all_to_all(qkv_out, 'head', split_axis=0, concat_axis=0, tiled=True)  9.8 us
    pallas_call x2, Pallas kernels, attend(): pl.pallas_call(functools.partial(attention_kernel, blocks, before is not...  8.33 us
    ppermute x1, waiting for transfers between devices, from_behind(): lax.ppermute(value, axis, [(source, source + steps) for source in range(i...  5.56 us
    unnamed x15, local copies, waits for them, and re-layouts  2.8 us
    ppermute x1, starting transfers between devices, from_behind(): lax.ppermute(value, axis, [(source, source + steps) for source in range(i...  1.92 us
  transfers between devices with their start and end apart: 2, of which 2 were waited for; matrix products, arithmetic and copies ran while one was open for 1% of the time, Pallas kernels for 4%

profile of v3, /device:TPU:256, one launch (start us, length us, event | category | flops | bytes accessed | tf_op | source)
XLA Modules:
  0.0 92.9 jit_solution(16006294717105381253)
XLA Ops:
  0.0 0.0 copy-start.1
  0.0 1.2 %copy.16 = bf16[8,8,16,256]{3,2,1,0:T(8,128)(2,1)S(1)} copy(bf16[8,8,16,256]{3,1,2,0:T(8,128)(2,1)} %bitcast.18) | data formatting | bytes 1048576
  1.2 0.0 copy-start.2
  1.2 0.2 copy.11
  1.4 0.0 copy-done.1
  1.4 0.1 copy.17
  1.5 0.2 copy.12
  1.7 0.6 copy-done.2
  2.3 0.1 copy.18
  2.4 0.2 copy.13
  2.5 1.3 %maximum_bitcast_fusion = bf16[16,3,64,256]{3,2,1,0:T(8,128)(2,1)} fusion(bf16[1,64,16,256]{3,1,0,2:T(8,128)(2,1)S(1)} %copy.13, bf16[1,64,16,256]{3,1,0,2:T(8,128)(2,1)S(1)} %copy.12, bf16[1,64,16,256]{3,1,0,2:T(8,128)(2,1)S(1)} %copy.11), kind=kLoop, calls=%fused_computation | loop fusion | flops 1572864 | bytes 3145728 | tf_op jit(solution)/shard_map/transpose | solution.py:99
  3.8 0.0 copy-start.5
  3.9 0.0 copy-start.4
  3.9 9.8 %all-to-all-start = ((bf16[16,3,64,256]{3,2,1,0:T(8,128)(2,1)}), bf16[16,3,64,256]{3,2,1,0:T(8,128)(2,1)S(1)}, u32[]{:S(2)}, u32[]{:S(2)}) async-start(bf16[16,3,64,256]{3,2,1,0:T(8,128)(2,1)} %maximum_bitcast_fusion), calls=%async_computation | async-start | bytes 3145728 | tf_op jit(solution)/shard_map/all_to_all | solution.py:100
  13.7 41.9 %all-to-all-done.qkv_ref = bf16[16,3,64,256]{3,2,1,0:T(8,128)(2,1)S(1)} async-done(((bf16[16,3,64,256]{3,2,1,0:T(8,128)(2,1)}), bf16[16,3,64,256]{3,2,1,0:T(8,128)(2,1)S(1)}, u32[]{:S(2)}, u32[]{:S(2)}) %all-to-all-start) | async-done | bytes 1572896 | tf_op jit(solution)/shard_map/all_to_all | solution.py:100
  55.6 0.0 copy-start
  55.7 1.9 %collective-permute-start = (bf16[8,2,64,256]{3,2,1,0:T(8,128)(2,1)S(1)}, bf16[8,2,64,256]{3,2,1,0:T(8,128)(2,1)S(1)}, u32[]{:S(2)}, u32[]{:S(2)}) collective-permute-start(bf16[8,2,64,256]{3,2,1,0:T(8,128)(2,1)S(1)} %slice.4), channel_id=1, source_target_pairs={{0,16},{16,32},{32,48},{48,64},{64,80},{80,96},{96,112},{112,128},... | collective-permute-start | bytes 1572872 | tf_op jit(solution)/shard_map/ppermute | solution.py:19
  57.6 0.0 copy-done.5
  57.6 0.1 iota_compare_fusion
  57.7 0.1 broadcast_subtract_fusion
  57.7 0.0 copy-done.4
  57.7 0.2 and_reduce_fusion
  58.0 0.1 copy.10
  58.1 0.6 convert_element_type.3.flags_ref
  58.7 0.0 copy-done
  58.7 4.0 %shard_map.55.refs_1_ = bf16[16,64,256]{2,1,0:T(8,128)(2,1)} custom-call(s32[4,3]{1,0:T(4,128)} %convert_element_type.3.flags_ref, bf16[16,3,64,256]{3,2,1,0:T(8,128)(2,1)} %copy-done), custom_call_target="tpu_custom_call" | custom-call | tf_op jit(solution)/shard_map/pallas_call | solution.py:84
  62.7 5.6 %collective-permute-done.refs_0_ = bf16[8,2,64,256]{3,2,1,0:T(8,128)(2,1)S(1)} collective-permute-done((bf16[8,2,64,256]{3,2,1,0:T(8,128)(2,1)S(1)}, bf16[8,2,64,256]{3,2,1,0:T(8,128)(2,1)S(1)}, u32[]{:S(2)}, u32[]{:S(2)}) %collective-permute-start) | collective-permute-done | bytes 524320 | tf_op jit(solution)/shard_map/ppermute | solution.py:19
  68.3 0.0 copy-start.3
  68.3 0.8 copy-done.3
  69.1 4.3 %shard_map.56 = bf16[16,64,256]{2,1,0:T(8,128)(2,1)} custom-call(s32[4,3]{1,0:T(4,128)} %convert_element_type.3.flags_ref, bf16[16,3,64,256]{3,2,1,0:T(8,128)(2,1)} %copy-done, bf16[8,2,64,256]{3,2,1,0:T(8,128)(2,1)} %copy-done.3, bf16[16,64,256]{2,1,0:T(8,128)(2,1)} %shard_map.55.refs_1_), custom_call_target="tpu_custom_call" | custom-call | tf_op jit(solution)/shard_map/pallas_call | solution.py:84
  73.4 18.7 %all_to_all.10 = bf16[16,64,256]{2,1,0:T(8,128)(2,1)S(1)} all-to-all(bf16[16,64,256]{2,1,0:T(8,128)(2,1)} %shard_map.56), channel_id=1, replica_groups=mesh['blk'=64,'head'=16] {'head'}, dimensions={0} | all-to-all | bytes 1048576 | tf_op jit(solution)/shard_map/all_to_all | solution.py:112
  92.1 0.8 copy.15
  (3 shorter events, 0.0 us)
Async XLA Ops:
  0.0 1.4 %copy-start.1 = (bf16[64,4096]{1,0:T(8,128)(2,1)S(1)}, bf16[64,4096]{1,0:T(8,128)(2,1)}, u32[]{:S(2)}) copy-start(bf16[64,4096]{1,0:T(8,128)(2,1)} %param.6) | copy-start | bytes 1572868
  1.2 1.0 %copy-start.2 = (bf16[64,4096]{1,0:T(8,128)(2,1)S(1)}, bf16[64,4096]{1,0:T(8,128)(2,1)}, u32[]{:S(2)}) copy-start(bf16[64,4096]{1,0:T(8,128)(2,1)} %param.7) | copy-start | bytes 1572868
  3.8 53.7 %copy-start.5 = (s32[4]{0:T(128)S(1)}, s32[4]{0:T(128)}, u32[]{:S(2)}) copy-start(s32[4]{0:T(128)} %param.9) | copy-start | bytes 52
  3.9 53.9 %copy-start.4 = (s32[4,3]{1,0:T(4,128)S(1)}, s32[4,3]{1,0:T(4,128)}, u32[]{:S(2)}) copy-start(s32[4,3]{1,0:T(4,128)} %param.8) | copy-start | bytes 148
  3.9 51.8 %all-to-all-start = ((bf16[16,3,64,256]{3,2,1,0:T(8,128)(2,1)}), bf16[16,3,64,256]{3,2,1,0:T(8,128)(2,1)S(1)}, u32[]{:S(2)}, u32[]{:S(2)}) async-start(bf16[16,3,64,256]{3,2,1,0:T(8,128)(2,1)} %maximum_bitcast_fusion), calls=%async_computation | async-start | bytes 3145728 | tf_op jit(solution)/shard_map/all_to_all | solution.py:100
  55.6 3.1 %copy-start = (bf16[16,3,64,256]{3,2,1,0:T(8,128)(2,1)}, bf16[16,3,64,256]{3,2,1,0:T(8,128)(2,1)S(1)}, u32[]{:S(2)}) copy-start(bf16[16,3,64,256]{3,2,1,0:T(8,128)(2,1)S(1)} %all-to-all-done.qkv_ref) | copy-start | bytes 4718596
  55.7 12.6 %collective-permute-start = (bf16[8,2,64,256]{3,2,1,0:T(8,128)(2,1)S(1)}, bf16[8,2,64,256]{3,2,1,0:T(8,128)(2,1)S(1)}, u32[]{:S(2)}, u32[]{:S(2)}) collective-permute-start(bf16[8,2,64,256]{3,2,1,0:T(8,128)(2,1)S(1)} %slice.4), channel_id=1, source_target_pairs={{0,16},{16,32},{32,48},{48,64},{64,80},{80,96},{96,112},{112,128},... | collective-permute-start | bytes 1572872 | tf_op jit(solution)/shard_map/ppermute | solution.py:19
  68.3 0.8 copy-start.3

commit v4 on v3

--- a/solution.py
+++ b/solution.py
@@ -93,24 +93,26 @@
     peers = lax.axis_size("head")
     chunk, width = queries.shape
     cols = width // peers
+    local_heads = cols // HDIM
     per_block = BLOCK // chunk
     owned_blocks = peers // per_block
     reach = CYCLE - 1
-    qkv_out = jnp.stack((queries, keys, values)).reshape(3, chunk, peers, cols).transpose(2, 0, 1, 3)
-    qkv = lax.all_to_all(qkv_out, "head", split_axis=0, concat_axis=0, tiled=True)
-    before = from_behind(qkv[peers - reach * per_block :, 1:], "blk", 1)
     own = lax.axis_index("blk")
     target = own * owned_blocks + jnp.arange(owned_blocks, dtype=jnp.int32)
     distance = reach - jnp.arange(CYCLE, dtype=jnp.int32)
     used = jnp.arange(CYCLE, dtype=jnp.int32)[None, :] < block_counts[:, None]
     hits = used[:, None, :] & (block_lists[:, None, :] == (target[:, None] - distance[None, :])[:, :, None])
     flags = jnp.any(hits, axis=2).astype(jnp.int32)
-    late = tuple(range(min(reach, owned_blocks)))
-    early = tuple(range(len(late), owned_blocks))
-    joined = attend(early, flags, qkv, None, None) if early else None
-    joined = attend(late, flags, qkv, before, joined)
-    back = lax.all_to_all(joined, "head", split_axis=0, concat_axis=0, tiled=True)
-    return back.transpose(1, 0, 2).reshape(chunk, width)
+    stacked = jnp.stack((queries, keys, values)).reshape(3, chunk, peers, local_heads, HDIM)
+    outgoing = stacked.transpose(3, 2, 0, 1, 4)
+    results = []
+    for head in range(local_heads):
+        qkv = lax.all_to_all(outgoing[head], "head", split_axis=0, concat_axis=0, tiled=True)
+        before = from_behind(qkv[peers - reach * per_block :, 1:], "blk", 1)
+        joined = attend(tuple(range(owned_blocks)), flags, qkv, before, None)
+        results.append(lax.all_to_all(joined, "head", split_axis=0, concat_axis=0, tiled=True))
+    back = jnp.stack(results, axis=2)
+    return back.transpose(1, 0, 2, 3).reshape(chunk, width)
 
 
 def solution(mesh):

time: 93.4 us -> 109 us (1.17)
  the two profiles are of different devices: /device:TPU:256 before, /device:TPU:840 now
where the time goes in v4:
time: 109 us
  blocking collectives  49.2 us (45%)
  waiting for transfers between devices  24.2 us (22%)
  starting transfers between devices  19 us (17%)
  Pallas kernels  7.44 us (7%)
  local copies, waits for them, and re-layouts  7.35 us (7%)
  other arithmetic  1.19 us (1%)
    all_to_all x1, blocking collectives, body(): lax.all_to_all(outgoing[head], 'head', split_axis=0, concat_axis=0, tiled...  29.6 us
    ppermute x2, waiting for transfers between devices, from_behind(): lax.ppermute(value, axis, [(source, source + steps) for source in range(i...  24.2 us
    all_to_all x1, blocking collectives, body(): lax.all_to_all(joined, 'head', split_axis=0, concat_axis=0, tiled=True)  19.6 us
    all_to_all x1, starting transfers between devices, body(): lax.all_to_all(joined, 'head', split_axis=0, concat_axis=0, tiled=True)  8.67 us
    pallas_call x2, Pallas kernels, attend(): pl.pallas_call(functools.partial(attention_kernel, blocks, before is not...  7.44 us
    all_to_all x1, starting transfers between devices, body(): lax.all_to_all(outgoing[head], 'head', split_axis=0, concat_axis=0, tiled...  6.46 us
    ppermute x2, starting transfers between devices, from_behind(): lax.ppermute(value, axis, [(source, source + steps) for source in range(i...  3.84 us
    another operation x6, local copies, waits for them, and re-layouts, body(): jnp.stack((queries, keys, values))  2.81 us
  transfers between devices with their start and end apart: 4, of which 2 were waited for; matrix products, arithmetic and copies ran while one was open for 1% of the time, Pallas kernels for 7%

profile of v4, /device:TPU:840, one launch (start us, length us, event | category | flops | bytes accessed | tf_op | source)
XLA Modules:
  0.0 108.5 jit_solution(17133302152158111125)
XLA Ops:
  0.0 0.0 copy-start.2
  0.0 1.5 %stack.21 = bf16[1,64,16,2,128]{4,3,2,1,0:T(2,128)(2,1)S(1)} reshape(bf16[64,4096]{1,0:T(8,128)(2,1)} %param.5) | data formatting | bytes 1048576 | tf_op jit(solution)/shard_map/stack | solution.py:106
  1.5 0.0 copy-start.3
  1.5 0.2 copy.11
  1.7 0.0 copy-done.2
  1.7 0.4 stack.22
  2.1 0.2 copy.12
  2.3 0.2 copy-done.3
  2.5 0.4 stack.23
  2.9 0.2 copy.13
  3.1 0.2 maximum_bitcast_fusion
  3.3 1.0 slice_bitcast_fusion.1
  4.3 0.0 copy-start.7
  4.3 0.0 copy-start.6
  4.3 29.6 %all_to_all.20.qkv_ref = bf16[16,3,64,128]{3,2,1,0:T(8,128)(2,1)S(1)} all-to-all(bf16[16,3,64,128]{3,2,1,0:T(8,128)(2,1)S(1)} %get-tuple-element.5), channel_id=1, replica_groups=mesh['blk'=64,'head'=16] {'head'}, dimensions={0} | all-to-all | bytes 1572864 | tf_op jit(solution)/shard_map/all_to_all | solution.py:110
  33.9 0.0 copy-start.1
  33.9 6.5 %all-to-all-start.2 = ((bf16[16,3,64,128]{3,2,1,0:T(8,128)(2,1)}), bf16[16,3,64,128]{3,2,1,0:T(8,128)(2,1)S(1)}, u32[]{:S(2)}, u32[]{:S(2)}) async-start(bf16[16,3,64,128]{3,2,1,0:T(8,128)(2,1)} %get-tuple-element.6), calls=%async_computation.2 | async-start | bytes 1572864 | tf_op jit(solution)/shard_map/all_to_all | solution.py:110
  40.4 0.1 broadcast_subtract_fusion
  40.5 1.9 %collective-permute-start = (bf16[8,2,64,128]{3,2,1,0:T(8,128)(2,1)S(1)}, bf16[8,2,64,128]{3,2,1,0:T(8,128)(2,1)S(1)}, u32[]{:S(2)}, u32[]{:S(2)}) collective-permute-start(bf16[8,2,64,128]{3,2,1,0:T(8,128)(2,1)S(1)} %slice.17), channel_id=1, source_target_pairs={{0,16},{16,32},{32,48},{48,64},{64,80},{80,96},{96,112},{112,128},... | collective-permute-start | bytes 786440 | tf_op jit(solution)/shard_map/ppermute | solution.py:19
  42.4 0.0 copy-done.7
  42.5 0.1 iota_compare_fusion
  42.5 0.0 copy-done.6
  42.5 0.2 and_reduce_fusion
  42.7 0.1 copy.10
  42.9 0.6 convert_element_type.3.flags_ref
  43.5 17.5 %collective-permute-done.refs_0_ = bf16[8,2,64,128]{3,2,1,0:T(8,128)(2,1)S(1)} collective-permute-done((bf16[8,2,64,128]{3,2,1,0:T(8,128)(2,1)S(1)}, bf16[8,2,64,128]{3,2,1,0:T(8,128)(2,1)S(1)}, u32[]{:S(2)}, u32[]{:S(2)}) %collective-permute-start) | collective-permute-done | bytes 262176 | tf_op jit(solution)/shard_map/ppermute | solution.py:19
  60.9 0.0 copy-done.1
  60.9 0.0 copy-start.4
  60.9 0.7 copy-done.4
  61.6 3.7 %shard_map.55 = bf16[16,64,128]{2,1,0:T(8,128)(2,1)} custom-call(s32[4,3]{1,0:T(4,128)} %convert_element_type.3.flags_ref, bf16[16,3,64,128]{3,2,1,0:T(8,128)(2,1)} %copy-done.1, bf16[8,2,64,128]{3,2,1,0:T(8,128)(2,1)} %copy-done.4), custom_call_target="tpu_custom_call" | custom-call | tf_op jit(solution)/shard_map/pallas_call | solution.py:84
  65.3 0.0 all-to-all-done.2.qkv_ref
  65.3 0.0 copy-start
  65.3 8.7 %all-to-all-start.1 = ((bf16[16,64,128]{2,1,0:T(8,128)(2,1)}), bf16[16,64,128]{2,1,0:T(8,128)(2,1)S(1)}, u32[]{:S(2)}, u32[]{:S(2)}) async-start(bf16[16,64,128]{2,1,0:T(8,128)(2,1)} %shard_map.55), calls=%async_computation.1 | async-start | bytes 524288 | tf_op jit(solution)/shard_map/all_to_all | solution.py:113
  74.1 1.9 %collective-permute-start.1 = (bf16[8,2,64,128]{3,2,1,0:T(8,128)(2,1)S(1)}, bf16[8,2,64,128]{3,2,1,0:T(8,128)(2,1)S(1)}, u32[]{:S(2)}, u32[]{:S(2)}) collective-permute-start(bf16[8,2,64,128]{3,2,1,0:T(8,128)(2,1)S(1)} %slice.19), channel_id=1, source_target_pairs={{0,16},{16,32},{32,48},{48,64},{64,80},{80,96},{96,112},{112,128},... | collective-permute-start | bytes 786440 | tf_op jit(solution)/shard_map/ppermute | solution.py:19
  76.0 6.7 %collective-permute-done.1.refs_0_ = bf16[8,2,64,128]{3,2,1,0:T(8,128)(2,1)S(1)} collective-permute-done((bf16[8,2,64,128]{3,2,1,0:T(8,128)(2,1)S(1)}, bf16[8,2,64,128]{3,2,1,0:T(8,128)(2,1)S(1)}, u32[]{:S(2)}, u32[]{:S(2)}) %collective-permute-start.1) | collective-permute-done | bytes 262176 | tf_op jit(solution)/shard_map/ppermute | solution.py:19
  82.7 0.0 copy-done
  82.7 0.0 copy-start.5
  82.7 0.7 copy-done.5
  83.4 3.7 %shard_map.56 = bf16[16,64,128]{2,1,0:T(8,128)(2,1)} custom-call(s32[4,3]{1,0:T(4,128)} %convert_element_type.3.flags_ref, bf16[16,3,64,128]{3,2,1,0:T(8,128)(2,1)} %copy-done, bf16[8,2,64,128]{3,2,1,0:T(8,128)(2,1)} %copy-done.5), custom_call_target="tpu_custom_call" | custom-call | tf_op jit(solution)/shard_map/pallas_call | solution.py:84
  87.1 0.0 all-to-all-done.1
  87.2 19.6 %all_to_all.21 = bf16[16,64,128]{2,1,0:T(8,128)(2,1)S(1)} all-to-all(bf16[16,64,128]{2,1,0:T(8,128)(2,1)} %shard_map.56), channel_id=1, replica_groups=mesh['blk'=64,'head'=16] {'head'}, dimensions={0} | all-to-all | bytes 524288 | tf_op jit(solution)/shard_map/all_to_all | solution.py:113
  106.7 0.1 maximum_bitcast_fusion.1
  106.8 0.5 copy.14
  107.3 1.2 %reshape.63 = bf16[64,4096]{1,0:T(8,128)(2,1)} reshape(bf16[64,16,2,128]{3,2,1,0:T(2,128)(2,1)S(1)} %copy.14) | data formatting | bytes 1048576 | tf_op jit(solution)/shard_map/reshape | solution.py:115
  (4 shorter events, 0.0 us)
Async XLA Ops:
  0.0 1.7 %copy-start.2 = (bf16[64,4096]{1,0:T(8,128)(2,1)S(1)}, bf16[64,4096]{1,0:T(8,128)(2,1)}, u32[]{:S(2)}) copy-start(bf16[64,4096]{1,0:T(8,128)(2,1)} %param.6) | copy-start | bytes 1572868
  1.5 1.0 copy-start.3
  4.3 38.2 %copy-start.7 = (s32[4]{0:T(128)S(1)}, s32[4]{0:T(128)}, u32[]{:S(2)}) copy-start(s32[4]{0:T(128)} %param.9) | copy-start | bytes 52
  4.3 38.2 %copy-start.6 = (s32[4,3]{1,0:T(4,128)S(1)}, s32[4,3]{1,0:T(4,128)}, u32[]{:S(2)}) copy-start(s32[4,3]{1,0:T(4,128)} %param.8) | copy-start | bytes 148
  33.9 27.0 %copy-start.1 = (bf16[16,3,64,128]{3,2,1,0:T(8,128)(2,1)}, bf16[16,3,64,128]{3,2,1,0:T(8,128)(2,1)S(1)}, u32[]{:S(2)}) copy-start(bf16[16,3,64,128]{3,2,1,0:T(8,128)(2,1)S(1)} %all_to_all.20.qkv_ref) | copy-start | bytes 2359300
  33.9 31.4 %all-to-all-start.2 = ((bf16[16,3,64,128]{3,2,1,0:T(8,128)(2,1)}), bf16[16,3,64,128]{3,2,1,0:T(8,128)(2,1)S(1)}, u32[]{:S(2)}, u32[]{:S(2)}) async-start(bf16[16,3,64,128]{3,2,1,0:T(8,128)(2,1)} %get-tuple-element.6), calls=%async_computation.2 | async-start | bytes 1572864 | tf_op jit(solution)/shard_map/all_to_all | solution.py:110
  40.5 20.4 %collective-permute-start = (bf16[8,2,64,128]{3,2,1,0:T(8,128)(2,1)S(1)}, bf16[8,2,64,128]{3,2,1,0:T(8,128)(2,1)S(1)}, u32[]{:S(2)}, u32[]{:S(2)}) collective-permute-start(bf16[8,2,64,128]{3,2,1,0:T(8,128)(2,1)S(1)} %slice.17), channel_id=1, source_target_pairs={{0,16},{16,32},{32,48},{48,64},{64,80},{80,96},{96,112},{112,128},... | collective-permute-start | bytes 786440 | tf_op jit(solution)/shard_map/ppermute | solution.py:19
  60.9 0.7 copy-start.4
  65.3 17.4 %copy-start = (bf16[16,3,64,128]{3,2,1,0:T(8,128)(2,1)}, bf16[16,3,64,128]{3,2,1,0:T(8,128)(2,1)S(1)}, u32[]{:S(2)}) copy-start(bf16[16,3,64,128]{3,2,1,0:T(8,128)(2,1)S(1)} %all-to-all-done.2.qkv_ref) | copy-start | bytes 2359300
  65.3 21.8 %all-to-all-start.1 = ((bf16[16,64,128]{2,1,0:T(8,128)(2,1)}), bf16[16,64,128]{2,1,0:T(8,128)(2,1)S(1)}, u32[]{:S(2)}, u32[]{:S(2)}) async-start(bf16[16,64,128]{2,1,0:T(8,128)(2,1)} %shard_map.55), calls=%async_computation.1 | async-start | bytes 524288 | tf_op jit(solution)/shard_map/all_to_all | solution.py:113
  74.1 8.7 %collective-permute-start.1 = (bf16[8,2,64,128]{3,2,1,0:T(8,128)(2,1)S(1)}, bf16[8,2,64,128]{3,2,1,0:T(8,128)(2,1)S(1)}, u32[]{:S(2)}, u32[]{:S(2)}) collective-permute-start(bf16[8,2,64,128]{3,2,1,0:T(8,128)(2,1)S(1)} %slice.19), channel_id=1, source_target_pairs={{0,16},{16,32},{32,48},{48,64},{64,80},{80,96},{96,112},{112,128},... | collective-permute-start | bytes 786440 | tf_op jit(solution)/shard_map/ppermute | solution.py:19
  82.7 0.7 copy-start.5

commit v5 on v2

v5 whole, which is shorter than its diff:
```python
import jax
import jax.numpy as jnp
from jax import lax
from jax.experimental import pallas as pl
from jax.experimental.pallas import tpu as pltpu
from jax.sharding import PartitionSpec as P

HEADS = 32
HDIM = 128
BLOCK = 256
CYCLE = 3


def from_behind(value, axis, steps):
    count = lax.axis_size(axis)
    initial, last = (max(0, -steps), min(count, count - steps))
    return lax.ppermute(value, axis, [(source, source + steps) for source in range(initial, last)])


def attention_kernel(flags_ref, slots_ref, qkv_ref, before_ref, out_ref):
    peers, _, chunk, width = qkv_ref.shape
    per_block = BLOCK // chunk
    owned_blocks = peers // per_block
    local_heads = width // HDIM
    reach = CYCLE - 1
    halo = reach * per_block
    scale = 1.0 / HDIM**0.5
    row_pos = lax.broadcasted_iota(jnp.int32, (BLOCK, BLOCK), 0)
    col_pos = lax.broadcasted_iota(jnp.int32, (BLOCK, BLOCK), 1)
    causal = col_pos <= row_pos

    def gather(ref, first, t, cols, wrap):
        pieces = []
        for part in range(per_block):
            slot = slots_ref[first + part]
            if wrap:
                slot = slot % halo
            pieces.append(ref[slot, t, :, cols])
        return jnp.concatenate(pieces, axis=0)

    for local in range(owned_blocks):
        wanted = [flags_ref[local, place] != 0 for place in range(CYCLE)]
        masks = []
        for place in range(CYCLE):
            if place == reach:
                masks.append(causal & wanted[place])
            else:
                masks.append(jnp.broadcast_to(wanted[place], (BLOCK, BLOCK)))
        for head in range(local_heads):
            cols = slice(head * HDIM, (head + 1) * HDIM)
            q = gather(qkv_ref, local * per_block, 0, cols, False)
            parts = []
            for place in range(CYCLE):
                source = local - (reach - place)
                if source >= 0:
                    k = gather(qkv_ref, source * per_block, 1, cols, False)
                    v = gather(qkv_ref, source * per_block, 2, cols, False)
                else:
                    first = (source + owned_blocks) * per_block
                    k = gather(before_ref, first, 0, cols, True)
                    v = gather(before_ref, first, 1, cols, True)
                s = lax.dot_general(q, k, (((1,), (1,)), ((), ())), preferred_element_type=jnp.float32) * scale
                s = jnp.where(masks[place], s, -1e30)
                parts.append((s, v))
            top = jnp.max(parts[0][0], axis=1, keepdims=True)
            for s, _ in parts[1:]:
                top = jnp.maximum(top, jnp.max(s, axis=1, keepdims=True))
            total = None
            summed = None
            for place, (s, v) in enumerate(parts):
                w = jnp.where(masks[place], jnp.exp(s - top), 0.0)
                t = jnp.sum(w, axis=1, keepdims=True)
                o = jnp.dot(w.astype(jnp.bfloat16), v, preferred_element_type=jnp.float32)
                total = t if total is None else total + t
                summed = o if summed is None else summed + o
            result = (summed / total).astype(out_ref.dtype)
            for part in range(per_block):
                slot = slots_ref[local * per_block + part]
                out_ref[slot, :, cols] = result[part * chunk : (part + 1) * chunk]


def exchange(slabs, me, axis):
    peers = slabs.shape[0]
    got = [lax.dynamic_index_in_dim(slabs, me, 0, keepdims=False)]
    for step in range(1, peers):
        send = lax.dynamic_index_in_dim(slabs, me ^ step, 0, keepdims=False)
        got.append(lax.ppermute(send, axis, [(j, j ^ step) for j in range(peers)]))
    return jnp.stack(got)


def body(queries, keys, values, block_lists, block_counts):
    peers = lax.axis_size("head")
    chunk, width = queries.shape
    cols = width // peers
    per_block = BLOCK // chunk
    owned_blocks = peers // per_block
    reach = CYCLE - 1
    halo = reach * per_block
    own = lax.axis_index("blk")
    me = lax.axis_index("head").astype(jnp.int32)
    target = own * owned_blocks + jnp.arange(owned_blocks, dtype=jnp.int32)
    distance = reach - jnp.arange(CYCLE, dtype=jnp.int32)
    used = jnp.arange(CYCLE, dtype=jnp.int32)[None, :] < block_counts[:, None]
    hits = used[:, None, :] & (block_lists[:, None, :] == (target[:, None] - distance[None, :])[:, :, None])
    flags = jnp.any(hits, axis=2).astype(jnp.int32)
    slots = jnp.bitwise_xor(me, jnp.arange(peers, dtype=jnp.int32))
    outgoing = jnp.stack((queries, keys, values)).reshape(3, chunk, peers, cols).transpose(2, 0, 1, 3)
    qkv = exchange(outgoing, me, "head")
    tail = lax.dynamic_slice_in_dim(qkv[:, 1:], slots[peers - halo] - slots[peers - halo] % halo, halo, 0)
    before = from_behind(tail, "blk", 1)
    vmem = pl.BlockSpec(memory_space=pltpu.VMEM)
    smem = pl.BlockSpec(memory_space=pltpu.SMEM)
    joined = pl.pallas_call(
        attention_kernel,
        out_shape=jax.ShapeDtypeStruct((peers, chunk, cols), queries.dtype),
        in_specs=[smem, smem, vmem, vmem],
        out_specs=vmem,
    )(flags, slots, qkv, before)
    back = exchange(joined, jnp.int32(0), "head")
    ordered = jnp.take(back, slots, axis=0)
    return ordered.transpose(1, 0, 2).reshape(chunk, width)


def solution(mesh):
    return jax.shard_map(
        body,
        mesh=mesh,
        in_specs=(
            P(("blk", "head"), None),
            P(("blk", "head"), None),
            P(("blk", "head"), None),
            P("blk", None),
            P("blk"),
        ),
        out_specs=P(("blk", "head"), None),
        check_vma=False,
    )
```

time: 99 us -> 179 us (1.81)
  the two profiles are of different devices: /device:TPU:520 before, /device:TPU:768 now
where the time goes in v5:
time: 179 us; the launch traced here: 178 us
  starting transfers between devices  139 us (78%)
  waiting for transfers between devices  21.2 us (12%)
  local copies, waits for them, and re-layouts  7.45 us (4%)
  Pallas kernels  5.79 us (3%)
  between operations  3.55 us (2%)
    ppermute x30, starting transfers between devices, exchange(): got.append(lax.ppermute(send, axis, [(j, j ^ step) for j in range(peers)]))  137 us
    ppermute x30, waiting for transfers between devices, exchange(): got.append(lax.ppermute(send, axis, [(j, j ^ step) for j in range(peers)]))  11.6 us
    ppermute x1, waiting for transfers between devices, from_behind(): lax.ppermute(value, axis, [(source, source + steps) for source in range(i...  9.64 us
    pallas_call x1, Pallas kernels, body(): pl.pallas_call(attention_kernel, out_shape=jax.ShapeDtypeStruct((peers, c...  5.79 us
    unnamed x48, local copies, waits for them, and re-layouts  3.76 us
  transfers between devices with their start and end apart: 31, of which 4 were waited for; matrix products, arithmetic and copies ran while one was open for 1% of the time, Pallas kernels for 0%

profile of v5, /device:TPU:768, one launch (start us, length us, event | category | flops | bytes accessed | tf_op | source)
XLA Modules:
  0.0 178.1 jit_solution(13086302541874614015)
XLA Ops:
  0.0 1.2 copy.19
  1.2 0.2 copy_dynamic-update-slice_fusion.2
  1.9 0.2 copy_dynamic-update-slice_fusion
  2.1 0.2 dynamic-slice_bitcast_fusion
  2.3 3.4 %collective-permute-start = (bf16[3,64,256]{2,1,0:T(8,128)(2,1)S(1)}, bf16[3,64,256]{2,1,0:T(8,128)(2,1)S(1)}, u32[]{:S(2)}, u32[]{:S(2)}) collective-permute-start(bf16[3,64,256]{2,1,0:T(8,128)(2,1)S(1)} %get-tuple-element.19), channel_id=1, source_target_pairs={{0,1},{1,0},{2,3},{3,2},{4,5},{5,4},{6,7},{7,6},{8,9},{9,8},{10,11... | collective-permute-start | bytes 294920 | tf_op jit(solution)/shard_map/ppermute | solution.py:87
  5.7 4.6 %collective-permute-start.1 = (bf16[3,64,256]{2,1,0:T(8,128)(2,1)S(1)}, bf16[3,64,256]{2,1,0:T(8,128)(2,1)S(1)}, u32[]{:S(2)}, u32[]{:S(2)}) collective-permute-start(bf16[3,64,256]{2,1,0:T(8,128)(2,1)S(1)} %get-tuple-element.18), channel_id=1, source_target_pairs={{0,2},{1,3},{2,0},{3,1},{4,6},{5,7},{6,4},{7,5},{8,10},{9,11},{10,... | collective-permute-start | bytes 294920 | tf_op jit(solution)/shard_map/ppermute | solution.py:87
  10.4 2.4 %collective-permute-start.2 = (bf16[3,64,256]{2,1,0:T(8,128)(2,1)S(1)}, bf16[3,64,256]{2,1,0:T(8,128)(2,1)S(1)}, u32[]{:S(2)}, u32[]{:S(2)}) collective-permute-start(bf16[3,64,256]{2,1,0:T(8,128)(2,1)S(1)} %get-tuple-element.17), channel_id=1, source_target_pairs={{0,3},{1,2},{2,1},{3,0},{4,7},{5,6},{6,5},{7,4},{8,11},{9,10},{10,... | collective-permute-start | bytes 294920 | tf_op jit(solution)/shard_map/ppermute | solution.py:87
  12.8 4.5 %collective-permute-start.3 = (bf16[3,64,256]{2,1,0:T(8,128)(2,1)S(1)}, bf16[3,64,256]{2,1,0:T(8,128)(2,1)S(1)}, u32[]{:S(2)}, u32[]{:S(2)}) collective-permute-start(bf16[3,64,256]{2,1,0:T(8,128)(2,1)S(1)} %get-tuple-element.16), channel_id=1, source_target_pairs={{0,4},{1,5},{2,6},{3,7},{4,0},{5,1},{6,2},{7,3},{8,12},{9,13},{10,... | collective-permute-start | bytes 294920 | tf_op jit(solution)/shard_map/ppermute | solution.py:87
  17.3 2.0 %collective-permute-start.4 = (bf16[3,64,256]{2,1,0:T(8,128)(2,1)S(1)}, bf16[3,64,256]{2,1,0:T(8,128)(2,1)S(1)}, u32[]{:S(2)}, u32[]{:S(2)}) collective-permute-start(bf16[3,64,256]{2,1,0:T(8,128)(2,1)S(1)} %get-tuple-element.15), channel_id=1, source_target_pairs={{0,5},{1,4},{2,7},{3,6},{4,1},{5,0},{6,3},{7,2},{8,13},{9,12},{10,... | collective-permute-start | bytes 294920 | tf_op jit(solution)/shard_map/ppermute | solution.py:87
  19.3 0.6 slice.24
  22.6 7.9 %collective-permute-start.5 = (bf16[3,64,256]{2,1,0:T(8,128)(2,1)S(1)}, bf16[3,64,256]{2,1,0:T(8,128)(2,1)S(1)}, u32[]{:S(2)}, u32[]{:S(2)}) collective-permute-start(bf16[3,64,256]{2,1,0:T(8,128)(2,1)S(1)} %get-tuple-element.14), channel_id=1, source_target_pairs={{0,6},{1,7},{2,4},{3,5},{4,2},{5,3},{6,0},{7,1},{8,14},{9,15},{10,... | collective-permute-start | bytes 294920 | tf_op jit(solution)/shard_map/ppermute | solution.py:87
  30.5 2.2 %collective-permute-start.6 = (bf16[3,64,256]{2,1,0:T(8,128)(2,1)S(1)}, bf16[3,64,256]{2,1,0:T(8,128)(2,1)S(1)}, u32[]{:S(2)}, u32[]{:S(2)}) collective-permute-start(bf16[3,64,256]{2,1,0:T(8,128)(2,1)S(1)} %get-tuple-element.13), channel_id=1, source_target_pairs={{0,7},{1,6},{2,5},{3,4},{4,3},{5,2},{6,1},{7,0},{8,15},{9,14},{10,... | collective-permute-start | bytes 294920 | tf_op jit(solution)/shard_map/ppermute | solution.py:87
  32.7 7.7 %collective-permute-start.7 = (bf16[3,64,256]{2,1,0:T(8,128)(2,1)S(1)}, bf16[3,64,256]{2,1,0:T(8,128)(2,1)S(1)}, u32[]{:S(2)}, u32[]{:S(2)}) collective-permute-start(bf16[3,64,256]{2,1,0:T(8,128)(2,1)S(1)} %get-tuple-element.12), channel_id=1, source_target_pairs={{0,8},{1,9},{2,10},{3,11},{4,12},{5,13},{6,14},{7,15},{8,0},{9,1},... | collective-permute-start | bytes 294920 | tf_op jit(solution)/shard_map/ppermute | solution.py:87
  40.4 1.9 %collective-permute-start.8 = (bf16[3,64,256]{2,1,0:T(8,128)(2,1)S(1)}, bf16[3,64,256]{2,1,0:T(8,128)(2,1)S(1)}, u32[]{:S(2)}, u32[]{:S(2)}) collective-permute-start(bf16[3,64,256]{2,1,0:T(8,128)(2,1)S(1)} %get-tuple-element.11), channel_id=1, source_target_pairs={{0,9},{1,8},{2,11},{3,10},{4,13},{5,12},{6,15},{7,14},{8,1},{9,0},... | collective-permute-start | bytes 294920 | tf_op jit(solution)/shard_map/ppermute | solution.py:87
  42.4 10.9 %collective-permute-start.9 = (bf16[3,64,256]{2,1,0:T(8,128)(2,1)S(1)}, bf16[3,64,256]{2,1,0:T(8,128)(2,1)S(1)}, u32[]{:S(2)}, u32[]{:S(2)}) collective-permute-start(bf16[3,64,256]{2,1,0:T(8,128)(2,1)S(1)} %get-tuple-element.10), channel_id=1, source_target_pairs={{0,10},{1,11},{2,8},{3,9},{4,14},{5,15},{6,12},{7,13},{8,2},{9,3},... | collective-permute-start | bytes 294920 | tf_op jit(solution)/shard_map/ppermute | solution.py:87
  53.3 1.9 %collective-permute-start.10 = (bf16[3,64,256]{2,1,0:T(8,128)(2,1)S(1)}, bf16[3,64,256]{2,1,0:T(8,128)(2,1)S(1)}, u32[]{:S(2)}, u32[]{:S(2)}) collective-permute-start(bf16[3,64,256]{2,1,0:T(8,128)(2,1)S(1)} %get-tuple-element.9), channel_id=1, source_target_pairs={{0,11},{1,10},{2,9},{3,8},{4,15},{5,14},{6,13},{7,12},{8,3},{9,2},... | collective-permute-start | bytes 294920 | tf_op jit(solution)/shard_map/ppermute | solution.py:87
  55.3 6.2 %collective-permute-start.11 = (bf16[3,64,256]{2,1,0:T(8,128)(2,1)S(1)}, bf16[3,64,256]{2,1,0:T(8,128)(2,1)S(1)}, u32[]{:S(2)}, u32[]{:S(2)}) collective-permute-start(bf16[3,64,256]{2,1,0:T(8,128)(2,1)S(1)} %get-tuple-element.8), channel_id=1, source_target_pairs={{0,12},{1,13},{2,14},{3,15},{4,8},{5,9},{6,10},{7,11},{8,4},{9,5},... | collective-permute-start | bytes 294920 | tf_op jit(solution)/shard_map/ppermute | solution.py:87
  61.5 1.9 %collective-permute-start.12 = (bf16[3,64,256]{2,1,0:T(8,128)(2,1)S(1)}, bf16[3,64,256]{2,1,0:T(8,128)(2,1)S(1)}, u32[]{:S(2)}, u32[]{:S(2)}) collective-permute-start(bf16[3,64,256]{2,1,0:T(8,128)(2,1)S(1)} %get-tuple-element.7), channel_id=1, source_target_pairs={{0,13},{1,12},{2,15},{3,14},{4,9},{5,8},{6,11},{7,10},{8,5},{9,4},... | collective-permute-start | bytes 294920 | tf_op jit(solution)/shard_map/ppermute | solution.py:87
  63.5 9.1 %collective-permute-start.13 = (bf16[3,64,256]{2,1,0:T(8,128)(2,1)S(1)}, bf16[3,64,256]{2,1,0:T(8,128)(2,1)S(1)}, u32[]{:S(2)}, u32[]{:S(2)}) collective-permute-start(bf16[3,64,256]{2,1,0:T(8,128)(2,1)S(1)} %get-tuple-element.6), channel_id=1, source_target_pairs={{0,14},{1,15},{2,12},{3,13},{4,10},{5,11},{6,8},{7,9},{8,6},{9,7},... | collective-permute-start | bytes 294920 | tf_op jit(solution)/shard_map/ppermute | solution.py:87
  72.6 1.9 %collective-permute-start.14 = (bf16[3,64,256]{2,1,0:T(8,128)(2,1)S(1)}, bf16[3,64,256]{2,1,0:T(8,128)(2,1)S(1)}, u32[]{:S(2)}, u32[]{:S(2)}) collective-permute-start(bf16[3,64,256]{2,1,0:T(8,128)(2,1)S(1)} %get-tuple-element.5), channel_id=1, source_target_pairs={{0,15},{1,14},{2,13},{3,12},{4,11},{5,10},{6,9},{7,8},{8,7},{9,6},... | collective-permute-start | bytes 294920 | tf_op jit(solution)/shard_map/ppermute | solution.py:87
  74.7 1.1 collective-permute-done.13
  75.8 7.7 %collective-permute-done.14 = bf16[3,64,256]{2,1,0:T(8,128)(2,1)S(1)} collective-permute-done((bf16[3,64,256]{2,1,0:T(8,128)(2,1)S(1)}, bf16[3,64,256]{2,1,0:T(8,128)(2,1)S(1)}, u32[]{:S(2)}, u32[]{:S(2)}) %collective-permute-start.14) | collective-permute-done | bytes 98336 | tf_op jit(solution)/shard_map/ppermute | solution.py:87
  83.7 1.0 copy-done
  84.7 1.9 %collective-permute-start.15 = (bf16[8,2,64,256]{3,2,1,0:T(8,128)(2,1)S(1)}, bf16[8,2,64,256]{3,2,1,0:T(8,128)(2,1)S(1)}, u32[]{:S(2)}, u32[]{:S(2)}) collective-permute-start(bf16[8,2,64,256]{3,2,1,0:T(8,128)(2,1)S(1)} %constant_dynamic-slice_fusion), channel_id=1, source_target_pairs={{0,16},{16,32},{32,48},{48,64},{64,80},{80,96},{96,112},{112,128},... | collective-permute-start | bytes 1572872 | tf_op jit(solution)/shard_map/ppermute | solution.py:17
  86.7 0.2 and_reduce_fusion
  87.0 0.6 convert_element_type.3.flags_ref
  87.6 9.6 %collective-permute-done.15.before_ref = bf16[8,2,64,256]{3,2,1,0:T(8,128)(2,1)S(1)} collective-permute-done((bf16[8,2,64,256]{3,2,1,0:T(8,128)(2,1)S(1)}, bf16[8,2,64,256]{3,2,1,0:T(8,128)(2,1)S(1)}, u32[]{:S(2)}, u32[]{:S(2)}) %collective-permute-start.15) | collective-permute-done | bytes 524320 | tf_op jit(solution)/shard_map/ppermute | solution.py:17
  97.3 0.8 copy-done.1
  98.1 5.8 %shard_map.55 = bf16[16,64,256]{2,1,0:T(8,128)(2,1)} custom-call(s32[4,3]{1,0:T(4,128)} %convert_element_type.3.flags_ref, s32[16]{0:T(128)} %copy-done.5, bf16[16,3,64,256]{3,2,1,0:T(8,128)(2,1)} %copy-done, bf16[8,2,64,256]{3,2,1,0:T(8,128)(2,1)} %copy-done.1), custom_call_target="tpu_custom_call" | custom-call | tf_op jit(solution)/shard_map/pallas_call | solution.py:113
  103.8 1.0 slice_bitcast_fusion
  104.9 1.9 %collective-permute-start.16 = (bf16[64,256]{1,0:T(8,128)(2,1)S(1)}, bf16[64,256]{1,0:T(8,128)(2,1)S(1)}, u32[]{:S(2)}, u32[]{:S(2)}) collective-permute-start(bf16[64,256]{1,0:T(8,128)(2,1)S(1)} %get-tuple-element.34), channel_id=1, source_target_pairs={{0,1},{1,0},{2,3},{3,2},{4,5},{5,4},{6,7},{7,6},{8,9},{9,8},{10,11... | collective-permute-start | bytes 98312 | tf_op jit(solution)/shard_map/ppermute | solution.py:87
  106.8 3.8 %collective-permute-start.17 = (bf16[64,256]{1,0:T(8,128)(2,1)S(1)}, bf16[64,256]{1,0:T(8,128)(2,1)S(1)}, u32[]{:S(2)}, u32[]{:S(2)}) collective-permute-start(bf16[64,256]{1,0:T(8,128)(2,1)S(1)} %get-tuple-element.33), channel_id=1, source_target_pairs={{0,2},{1,3},{2,0},{3,1},{4,6},{5,7},{6,4},{7,5},{8,10},{9,11},{10,... | collective-permute-start | bytes 98312 | tf_op jit(solution)/shard_map/ppermute | solution.py:87
  110.7 4.7 %collective-permute-start.18 = (bf16[64,256]{1,0:T(8,128)(2,1)S(1)}, bf16[64,256]{1,0:T(8,128)(2,1)S(1)}, u32[]{:S(2)}, u32[]{:S(2)}) collective-permute-start(bf16[64,256]{1,0:T(8,128)(2,1)S(1)} %get-tuple-element.32), channel_id=1, source_target_pairs={{0,3},{1,2},{2,1},{3,0},{4,7},{5,6},{6,5},{7,4},{8,11},{9,10},{10,... | collective-permute-start | bytes 98312 | tf_op jit(solution)/shard_map/ppermute | solution.py:87
  115.3 5.0 %collective-permute-start.19 = (bf16[64,256]{1,0:T(8,128)(2,1)S(1)}, bf16[64,256]{1,0:T(8,128)(2,1)S(1)}, u32[]{:S(2)}, u32[]{:S(2)}) collective-permute-start(bf16[64,256]{1,0:T(8,128)(2,1)S(1)} %get-tuple-element.31), channel_id=1, source_target_pairs={{0,4},{1,5},{2,6},{3,7},{4,0},{5,1},{6,2},{7,3},{8,12},{9,13},{10,... | collective-permute-start | bytes 98312 | tf_op jit(solution)/shard_map/ppermute | solution.py:87
  120.4 1.9 %collective-permute-start.20 = (bf16[64,256]{1,0:T(8,128)(2,1)S(1)}, bf16[64,256]{1,0:T(8,128)(2,1)S(1)}, u32[]{:S(2)}, u32[]{:S(2)}) collective-permute-start(bf16[64,256]{1,0:T(8,128)(2,1)S(1)} %get-tuple-element.30), channel_id=1, source_target_pairs={{0,5},{1,4},{2,7},{3,6},{4,1},{5,0},{6,3},{7,2},{8,13},{9,12},{10,... | collective-permute-start | bytes 98312 | tf_op jit(solution)/shard_map/ppermute | solution.py:87
  122.3 5.6 %collective-permute-start.21 = (bf16[64,256]{1,0:T(8,128)(2,1)S(1)}, bf16[64,256]{1,0:T(8,128)(2,1)S(1)}, u32[]{:S(2)}, u32[]{:S(2)}) collective-permute-start(bf16[64,256]{1,0:T(8,128)(2,1)S(1)} %get-tuple-element.29), channel_id=1, source_target_pairs={{0,6},{1,7},{2,4},{3,5},{4,2},{5,3},{6,0},{7,1},{8,14},{9,15},{10,... | collective-permute-start | bytes 98312 | tf_op jit(solution)/shard_map/ppermute | solution.py:87
  128.0 4.1 %collective-permute-start.22 = (bf16[64,256]{1,0:T(8,128)(2,1)S(1)}, bf16[64,256]{1,0:T(8,128)(2,1)S(1)}, u32[]{:S(2)}, u32[]{:S(2)}) collective-permute-start(bf16[64,256]{1,0:T(8,128)(2,1)S(1)} %get-tuple-element.28), channel_id=1, source_target_pairs={{0,7},{1,6},{2,5},{3,4},{4,3},{5,2},{6,1},{7,0},{8,15},{9,14},{10,... | collective-permute-start | bytes 98312 | tf_op jit(solution)/shard_map/ppermute | solution.py:87
  132.1 3.6 %collective-permute-start.23 = (bf16[64,256]{1,0:T(8,128)(2,1)S(1)}, bf16[64,256]{1,0:T(8,128)(2,1)S(1)}, u32[]{:S(2)}, u32[]{:S(2)}) collective-permute-start(bf16[64,256]{1,0:T(8,128)(2,1)S(1)} %get-tuple-element.27), channel_id=1, source_target_pairs={{0,8},{1,9},{2,10},{3,11},{4,12},{5,13},{6,14},{7,15},{8,0},{9,1},... | collective-permute-start | bytes 98312 | tf_op jit(solution)/shard_map/ppermute | solution.py:87
  135.8 4.9 %collective-permute-start.24 = (bf16[64,256]{1,0:T(8,128)(2,1)S(1)}, bf16[64,256]{1,0:T(8,128)(2,1)S(1)}, u32[]{:S(2)}, u32[]{:S(2)}) collective-permute-start(bf16[64,256]{1,0:T(8,128)(2,1)S(1)} %get-tuple-element.26), channel_id=1, source_target_pairs={{0,9},{1,8},{2,11},{3,10},{4,13},{5,12},{6,15},{7,14},{8,1},{9,0},... | collective-permute-start | bytes 98312 | tf_op jit(solution)/shard_map/ppermute | solution.py:87
  140.7 5.9 %collective-permute-start.25 = (bf16[64,256]{1,0:T(8,128)(2,1)S(1)}, bf16[64,256]{1,0:T(8,128)(2,1)S(1)}, u32[]{:S(2)}, u32[]{:S(2)}) collective-permute-start(bf16[64,256]{1,0:T(8,128)(2,1)S(1)} %get-tuple-element.25), channel_id=1, source_target_pairs={{0,10},{1,11},{2,8},{3,9},{4,14},{5,15},{6,12},{7,13},{8,2},{9,3},... | collective-permute-start | bytes 98312 | tf_op jit(solution)/shard_map/ppermute | solution.py:87
  146.7 8.0 %collective-permute-start.26 = (bf16[64,256]{1,0:T(8,128)(2,1)S(1)}, bf16[64,256]{1,0:T(8,128)(2,1)S(1)}, u32[]{:S(2)}, u32[]{:S(2)}) collective-permute-start(bf16[64,256]{1,0:T(8,128)(2,1)S(1)} %get-tuple-element.24), channel_id=1, source_target_pairs={{0,11},{1,10},{2,9},{3,8},{4,15},{5,14},{6,13},{7,12},{8,3},{9,2},... | collective-permute-start | bytes 98312 | tf_op jit(solution)/shard_map/ppermute | solution.py:87
  154.7 2.7 %collective-permute-start.27 = (bf16[64,256]{1,0:T(8,128)(2,1)S(1)}, bf16[64,256]{1,0:T(8,128)(2,1)S(1)}, u32[]{:S(2)}, u32[]{:S(2)}) collective-permute-start(bf16[64,256]{1,0:T(8,128)(2,1)S(1)} %get-tuple-element.23), channel_id=1, source_target_pairs={{0,12},{1,13},{2,14},{3,15},{4,8},{5,9},{6,10},{7,11},{8,4},{9,5},... | collective-permute-start | bytes 98312 | tf_op jit(solution)/shard_map/ppermute | solution.py:87
  157.5 2.8 %collective-permute-start.28 = (bf16[64,256]{1,0:T(8,128)(2,1)S(1)}, bf16[64,256]{1,0:T(8,128)(2,1)S(1)}, u32[]{:S(2)}, u32[]{:S(2)}) collective-permute-start(bf16[64,256]{1,0:T(8,128)(2,1)S(1)} %get-tuple-element.22), channel_id=1, source_target_pairs={{0,13},{1,12},{2,15},{3,14},{4,9},{5,8},{6,11},{7,10},{8,5},{9,4},... | collective-permute-start | bytes 98312 | tf_op jit(solution)/shard_map/ppermute | solution.py:87
  160.3 6.2 %collective-permute-start.29 = (bf16[64,256]{1,0:T(8,128)(2,1)S(1)}, bf16[64,256]{1,0:T(8,128)(2,1)S(1)}, u32[]{:S(2)}, u32[]{:S(2)}) collective-permute-start(bf16[64,256]{1,0:T(8,128)(2,1)S(1)} %get-tuple-element.21), channel_id=1, source_target_pairs={{0,14},{1,15},{2,12},{3,13},{4,10},{5,11},{6,8},{7,9},{8,6},{9,7},... | collective-permute-start | bytes 98312 | tf_op jit(solution)/shard_map/ppermute | solution.py:87
  166.5 7.2 %collective-permute-start.30 = (bf16[64,256]{1,0:T(8,128)(2,1)S(1)}, bf16[64,256]{1,0:T(8,128)(2,1)S(1)}, u32[]{:S(2)}, u32[]{:S(2)}) collective-permute-start(bf16[64,256]{1,0:T(8,128)(2,1)S(1)} %get-tuple-element.20), channel_id=1, source_target_pairs={{0,15},{1,14},{2,13},{3,12},{4,11},{5,10},{6,9},{7,8},{8,7},{9,6},... | collective-permute-start | bytes 98312 | tf_op jit(solution)/shard_map/ppermute | solution.py:87
  173.9 2.7 %collective-permute-done.30 = bf16[64,256]{1,0:T(8,128)(2,1)S(1)} collective-permute-done((bf16[64,256]{1,0:T(8,128)(2,1)S(1)}, bf16[64,256]{1,0:T(8,128)(2,1)S(1)}, u32[]{:S(2)}, u32[]{:S(2)}) %collective-permute-start.30) | collective-permute-done | bytes 32800 | tf_op jit(solution)/shard_map/ppermute | solution.py:87
  176.6 0.6 gather_fusion
  177.3 0.8 copy.18
  (85 shorter events, 1.2 us)
Async XLA Ops:
  0.0 1.4 copy-start.2
  0.0 1.5 copy-start.3
  2.3 20.2 %collective-permute-start = (bf16[3,64,256]{2,1,0:T(8,128)(2,1)S(1)}, bf16[3,64,256]{2,1,0:T(8,128)(2,1)S(1)}, u32[]{:S(2)}, u32[]{:S(2)}) collective-permute-start(bf16[3,64,256]{2,1,0:T(8,128)(2,1)S(1)} %get-tuple-element.19), channel_id=1, source_target_pairs={{0,1},{1,0},{2,3},{3,2},{4,5},{5,4},{6,7},{7,6},{8,9},{9,8},{10,11... | collective-permute-start | bytes 294920 | tf_op jit(solution)/shard_map/ppermute | solution.py:87
  5.7 24.7 %collective-permute-start.1 = (bf16[3,64,256]{2,1,0:T(8,128)(2,1)S(1)}, bf16[3,64,256]{2,1,0:T(8,128)(2,1)S(1)}, u32[]{:S(2)}, u32[]{:S(2)}) collective-permute-start(bf16[3,64,256]{2,1,0:T(8,128)(2,1)S(1)} %get-tuple-element.18), channel_id=1, source_target_pairs={{0,2},{1,3},{2,0},{3,1},{4,6},{5,7},{6,4},{7,5},{8,10},{9,11},{10,... | collective-permute-start | bytes 294920 | tf_op jit(solution)/shard_map/ppermute | solution.py:87
  10.4 22.3 %collective-permute-start.2 = (bf16[3,64,256]{2,1,0:T(8,128)(2,1)S(1)}, bf16[3,64,256]{2,1,0:T(8,128)(2,1)S(1)}, u32[]{:S(2)}, u32[]{:S(2)}) collective-permute-start(bf16[3,64,256]{2,1,0:T(8,128)(2,1)S(1)} %get-tuple-element.17), channel_id=1, source_target_pairs={{0,3},{1,2},{2,1},{3,0},{4,7},{5,6},{6,5},{7,4},{8,11},{9,10},{10,... | collective-permute-start | bytes 294920 | tf_op jit(solution)/shard_map/ppermute | solution.py:87
  12.8 27.7 %collective-permute-start.3 = (bf16[3,64,256]{2,1,0:T(8,128)(2,1)S(1)}, bf16[3,64,256]{2,1,0:T(8,128)(2,1)S(1)}, u32[]{:S(2)}, u32[]{:S(2)}) collective-permute-start(bf16[3,64,256]{2,1,0:T(8,128)(2,1)S(1)} %get-tuple-element.16), channel_id=1, source_target_pairs={{0,4},{1,5},{2,6},{3,7},{4,0},{5,1},{6,2},{7,3},{8,12},{9,13},{10,... | collective-permute-start | bytes 294920 | tf_op jit(solution)/shard_map/ppermute | solution.py:87
  17.3 25.1 %collective-permute-start.4 = (bf16[3,64,256]{2,1,0:T(8,128)(2,1)S(1)}, bf16[3,64,256]{2,1,0:T(8,128)(2,1)S(1)}, u32[]{:S(2)}, u32[]{:S(2)}) collective-permute-start(bf16[3,64,256]{2,1,0:T(8,128)(2,1)S(1)} %get-tuple-element.15), channel_id=1, source_target_pairs={{0,5},{1,4},{2,7},{3,6},{4,1},{5,0},{6,3},{7,2},{8,13},{9,12},{10,... | collective-permute-start | bytes 294920 | tf_op jit(solution)/shard_map/ppermute | solution.py:87
  19.2 64.2 %copy-start.5 = (s32[16]{0:T(128)}, s32[16]{0:T(128)S(1)}, u32[]{:S(2)}) copy-start(s32[16]{0:T(128)S(1)} %iota_xor_fusion.slots_ref) | copy-start | bytes 196
  22.6 30.8 %collective-permute-start.5 = (bf16[3,64,256]{2,1,0:T(8,128)(2,1)S(1)}, bf16[3,64,256]{2,1,0:T(8,128)(2,1)S(1)}, u32[]{:S(2)}, u32[]{:S(2)}) collective-permute-start(bf16[3,64,256]{2,1,0:T(8,128)(2,1)S(1)} %get-tuple-element.14), channel_id=1, source_target_pairs={{0,6},{1,7},{2,4},{3,5},{4,2},{5,3},{6,0},{7,1},{8,14},{9,15},{10,... | collective-permute-start | bytes 294920 | tf_op jit(solution)/shard_map/ppermute | solution.py:87
  30.5 24.8 %collective-permute-start.6 = (bf16[3,64,256]{2,1,0:T(8,128)(2,1)S(1)}, bf16[3,64,256]{2,1,0:T(8,128)(2,1)S(1)}, u32[]{:S(2)}, u32[]{:S(2)}) collective-permute-start(bf16[3,64,256]{2,1,0:T(8,128)(2,1)S(1)} %get-tuple-element.13), channel_id=1, source_target_pairs={{0,7},{1,6},{2,5},{3,4},{4,3},{5,2},{6,1},{7,0},{8,15},{9,14},{10,... | collective-permute-start | bytes 294920 | tf_op jit(solution)/shard_map/ppermute | solution.py:87
  32.7 28.8 %collective-permute-start.7 = (bf16[3,64,256]{2,1,0:T(8,128)(2,1)S(1)}, bf16[3,64,256]{2,1,0:T(8,128)(2,1)S(1)}, u32[]{:S(2)}, u32[]{:S(2)}) collective-permute-start(bf16[3,64,256]{2,1,0:T(8,128)(2,1)S(1)} %get-tuple-element.12), channel_id=1, source_target_pairs={{0,8},{1,9},{2,10},{3,11},{4,12},{5,13},{6,14},{7,15},{8,0},{9,1},... | collective-permute-start | bytes 294920 | tf_op jit(solution)/shard_map/ppermute | solution.py:87
  40.4 23.0 %collective-permute-start.8 = (bf16[3,64,256]{2,1,0:T(8,128)(2,1)S(1)}, bf16[3,64,256]{2,1,0:T(8,128)(2,1)S(1)}, u32[]{:S(2)}, u32[]{:S(2)}) collective-permute-start(bf16[3,64,256]{2,1,0:T(8,128)(2,1)S(1)} %get-tuple-element.11), channel_id=1, source_target_pairs={{0,9},{1,8},{2,11},{3,10},{4,13},{5,12},{6,15},{7,14},{8,1},{9,0},... | collective-permute-start | bytes 294920 | tf_op jit(solution)/shard_map/ppermute | solution.py:87
  42.4 30.2 %collective-permute-start.9 = (bf16[3,64,256]{2,1,0:T(8,128)(2,1)S(1)}, bf16[3,64,256]{2,1,0:T(8,128)(2,1)S(1)}, u32[]{:S(2)}, u32[]{:S(2)}) collective-permute-start(bf16[3,64,256]{2,1,0:T(8,128)(2,1)S(1)} %get-tuple-element.10), channel_id=1, source_target_pairs={{0,10},{1,11},{2,8},{3,9},{4,14},{5,15},{6,12},{7,13},{8,2},{9,3},... | collective-permute-start | bytes 294920 | tf_op jit(solution)/shard_map/ppermute | solution.py:87
  53.3 21.2 %collective-permute-start.10 = (bf16[3,64,256]{2,1,0:T(8,128)(2,1)S(1)}, bf16[3,64,256]{2,1,0:T(8,128)(2,1)S(1)}, u32[]{:S(2)}, u32[]{:S(2)}) collective-permute-start(bf16[3,64,256]{2,1,0:T(8,128)(2,1)S(1)} %get-tuple-element.9), channel_id=1, source_target_pairs={{0,11},{1,10},{2,9},{3,8},{4,15},{5,14},{6,13},{7,12},{8,3},{9,2},... | collective-permute-start | bytes 294920 | tf_op jit(solution)/shard_map/ppermute | solution.py:87
  55.3 19.3 %collective-permute-start.11 = (bf16[3,64,256]{2,1,0:T(8,128)(2,1)S(1)}, bf16[3,64,256]{2,1,0:T(8,128)(2,1)S(1)}, u32[]{:S(2)}, u32[]{:S(2)}) collective-permute-start(bf16[3,64,256]{2,1,0:T(8,128)(2,1)S(1)} %get-tuple-element.8), channel_id=1, source_target_pairs={{0,12},{1,13},{2,14},{3,15},{4,8},{5,9},{6,10},{7,11},{8,4},{9,5},... | collective-permute-start | bytes 294920 | tf_op jit(solution)/shard_map/ppermute | solution.py:87
  61.5 13.1 %collective-permute-start.12 = (bf16[3,64,256]{2,1,0:T(8,128)(2,1)S(1)}, bf16[3,64,256]{2,1,0:T(8,128)(2,1)S(1)}, u32[]{:S(2)}, u32[]{:S(2)}) collective-permute-start(bf16[3,64,256]{2,1,0:T(8,128)(2,1)S(1)} %get-tuple-element.7), channel_id=1, source_target_pairs={{0,13},{1,12},{2,15},{3,14},{4,9},{5,8},{6,11},{7,10},{8,5},{9,4},... | collective-permute-start | bytes 294920 | tf_op jit(solution)/shard_map/ppermute | solution.py:87
  63.5 12.3 %collective-permute-start.13 = (bf16[3,64,256]{2,1,0:T(8,128)(2,1)S(1)}, bf16[3,64,256]{2,1,0:T(8,128)(2,1)S(1)}, u32[]{:S(2)}, u32[]{:S(2)}) collective-permute-start(bf16[3,64,256]{2,1,0:T(8,128)(2,1)S(1)} %get-tuple-element.6), channel_id=1, source_target_pairs={{0,14},{1,15},{2,12},{3,13},{4,10},{5,11},{6,8},{7,9},{8,6},{9,7},... | collective-permute-start | bytes 294920 | tf_op jit(solution)/shard_map/ppermute | solution.py:87
  72.6 10.8 %collective-permute-start.14 = (bf16[3,64,256]{2,1,0:T(8,128)(2,1)S(1)}, bf16[3,64,256]{2,1,0:T(8,128)(2,1)S(1)}, u32[]{:S(2)}, u32[]{:S(2)}) collective-permute-start(bf16[3,64,256]{2,1,0:T(8,128)(2,1)S(1)} %get-tuple-element.5), channel_id=1, source_target_pairs={{0,15},{1,14},{2,13},{3,12},{4,11},{5,10},{6,9},{7,8},{8,7},{9,6},... | collective-permute-start | bytes 294920 | tf_op jit(solution)/shard_map/ppermute | solution.py:87
  83.5 1.2 copy-start
  83.5 3.1 %copy-start.6 = (s32[4]{0:T(128)S(1)}, s32[4]{0:T(128)}, u32[]{:S(2)}) copy-start(s32[4]{0:T(128)} %param.9) | copy-start | bytes 52
  83.5 3.2 %copy-start.4 = (s32[4,3]{1,0:T(4,128)S(1)}, s32[4,3]{1,0:T(4,128)}, u32[]{:S(2)}) copy-start(s32[4,3]{1,0:T(4,128)} %param.8) | copy-start | bytes 148
  84.7 12.6 %collective-permute-start.15 = (bf16[8,2,64,256]{3,2,1,0:T(8,128)(2,1)S(1)}, bf16[8,2,64,256]{3,2,1,0:T(8,128)(2,1)S(1)}, u32[]{:S(2)}, u32[]{:S(2)}) collective-permute-start(bf16[8,2,64,256]{3,2,1,0:T(8,128)(2,1)S(1)} %constant_dynamic-slice_fusion), channel_id=1, source_target_pairs={{0,16},{16,32},{32,48},{48,64},{64,80},{80,96},{96,112},{112,128},... | collective-permute-start | bytes 1572872 | tf_op jit(solution)/shard_map/ppermute | solution.py:17
  97.3 0.8 copy-start.1
  104.9 17.4 %collective-permute-start.16 = (bf16[64,256]{1,0:T(8,128)(2,1)S(1)}, bf16[64,256]{1,0:T(8,128)(2,1)S(1)}, u32[]{:S(2)}, u32[]{:S(2)}) collective-permute-start(bf16[64,256]{1,0:T(8,128)(2,1)S(1)} %get-tuple-element.34), channel_id=1, source_target_pairs={{0,1},{1,0},{2,3},{3,2},{4,5},{5,4},{6,7},{7,6},{8,9},{9,8},{10,11... | collective-permute-start | bytes 98312 | tf_op jit(solution)/shard_map/ppermute | solution.py:87
  106.8 21.1 %collective-permute-start.17 = (bf16[64,256]{1,0:T(8,128)(2,1)S(1)}, bf16[64,256]{1,0:T(8,128)(2,1)S(1)}, u32[]{:S(2)}, u32[]{:S(2)}) collective-permute-start(bf16[64,256]{1,0:T(8,128)(2,1)S(1)} %get-tuple-element.33), channel_id=1, source_target_pairs={{0,2},{1,3},{2,0},{3,1},{4,6},{5,7},{6,4},{7,5},{8,10},{9,11},{10,... | collective-permute-start | bytes 98312 | tf_op jit(solution)/shard_map/ppermute | solution.py:87
  110.7 21.4 %collective-permute-start.18 = (bf16[64,256]{1,0:T(8,128)(2,1)S(1)}, bf16[64,256]{1,0:T(8,128)(2,1)S(1)}, u32[]{:S(2)}, u32[]{:S(2)}) collective-permute-start(bf16[64,256]{1,0:T(8,128)(2,1)S(1)} %get-tuple-element.32), channel_id=1, source_target_pairs={{0,3},{1,2},{2,1},{3,0},{4,7},{5,6},{6,5},{7,4},{8,11},{9,10},{10,... | collective-permute-start | bytes 98312 | tf_op jit(solution)/shard_map/ppermute | solution.py:87
  115.3 20.4 %collective-permute-start.19 = (bf16[64,256]{1,0:T(8,128)(2,1)S(1)}, bf16[64,256]{1,0:T(8,128)(2,1)S(1)}, u32[]{:S(2)}, u32[]{:S(2)}) collective-permute-start(bf16[64,256]{1,0:T(8,128)(2,1)S(1)} %get-tuple-element.31), channel_id=1, source_target_pairs={{0,4},{1,5},{2,6},{3,7},{4,0},{5,1},{6,2},{7,3},{8,12},{9,13},{10,... | collective-permute-start | bytes 98312 | tf_op jit(solution)/shard_map/ppermute | solution.py:87
  120.4 20.3 %collective-permute-start.20 = (bf16[64,256]{1,0:T(8,128)(2,1)S(1)}, bf16[64,256]{1,0:T(8,128)(2,1)S(1)}, u32[]{:S(2)}, u32[]{:S(2)}) collective-permute-start(bf16[64,256]{1,0:T(8,128)(2,1)S(1)} %get-tuple-element.30), channel_id=1, source_target_pairs={{0,5},{1,4},{2,7},{3,6},{4,1},{5,0},{6,3},{7,2},{8,13},{9,12},{10,... | collective-permute-start | bytes 98312 | tf_op jit(solution)/shard_map/ppermute | solution.py:87
  122.3 24.4 %collective-permute-start.21 = (bf16[64,256]{1,0:T(8,128)(2,1)S(1)}, bf16[64,256]{1,0:T(8,128)(2,1)S(1)}, u32[]{:S(2)}, u32[]{:S(2)}) collective-permute-start(bf16[64,256]{1,0:T(8,128)(2,1)S(1)} %get-tuple-element.29), channel_id=1, source_target_pairs={{0,6},{1,7},{2,4},{3,5},{4,2},{5,3},{6,0},{7,1},{8,14},{9,15},{10,... | collective-permute-start | bytes 98312 | tf_op jit(solution)/shard_map/ppermute | solution.py:87
  128.0 26.8 %collective-permute-start.22 = (bf16[64,256]{1,0:T(8,128)(2,1)S(1)}, bf16[64,256]{1,0:T(8,128)(2,1)S(1)}, u32[]{:S(2)}, u32[]{:S(2)}) collective-permute-start(bf16[64,256]{1,0:T(8,128)(2,1)S(1)} %get-tuple-element.28), channel_id=1, source_target_pairs={{0,7},{1,6},{2,5},{3,4},{4,3},{5,2},{6,1},{7,0},{8,15},{9,14},{10,... | collective-permute-start | bytes 98312 | tf_op jit(solution)/shard_map/ppermute | solution.py:87
  132.1 25.4 %collective-permute-start.23 = (bf16[64,256]{1,0:T(8,128)(2,1)S(1)}, bf16[64,256]{1,0:T(8,128)(2,1)S(1)}, u32[]{:S(2)}, u32[]{:S(2)}) collective-permute-start(bf16[64,256]{1,0:T(8,128)(2,1)S(1)} %get-tuple-element.27), channel_id=1, source_target_pairs={{0,8},{1,9},{2,10},{3,11},{4,12},{5,13},{6,14},{7,15},{8,0},{9,1},... | collective-permute-start | bytes 98312 | tf_op jit(solution)/shard_map/ppermute | solution.py:87
  135.8 24.5 %collective-permute-start.24 = (bf16[64,256]{1,0:T(8,128)(2,1)S(1)}, bf16[64,256]{1,0:T(8,128)(2,1)S(1)}, u32[]{:S(2)}, u32[]{:S(2)}) collective-permute-start(bf16[64,256]{1,0:T(8,128)(2,1)S(1)} %get-tuple-element.26), channel_id=1, source_target_pairs={{0,9},{1,8},{2,11},{3,10},{4,13},{5,12},{6,15},{7,14},{8,1},{9,0},... | collective-permute-start | bytes 98312 | tf_op jit(solution)/shard_map/ppermute | solution.py:87
  140.7 25.8 %collective-permute-start.25 = (bf16[64,256]{1,0:T(8,128)(2,1)S(1)}, bf16[64,256]{1,0:T(8,128)(2,1)S(1)}, u32[]{:S(2)}, u32[]{:S(2)}) collective-permute-start(bf16[64,256]{1,0:T(8,128)(2,1)S(1)} %get-tuple-element.25), channel_id=1, source_target_pairs={{0,10},{1,11},{2,8},{3,9},{4,14},{5,15},{6,12},{7,13},{8,2},{9,3},... | collective-permute-start | bytes 98312 | tf_op jit(solution)/shard_map/ppermute | solution.py:87
  146.7 27.1 %collective-permute-start.26 = (bf16[64,256]{1,0:T(8,128)(2,1)S(1)}, bf16[64,256]{1,0:T(8,128)(2,1)S(1)}, u32[]{:S(2)}, u32[]{:S(2)}) collective-permute-start(bf16[64,256]{1,0:T(8,128)(2,1)S(1)} %get-tuple-element.24), channel_id=1, source_target_pairs={{0,11},{1,10},{2,9},{3,8},{4,15},{5,14},{6,13},{7,12},{8,3},{9,2},... | collective-permute-start | bytes 98312 | tf_op jit(solution)/shard_map/ppermute | solution.py:87
  154.7 19.1 %collective-permute-start.27 = (bf16[64,256]{1,0:T(8,128)(2,1)S(1)}, bf16[64,256]{1,0:T(8,128)(2,1)S(1)}, u32[]{:S(2)}, u32[]{:S(2)}) collective-permute-start(bf16[64,256]{1,0:T(8,128)(2,1)S(1)} %get-tuple-element.23), channel_id=1, source_target_pairs={{0,12},{1,13},{2,14},{3,15},{4,8},{5,9},{6,10},{7,11},{8,4},{9,5},... | collective-permute-start | bytes 98312 | tf_op jit(solution)/shard_map/ppermute | solution.py:87
  157.5 16.3 %collective-permute-start.28 = (bf16[64,256]{1,0:T(8,128)(2,1)S(1)}, bf16[64,256]{1,0:T(8,128)(2,1)S(1)}, u32[]{:S(2)}, u32[]{:S(2)}) collective-permute-start(bf16[64,256]{1,0:T(8,128)(2,1)S(1)} %get-tuple-element.22), channel_id=1, source_target_pairs={{0,13},{1,12},{2,15},{3,14},{4,9},{5,8},{6,11},{7,10},{8,5},{9,4},... | collective-permute-start | bytes 98312 | tf_op jit(solution)/shard_map/ppermute | solution.py:87
  160.3 13.5 %collective-permute-start.29 = (bf16[64,256]{1,0:T(8,128)(2,1)S(1)}, bf16[64,256]{1,0:T(8,128)(2,1)S(1)}, u32[]{:S(2)}, u32[]{:S(2)}) collective-permute-start(bf16[64,256]{1,0:T(8,128)(2,1)S(1)} %get-tuple-element.21), channel_id=1, source_target_pairs={{0,14},{1,15},{2,12},{3,13},{4,10},{5,11},{6,8},{7,9},{8,6},{9,7},... | collective-permute-start | bytes 98312 | tf_op jit(solution)/shard_map/ppermute | solution.py:87
  166.5 10.0 %collective-permute-start.30 = (bf16[64,256]{1,0:T(8,128)(2,1)S(1)}, bf16[64,256]{1,0:T(8,128)(2,1)S(1)}, u32[]{:S(2)}, u32[]{:S(2)}) collective-permute-start(bf16[64,256]{1,0:T(8,128)(2,1)S(1)} %get-tuple-element.20), channel_id=1, source_target_pairs={{0,15},{1,14},{2,13},{3,12},{4,11},{5,10},{6,9},{7,8},{8,7},{9,6},... | collective-permute-start | bytes 98312 | tf_op jit(solution)/shard_map/ppermute | solution.py:87

commit v6 on v3

--- a/solution.py
+++ b/solution.py
@@ -68,13 +68,20 @@
             total = None
             summed = None
             for place, (s, v) in enumerate(parts):
-                w = jnp.where(masks[place], jnp.exp(s - top), 0.0)
+                w = jnp.exp(s - top)
                 t = jnp.sum(w, axis=1, keepdims=True)
                 o = jnp.dot(w.astype(jnp.bfloat16), v, preferred_element_type=jnp.float32)
                 total = t if total is None else total + t
                 summed = o if summed is None else summed + o
             result = (summed / total).astype(out_ref.dtype)
             out_ref[rows, :, cols] = result.reshape(per_block, chunk, HDIM)
+
+
+def slab_kernel(q_ref, k_ref, v_ref, out_ref):
+    peers, _, _, cols = out_ref.shape
+    for t, ref in enumerate((q_ref, k_ref, v_ref)):
+        for dest in range(peers):
+            out_ref[dest, t] = ref[:, dest * cols : (dest + 1) * cols]
 
 
 def attend(blocks, flags, qkv, before, prior):
@@ -96,7 +103,12 @@
     per_block = BLOCK // chunk
     owned_blocks = peers // per_block
     reach = CYCLE - 1
-    qkv_out = jnp.stack((queries, keys, values)).reshape(3, chunk, peers, cols).transpose(2, 0, 1, 3)
+    qkv_out = pl.pallas_call(
+        slab_kernel,
+        out_shape=jax.ShapeDtypeStruct((peers, 3, chunk, cols), queries.dtype),
+        in_specs=[pl.BlockSpec(memory_space=pltpu.VMEM)] * 3,
+        out_specs=pl.BlockSpec(memory_space=pltpu.VMEM),
+    )(queries, keys, values)
     qkv = lax.all_to_all(qkv_out, "head", split_axis=0, concat_axis=0, tiled=True)
     before = from_behind(qkv[peers - reach * per_block :, 1:], "blk", 1)
     own = lax.axis_index("blk")

time: 93.4 us -> 92 us (0.985)
  local copies, waits for them, and re-layouts: 4.26 us -> 1.78 us
  Pallas kernels: 8.33 us -> 10.8 us
  other arithmetic: 2.28 us -> 0.97 us
    pallas_call x0 -> x1, Pallas kernels: none -> 2.62 us  [body(): pl.pallas_call(slab_kernel, out_shape=jax.ShapeDtypeStruct((peers, 3, chu...]
    unnamed x15 -> x8, local copies, waits for them, and re-layouts: 2.8 us -> 0.8 us
    transpose x1 -> x0, other arithmetic: 1.32 us -> none  [body(): jnp.stack((queries, keys, values)).reshape(3, chunk, peers, cols)]
where the time goes in v6:
time: 92 us; the launch traced here: 91.6 us
  waiting for transfers between devices  47.6 us (52%)
  blocking collectives  18.7 us (20%)
  starting transfers between devices  11.7 us (13%)
  Pallas kernels  10.8 us (12%)
  local copies, waits for them, and re-layouts  1.78 us (2%)
  other arithmetic  0.97 us (1%)
    all_to_all x1, waiting for transfers between devices, body(): lax.all_to_all(qkv_out, 'head', split_axis=0, concat_axis=0, tiled=True)  41.9 us
    all_to_all x1, blocking collectives, body(): lax.all_to_all(joined, 'head', split_axis=0, concat_axis=0, tiled=True)  18.7 us
    all_to_all x1, starting transfers between devices, body(): lax.all_to_all(qkv_out, 'head', split_axis=0, concat_axis=0, tiled=True)  9.8 us
    pallas_call x2, Pallas kernels, attend(): pl.pallas_call(functools.partial(attention_kernel, blocks, before is not...  8.17 us
    ppermute x1, waiting for transfers between devices, from_behind(): lax.ppermute(value, axis, [(source, source + steps) for source in range(i...  5.64 us
    pallas_call x1, Pallas kernels, body(): pl.pallas_call(slab_kernel, out_shape=jax.ShapeDtypeStruct((peers, 3, chu...  2.62 us
    ppermute x1, starting transfers between devices, from_behind(): lax.ppermute(value, axis, [(source, source + steps) for source in range(i...  1.92 us
  transfers between devices with their start and end apart: 2, of which 2 were waited for; matrix products, arithmetic and copies ran while one was open for 1% of the time, Pallas kernels for 4%

profile of v6, /device:TPU:256, one launch (start us, length us, event | category | flops | bytes accessed | tf_op | source)
XLA Modules:
  0.0 91.6 jit_solution(679877746262455112)
XLA Ops:
  0.0 2.6 %shard_map.55 = bf16[16,3,64,256]{3,2,1,0:T(8,128)(2,1)} custom-call(bf16[64,4096]{1,0:T(8,128)(2,1)} %q_ref.1, bf16[64,4096]{1,0:T(8,128)(2,1)} %k_ref.1, bf16[64,4096]{1,0:T(8,128)(2,1)} %v_ref.1), custom_call_target="tpu_custom_call" | custom-call | tf_op jit(solution)/shard_map/pallas_call | solution.py:106
  2.6 0.0 copy-start.3
  2.6 0.0 copy-start.2
  2.6 9.8 %all-to-all-start = ((bf16[16,3,64,256]{3,2,1,0:T(8,128)(2,1)}), bf16[16,3,64,256]{3,2,1,0:T(8,128)(2,1)S(1)}, u32[]{:S(2)}, u32[]{:S(2)}) async-start(bf16[16,3,64,256]{3,2,1,0:T(8,128)(2,1)} %shard_map.55), calls=%async_computation | async-start | bytes 3145728 | tf_op jit(solution)/shard_map/all_to_all | solution.py:112
  12.5 41.9 %all-to-all-done.qkv_ref = bf16[16,3,64,256]{3,2,1,0:T(8,128)(2,1)S(1)} async-done(((bf16[16,3,64,256]{3,2,1,0:T(8,128)(2,1)}), bf16[16,3,64,256]{3,2,1,0:T(8,128)(2,1)S(1)}, u32[]{:S(2)}, u32[]{:S(2)}) %all-to-all-start) | async-done | bytes 1572896 | tf_op jit(solution)/shard_map/all_to_all | solution.py:112
  54.4 0.0 copy-start
  54.4 1.9 %collective-permute-start = (bf16[8,2,64,256]{3,2,1,0:T(8,128)(2,1)S(1)}, bf16[8,2,64,256]{3,2,1,0:T(8,128)(2,1)S(1)}, u32[]{:S(2)}, u32[]{:S(2)}) collective-permute-start(bf16[8,2,64,256]{3,2,1,0:T(8,128)(2,1)S(1)} %slice.4), channel_id=1, source_target_pairs={{0,16},{16,32},{32,48},{48,64},{64,80},{80,96},{96,112},{112,128},... | collective-permute-start | bytes 1572872 | tf_op jit(solution)/shard_map/ppermute | solution.py:19
  56.4 0.0 copy-done.3
  56.4 0.1 iota_compare_fusion
  56.4 0.1 broadcast_subtract_fusion
  56.5 0.0 copy-done.2
  56.5 0.2 and_reduce_fusion
  56.7 0.1 copy.7
  56.8 0.6 convert_element_type.3.flags_ref
  57.4 0.0 copy-done
  57.5 3.9 %shard_map.56.refs_1_ = bf16[16,64,256]{2,1,0:T(8,128)(2,1)} custom-call(s32[4,3]{1,0:T(4,128)} %convert_element_type.3.flags_ref, bf16[16,3,64,256]{3,2,1,0:T(8,128)(2,1)} %copy-done), custom_call_target="tpu_custom_call" | custom-call | tf_op jit(solution)/shard_map/pallas_call | solution.py:91
  61.4 5.6 %collective-permute-done.refs_0_ = bf16[8,2,64,256]{3,2,1,0:T(8,128)(2,1)S(1)} collective-permute-done((bf16[8,2,64,256]{3,2,1,0:T(8,128)(2,1)S(1)}, bf16[8,2,64,256]{3,2,1,0:T(8,128)(2,1)S(1)}, u32[]{:S(2)}, u32[]{:S(2)}) %collective-permute-start) | collective-permute-done | bytes 524320 | tf_op jit(solution)/shard_map/ppermute | solution.py:19
  67.0 0.0 copy-start.1
  67.0 0.8 copy-done.1
  67.8 4.2 %shard_map.57 = bf16[16,64,256]{2,1,0:T(8,128)(2,1)} custom-call(s32[4,3]{1,0:T(4,128)} %convert_element_type.3.flags_ref, bf16[16,3,64,256]{3,2,1,0:T(8,128)(2,1)} %copy-done, bf16[8,2,64,256]{3,2,1,0:T(8,128)(2,1)} %copy-done.1, bf16[16,64,256]{2,1,0:T(8,128)(2,1)} %shard_map.56.refs_1_), custom_call_target="tpu_custom_call" | custom-call | tf_op jit(solution)/shard_map/pallas_call | solution.py:91
  72.1 18.7 %all_to_all.10 = bf16[16,64,256]{2,1,0:T(8,128)(2,1)S(1)} all-to-all(bf16[16,64,256]{2,1,0:T(8,128)(2,1)} %shard_map.57), channel_id=1, replica_groups=mesh['blk'=64,'head'=16] {'head'}, dimensions={0} | all-to-all | bytes 1048576 | tf_op jit(solution)/shard_map/all_to_all | solution.py:124
  90.8 0.8 copy.9
  (3 shorter events, 0.0 us)
Async XLA Ops:
  2.6 53.7 %copy-start.3 = (s32[4]{0:T(128)S(1)}, s32[4]{0:T(128)}, u32[]{:S(2)}) copy-start(s32[4]{0:T(128)} %param.9) | copy-start | bytes 52
  2.6 53.9 %copy-start.2 = (s32[4,3]{1,0:T(4,128)S(1)}, s32[4,3]{1,0:T(4,128)}, u32[]{:S(2)}) copy-start(s32[4,3]{1,0:T(4,128)} %param.8) | copy-start | bytes 148
  2.6 51.8 %all-to-all-start = ((bf16[16,3,64,256]{3,2,1,0:T(8,128)(2,1)}), bf16[16,3,64,256]{3,2,1,0:T(8,128)(2,1)S(1)}, u32[]{:S(2)}, u32[]{:S(2)}) async-start(bf16[16,3,64,256]{3,2,1,0:T(8,128)(2,1)} %shard_map.55), calls=%async_computation | async-start | bytes 3145728 | tf_op jit(solution)/shard_map/all_to_all | solution.py:112
  54.4 3.1 %copy-start = (bf16[16,3,64,256]{3,2,1,0:T(8,128)(2,1)}, bf16[16,3,64,256]{3,2,1,0:T(8,128)(2,1)S(1)}, u32[]{:S(2)}) copy-start(bf16[16,3,64,256]{3,2,1,0:T(8,128)(2,1)S(1)} %all-to-all-done.qkv_ref) | copy-start | bytes 4718596
  54.4 12.6 %collective-permute-start = (bf16[8,2,64,256]{3,2,1,0:T(8,128)(2,1)S(1)}, bf16[8,2,64,256]{3,2,1,0:T(8,128)(2,1)S(1)}, u32[]{:S(2)}, u32[]{:S(2)}) collective-permute-start(bf16[8,2,64,256]{3,2,1,0:T(8,128)(2,1)S(1)} %slice.4), channel_id=1, source_target_pairs={{0,16},{16,32},{32,48},{48,64},{64,80},{80,96},{96,112},{112,128},... | collective-permute-start | bytes 1572872 | tf_op jit(solution)/shard_map/ppermute | solution.py:19
  67.0 0.8 copy-start.1

commit v7 on v6

--- a/solution.py
+++ b/solution.py
@@ -19,23 +19,18 @@
     return lax.ppermute(value, axis, [(source, source + steps) for source in range(initial, last)])
 
 
-def attention_kernel(blocks, has_before, has_prior, flags_ref, qkv_ref, *refs):
+def attention_kernel(blocks, has_before, flags_ref, qkv_ref, *refs):
     before_ref = refs[0] if has_before else None
     out_ref = refs[-1]
-    peers, _, chunk, width = qkv_ref.shape
+    _, _, chunk, width = qkv_ref.shape
     per_block = BLOCK // chunk
+    out_first = blocks[0] * per_block
     local_heads = width // HDIM
     reach = CYCLE - 1
     scale = 1.0 / HDIM**0.5
     row_pos = lax.broadcasted_iota(jnp.int32, (BLOCK, BLOCK), 0)
     col_pos = lax.broadcasted_iota(jnp.int32, (BLOCK, BLOCK), 1)
     causal = col_pos <= row_pos
-    if has_prior:
-        prior_ref = refs[-2]
-        for local in range(peers // per_block):
-            if local not in blocks:
-                rows = slice(local * per_block, (local + 1) * per_block)
-                out_ref[rows] = prior_ref[rows]
     for local in blocks:
         wanted = [flags_ref[local, place] != 0 for place in range(CYCLE)]
         masks = []
@@ -74,7 +69,8 @@
                 total = t if total is None else total + t
                 summed = o if summed is None else summed + o
             result = (summed / total).astype(out_ref.dtype)
-            out_ref[rows, :, cols] = result.reshape(per_block, chunk, HDIM)
+            out_rows = slice(local * per_block - out_first, (local + 1) * per_block - out_first)
+            out_ref[out_rows, :, cols] = result.reshape(per_block, chunk, HDIM)
 
 
 def slab_kernel(q_ref, k_ref, v_ref, out_ref):
@@ -85,15 +81,31 @@
 
 
 def attend(blocks, flags, qkv, before, prior):
-    vmem = pl.BlockSpec(memory_space=pltpu.VMEM)
-    extra = tuple(x for x in (before, prior) if x is not None)
     peers, _, chunk, width = qkv.shape
+    per_block = BLOCK // chunk
+    rows = len(blocks) * per_block
+    reads = (blocks[-1] + 1) * per_block if blocks[0] == 0 else peers
+    operands = [flags, qkv]
+    in_specs = [
+        pl.BlockSpec(memory_space=pltpu.SMEM),
+        pl.BlockSpec((reads,) + qkv.shape[1:], lambda i: (0, 0, 0, 0)),
+    ]
+    if before is not None:
+        operands.append(before)
+        in_specs.append(pl.BlockSpec(before.shape, lambda i: (0, 0, 0, 0)))
+    aliases = {}
+    if prior is not None:
+        aliases = {len(operands): 0}
+        operands.append(prior)
+        in_specs.append(pl.BlockSpec(memory_space=pl.ANY))
     return pl.pallas_call(
-        functools.partial(attention_kernel, blocks, before is not None, prior is not None),
+        functools.partial(attention_kernel, blocks, before is not None),
         out_shape=jax.ShapeDtypeStruct((peers, chunk, width), qkv.dtype),
-        in_specs=[pl.BlockSpec(memory_space=pltpu.SMEM)] + [vmem] * (1 + len(extra)),
-        out_specs=vmem,
-    )(flags, qkv, *extra)
+        grid=(1,),
+        in_specs=in_specs,
+        out_specs=pl.BlockSpec((rows, chunk, width), lambda i: (blocks[0] * per_block // rows, 0, 0)),
+        input_output_aliases=aliases,
+    )(*operands)
 
 
 def body(queries, keys, values, block_lists, block_counts):

time: 92 us -> 91.5 us (level)
  no operation moved by 1% of the time
where the time goes in v7:
time: 91.5 us; the launch traced here: 91.1 us
  waiting for transfers between devices  47.7 us (52%)
  blocking collectives  18.7 us (20%)
  starting transfers between devices  11.7 us (13%)
  Pallas kernels  10.2 us (11%)
  local copies, waits for them, and re-layouts  1.78 us (2%)
  other arithmetic  0.95 us (1%)
    all_to_all x1, waiting for transfers between devices, body(): lax.all_to_all(qkv_out, 'head', split_axis=0, concat_axis=0, tiled=True)  41.9 us
    all_to_all x1, blocking collectives, body(): lax.all_to_all(joined, 'head', split_axis=0, concat_axis=0, tiled=True)  18.7 us
    all_to_all x1, starting transfers between devices, body(): lax.all_to_all(qkv_out, 'head', split_axis=0, concat_axis=0, tiled=True)  9.8 us
    pallas_call x2, Pallas kernels, attend(): pl.pallas_call(functools.partial(attention_kernel, blocks, before is not...  7.6 us
    ppermute x1, waiting for transfers between devices, from_behind(): lax.ppermute(value, axis, [(source, source + steps) for source in range(i...  5.74 us
    pallas_call x1, Pallas kernels, body(): pl.pallas_call(slab_kernel, out_shape=jax.ShapeDtypeStruct((peers, 3, chu...  2.62 us
    ppermute x1, starting transfers between devices, from_behind(): lax.ppermute(value, axis, [(source, source + steps) for source in range(i...  1.92 us
  transfers between devices with their start and end apart: 2, of which 2 were waited for; matrix products, arithmetic and copies ran while one was open for 1% of the time, Pallas kernels for 4%

profile of v7, /device:TPU:256, one launch (start us, length us, event | category | flops | bytes accessed | tf_op | source)
XLA Modules:
  0.0 91.1 jit_solution(4635438505772398191)
XLA Ops:
  0.0 2.6 %shard_map.55 = bf16[16,3,64,256]{3,2,1,0:T(8,128)(2,1)} custom-call(bf16[64,4096]{1,0:T(8,128)(2,1)} %q_ref.1, bf16[64,4096]{1,0:T(8,128)(2,1)} %k_ref.1, bf16[64,4096]{1,0:T(8,128)(2,1)} %v_ref.1), custom_call_target="tpu_custom_call" | custom-call | tf_op jit(solution)/shard_map/pallas_call | solution.py:118
  2.6 0.0 copy-start.3
  2.6 0.0 copy-start.2
  2.6 9.8 %all-to-all-start = ((bf16[16,3,64,256]{3,2,1,0:T(8,128)(2,1)}), bf16[16,3,64,256]{3,2,1,0:T(8,128)(2,1)S(1)}, u32[]{:S(2)}, u32[]{:S(2)}) async-start(bf16[16,3,64,256]{3,2,1,0:T(8,128)(2,1)} %shard_map.55), calls=%async_computation | async-start | bytes 3145728 | tf_op jit(solution)/shard_map/all_to_all | solution.py:124
  12.5 41.9 %all-to-all-done.qkv_ref = bf16[16,3,64,256]{3,2,1,0:T(8,128)(2,1)S(1)} async-done(((bf16[16,3,64,256]{3,2,1,0:T(8,128)(2,1)}), bf16[16,3,64,256]{3,2,1,0:T(8,128)(2,1)S(1)}, u32[]{:S(2)}, u32[]{:S(2)}) %all-to-all-start) | async-done | bytes 1572896 | tf_op jit(solution)/shard_map/all_to_all | solution.py:124
  54.4 0.0 copy-start
  54.4 1.9 %collective-permute-start = (bf16[8,2,64,256]{3,2,1,0:T(8,128)(2,1)S(1)}, bf16[8,2,64,256]{3,2,1,0:T(8,128)(2,1)S(1)}, u32[]{:S(2)}, u32[]{:S(2)}) collective-permute-start(bf16[8,2,64,256]{3,2,1,0:T(8,128)(2,1)S(1)} %slice.4), channel_id=1, source_target_pairs={{0,16},{16,32},{32,48},{48,64},{64,80},{80,96},{96,112},{112,128},... | collective-permute-start | bytes 1572872 | tf_op jit(solution)/shard_map/ppermute | solution.py:19
  56.4 0.0 copy-done.3
  56.4 0.1 iota_compare_fusion
  56.4 0.1 broadcast_subtract_fusion
  56.5 0.0 copy-done.2
  56.5 0.2 and_reduce_fusion
  56.7 0.1 copy.8
  56.8 0.6 convert_element_type.3.flags_ref
  57.4 0.0 copy-done
  57.4 3.9 %shard_map.56.refs_1_ = bf16[16,64,256]{2,1,0:T(8,128)(2,1)} custom-call(s32[4,3]{1,0:T(4,128)} %convert_element_type.3.flags_ref, bf16[16,3,64,256]{3,2,1,0:T(8,128)(2,1)} %copy-done), custom_call_target="tpu_custom_call" | custom-call | tf_op jit(solution)/shard_map/pallas_call | solution.py:101
  61.3 5.7 %collective-permute-done.refs_0_ = bf16[8,2,64,256]{3,2,1,0:T(8,128)(2,1)S(1)} collective-permute-done((bf16[8,2,64,256]{3,2,1,0:T(8,128)(2,1)S(1)}, bf16[8,2,64,256]{3,2,1,0:T(8,128)(2,1)S(1)}, u32[]{:S(2)}, u32[]{:S(2)}) %collective-permute-start) | collective-permute-done | bytes 524320 | tf_op jit(solution)/shard_map/ppermute | solution.py:19
  67.0 0.0 copy-start.1
  67.0 0.8 copy-done.1
  67.8 3.7 %shard_map.57 = bf16[16,64,256]{2,1,0:T(8,128)(2,1)} custom-call(s32[4,3]{1,0:T(4,128)} %convert_element_type.3.flags_ref, bf16[16,3,64,256]{3,2,1,0:T(8,128)(2,1)} %copy-done, bf16[8,2,64,256]{3,2,1,0:T(8,128)(2,1)} %copy-done.1, bf16[16,64,256]{2,1,0:T(8,128)(2,1)} %shard_map.56.refs_1_), custom_call_target="tpu_custom_call", output_to_operand_aliasing={{}: (3, {})} | custom-call | tf_op jit(solution)/shard_map/pallas_call | solution.py:101
  71.6 18.7 %all_to_all.10 = bf16[16,64,256]{2,1,0:T(8,128)(2,1)S(1)} all-to-all(bf16[16,64,256]{2,1,0:T(8,128)(2,1)} %shard_map.57), channel_id=1, replica_groups=mesh['blk'=64,'head'=16] {'head'}, dimensions={0} | all-to-all | bytes 1048576 | tf_op jit(solution)/shard_map/all_to_all | solution.py:136
  90.3 0.8 copy.10
  (3 shorter events, 0.0 us)
Async XLA Ops:
  2.6 53.7 %copy-start.3 = (s32[4]{0:T(128)S(1)}, s32[4]{0:T(128)}, u32[]{:S(2)}) copy-start(s32[4]{0:T(128)} %param.9) | copy-start | bytes 52
  2.6 53.9 %copy-start.2 = (s32[4,3]{1,0:T(4,128)S(1)}, s32[4,3]{1,0:T(4,128)}, u32[]{:S(2)}) copy-start(s32[4,3]{1,0:T(4,128)} %param.8) | copy-start | bytes 148
  2.6 51.8 %all-to-all-start = ((bf16[16,3,64,256]{3,2,1,0:T(8,128)(2,1)}), bf16[16,3,64,256]{3,2,1,0:T(8,128)(2,1)S(1)}, u32[]{:S(2)}, u32[]{:S(2)}) async-start(bf16[16,3,64,256]{3,2,1,0:T(8,128)(2,1)} %shard_map.55), calls=%async_computation | async-start | bytes 3145728 | tf_op jit(solution)/shard_map/all_to_all | solution.py:124
  54.4 3.0 %copy-start = (bf16[16,3,64,256]{3,2,1,0:T(8,128)(2,1)}, bf16[16,3,64,256]{3,2,1,0:T(8,128)(2,1)S(1)}, u32[]{:S(2)}) copy-start(bf16[16,3,64,256]{3,2,1,0:T(8,128)(2,1)S(1)} %all-to-all-done.qkv_ref) | copy-start | bytes 4718596
  54.4 12.6 %collective-permute-start = (bf16[8,2,64,256]{3,2,1,0:T(8,128)(2,1)S(1)}, bf16[8,2,64,256]{3,2,1,0:T(8,128)(2,1)S(1)}, u32[]{:S(2)}, u32[]{:S(2)}) collective-permute-start(bf16[8,2,64,256]{3,2,1,0:T(8,128)(2,1)S(1)} %slice.4), channel_id=1, source_target_pairs={{0,16},{16,32},{32,48},{48,64},{64,80},{80,96},{96,112},{112,128},... | collective-permute-start | bytes 1572872 | tf_op jit(solution)/shard_map/ppermute | solution.py:19
  67.0 0.8 copy-start.1

commit v8 on v7

--- a/solution.py
+++ b/solution.py
@@ -28,46 +28,38 @@
     local_heads = width // HDIM
     reach = CYCLE - 1
     scale = 1.0 / HDIM**0.5
-    row_pos = lax.broadcasted_iota(jnp.int32, (BLOCK, BLOCK), 0)
-    col_pos = lax.broadcasted_iota(jnp.int32, (BLOCK, BLOCK), 1)
-    causal = col_pos <= row_pos
+    row_pos = lax.broadcasted_iota(jnp.int32, (BLOCK, CYCLE * BLOCK), 0)
+    col_pos = lax.broadcasted_iota(jnp.int32, (BLOCK, CYCLE * BLOCK), 1)
+    causal = (col_pos < reach * BLOCK) | (col_pos - reach * BLOCK <= row_pos)
     for local in blocks:
-        wanted = [flags_ref[local, place] != 0 for place in range(CYCLE)]
-        masks = []
+        allowed = causal
         for place in range(CYCLE):
-            if place == reach:
-                masks.append(causal & wanted[place])
-            else:
-                masks.append(jnp.broadcast_to(wanted[place], (BLOCK, BLOCK)))
+            inside = (col_pos >= place * BLOCK) & (col_pos < (place + 1) * BLOCK)
+            allowed = allowed & (jnp.logical_not(inside) | (flags_ref[local, place] != 0))
         rows = slice(local * per_block, (local + 1) * per_block)
+        first = local - reach
         for head in range(local_heads):
             cols = slice(head * HDIM, (head + 1) * HDIM)
             q = qkv_ref[rows, 0, :, cols].reshape(BLOCK, HDIM)
-            parts = []
-            for place in range(CYCLE):
-                source = local - (reach - place)
-                if source >= 0:
-                    src = slice(source * per_block, (source + 1) * per_block)
-                    k = qkv_ref[src, 1, :, cols].reshape(BLOCK, HDIM)
-                    v = qkv_ref[src, 2, :, cols].reshape(BLOCK, HDIM)
-                else:
-                    src = slice((source + reach) * per_block, (source + reach + 1) * per_block)
-                    k = before_ref[src, 0, :, cols].reshape(BLOCK, HDIM)
-                    v = before_ref[src, 1, :, cols].reshape(BLOCK, HDIM)
-                s = lax.dot_general(q, k, (((1,), (1,)), ((), ())), preferred_element_type=jnp.float32) * scale
-                s = jnp.where(masks[place], s, -1e30)
-                parts.append((s, v))
-            top = jnp.max(parts[0][0], axis=1, keepdims=True)
-            for s, _ in parts[1:]:
-                top = jnp.maximum(top, jnp.max(s, axis=1, keepdims=True))
-            total = None
-            summed = None
-            for place, (s, v) in enumerate(parts):
-                w = jnp.exp(s - top)
-                t = jnp.sum(w, axis=1, keepdims=True)
-                o = jnp.dot(w.astype(jnp.bfloat16), v, preferred_element_type=jnp.float32)
-                total = t if total is None else total + t
-                summed = o if summed is None else summed + o
+            if first >= 0:
+                span = slice(first * per_block, (local + 1) * per_block)
+                k = qkv_ref[span, 1, :, cols].reshape(CYCLE * BLOCK, HDIM)
+                v = qkv_ref[span, 2, :, cols].reshape(CYCLE * BLOCK, HDIM)
+            else:
+                halo = slice((first + reach) * per_block, reach * per_block)
+                own = slice(0, (local + 1) * per_block)
+                k = jnp.concatenate(
+                    (before_ref[halo, 0, :, cols].reshape(-1, HDIM), qkv_ref[own, 1, :, cols].reshape(-1, HDIM)), axis=0
+                )
+                v = jnp.concatenate(
+                    (before_ref[halo, 1, :, cols].reshape(-1, HDIM), qkv_ref[own, 2, :, cols].reshape(-1, HDIM)), axis=0
+                )
+            s = lax.dot_general(q, k, (((1,), (1,)), ((), ())), preferred_element_type=jnp.float32) * scale
+            s = jnp.where(allowed, s, -1e30)
+            top = jnp.max(s, axis=1, keepdims=True)
+            w = jnp.exp(s - top)
+            total = jnp.sum(w, axis=1, keepdims=True)
+            summed = jnp.dot(w.astype(jnp.bfloat16), v, preferred_element_type=jnp.float32)
             result = (summed / total).astype(out_ref.dtype)
             out_rows = slice(local * per_block - out_first, (local + 1) * per_block - out_first)
             out_ref[out_rows, :, cols] = result.reshape(per_block, chunk, HDIM)

time: 91.5 us -> 91.6 us (level)
  no operation moved by 1% of the time
where the time goes in v8:
time: 91.6 us; the launch traced here: 91.2 us
  waiting for transfers between devices  47.6 us (52%)
  blocking collectives  18.7 us (20%)
  starting transfers between devices  11.7 us (13%)
  Pallas kernels  10.3 us (11%)
  local copies, waits for them, and re-layouts  1.78 us (2%)
  other arithmetic  0.95 us (1%)
    all_to_all x1, waiting for transfers between devices, body(): lax.all_to_all(qkv_out, 'head', split_axis=0, concat_axis=0, tiled=True)  41.9 us
    all_to_all x1, blocking collectives, body(): lax.all_to_all(joined, 'head', split_axis=0, concat_axis=0, tiled=True)  18.7 us
    all_to_all x1, starting transfers between devices, body(): lax.all_to_all(qkv_out, 'head', split_axis=0, concat_axis=0, tiled=True)  9.8 us
    pallas_call x2, Pallas kernels, attend(): pl.pallas_call(functools.partial(attention_kernel, blocks, before is not...  7.73 us
    ppermute x1, waiting for transfers between devices, from_behind(): lax.ppermute(value, axis, [(source, source + steps) for source in range(i...  5.68 us
    pallas_call x1, Pallas kernels, body(): pl.pallas_call(slab_kernel, out_shape=jax.ShapeDtypeStruct((peers, 3, chu...  2.62 us
    ppermute x1, starting transfers between devices, from_behind(): lax.ppermute(value, axis, [(source, source + steps) for source in range(i...  1.92 us
  transfers between devices with their start and end apart: 2, of which 2 were waited for; matrix products, arithmetic and copies ran while one was open for 1% of the time, Pallas kernels for 4%

profile of v8, /device:TPU:256, one launch (start us, length us, event | category | flops | bytes accessed | tf_op | source)
XLA Modules:
  0.0 91.2 jit_solution(15403909989677715670)
XLA Ops:
  0.0 2.6 %shard_map.55 = bf16[16,3,64,256]{3,2,1,0:T(8,128)(2,1)} custom-call(bf16[64,4096]{1,0:T(8,128)(2,1)} %q_ref.1, bf16[64,4096]{1,0:T(8,128)(2,1)} %k_ref.1, bf16[64,4096]{1,0:T(8,128)(2,1)} %v_ref.1), custom_call_target="tpu_custom_call" | custom-call | tf_op jit(solution)/shard_map/pallas_call | solution.py:110
  2.6 0.0 copy-start.3
  2.6 0.0 copy-start.2
  2.6 9.8 %all-to-all-start = ((bf16[16,3,64,256]{3,2,1,0:T(8,128)(2,1)}), bf16[16,3,64,256]{3,2,1,0:T(8,128)(2,1)S(1)}, u32[]{:S(2)}, u32[]{:S(2)}) async-start(bf16[16,3,64,256]{3,2,1,0:T(8,128)(2,1)} %shard_map.55), calls=%async_computation | async-start | bytes 3145728 | tf_op jit(solution)/shard_map/all_to_all | solution.py:116
  12.5 41.9 %all-to-all-done.qkv_ref = bf16[16,3,64,256]{3,2,1,0:T(8,128)(2,1)S(1)} async-done(((bf16[16,3,64,256]{3,2,1,0:T(8,128)(2,1)}), bf16[16,3,64,256]{3,2,1,0:T(8,128)(2,1)S(1)}, u32[]{:S(2)}, u32[]{:S(2)}) %all-to-all-start) | async-done | bytes 1572896 | tf_op jit(solution)/shard_map/all_to_all | solution.py:116
  54.4 0.0 copy-start
  54.4 1.9 %collective-permute-start = (bf16[8,2,64,256]{3,2,1,0:T(8,128)(2,1)S(1)}, bf16[8,2,64,256]{3,2,1,0:T(8,128)(2,1)S(1)}, u32[]{:S(2)}, u32[]{:S(2)}) collective-permute-start(bf16[8,2,64,256]{3,2,1,0:T(8,128)(2,1)S(1)} %slice.4), channel_id=1, source_target_pairs={{0,16},{16,32},{32,48},{48,64},{64,80},{80,96},{96,112},{112,128},... | collective-permute-start | bytes 1572872 | tf_op jit(solution)/shard_map/ppermute | solution.py:19
  56.4 0.0 copy-done.3
  56.4 0.1 iota_compare_fusion
  56.4 0.1 broadcast_subtract_fusion
  56.5 0.0 copy-done.2
  56.5 0.2 and_reduce_fusion
  56.7 0.1 copy.8
  56.8 0.6 convert_element_type.3.flags_ref
  57.4 0.0 copy-done
  57.4 3.9 %shard_map.56.refs_1_ = bf16[16,64,256]{2,1,0:T(8,128)(2,1)} custom-call(s32[4,3]{1,0:T(4,128)} %convert_element_type.3.flags_ref, bf16[16,3,64,256]{3,2,1,0:T(8,128)(2,1)} %copy-done), custom_call_target="tpu_custom_call" | custom-call | tf_op jit(solution)/shard_map/pallas_call | solution.py:93
  61.4 5.7 %collective-permute-done.refs_0_ = bf16[8,2,64,256]{3,2,1,0:T(8,128)(2,1)S(1)} collective-permute-done((bf16[8,2,64,256]{3,2,1,0:T(8,128)(2,1)S(1)}, bf16[8,2,64,256]{3,2,1,0:T(8,128)(2,1)S(1)}, u32[]{:S(2)}, u32[]{:S(2)}) %collective-permute-start) | collective-permute-done | bytes 524320 | tf_op jit(solution)/shard_map/ppermute | solution.py:19
  67.0 0.0 copy-start.1
  67.0 0.8 copy-done.1
  67.8 3.8 %shard_map.57 = bf16[16,64,256]{2,1,0:T(8,128)(2,1)} custom-call(s32[4,3]{1,0:T(4,128)} %convert_element_type.3.flags_ref, bf16[16,3,64,256]{3,2,1,0:T(8,128)(2,1)} %copy-done, bf16[8,2,64,256]{3,2,1,0:T(8,128)(2,1)} %copy-done.1, bf16[16,64,256]{2,1,0:T(8,128)(2,1)} %shard_map.56.refs_1_), custom_call_target="tpu_custom_call", output_to_operand_aliasing={{}: (3, {})} | custom-call | tf_op jit(solution)/shard_map/pallas_call | solution.py:93
  71.6 18.7 %all_to_all.10 = bf16[16,64,256]{2,1,0:T(8,128)(2,1)S(1)} all-to-all(bf16[16,64,256]{2,1,0:T(8,128)(2,1)} %shard_map.57), channel_id=1, replica_groups=mesh['blk'=64,'head'=16] {'head'}, dimensions={0} | all-to-all | bytes 1048576 | tf_op jit(solution)/shard_map/all_to_all | solution.py:128
  90.4 0.8 copy.10
  (3 shorter events, 0.0 us)
Async XLA Ops:
  2.6 53.7 %copy-start.3 = (s32[4]{0:T(128)S(1)}, s32[4]{0:T(128)}, u32[]{:S(2)}) copy-start(s32[4]{0:T(128)} %param.9) | copy-start | bytes 52
  2.6 53.9 %copy-start.2 = (s32[4,3]{1,0:T(4,128)S(1)}, s32[4,3]{1,0:T(4,128)}, u32[]{:S(2)}) copy-start(s32[4,3]{1,0:T(4,128)} %param.8) | copy-start | bytes 148
  2.6 51.8 %all-to-all-start = ((bf16[16,3,64,256]{3,2,1,0:T(8,128)(2,1)}), bf16[16,3,64,256]{3,2,1,0:T(8,128)(2,1)S(1)}, u32[]{:S(2)}, u32[]{:S(2)}) async-start(bf16[16,3,64,256]{3,2,1,0:T(8,128)(2,1)} %shard_map.55), calls=%async_computation | async-start | bytes 3145728 | tf_op jit(solution)/shard_map/all_to_all | solution.py:116
  54.4 3.0 %copy-start = (bf16[16,3,64,256]{3,2,1,0:T(8,128)(2,1)}, bf16[16,3,64,256]{3,2,1,0:T(8,128)(2,1)S(1)}, u32[]{:S(2)}) copy-start(bf16[16,3,64,256]{3,2,1,0:T(8,128)(2,1)S(1)} %all-to-all-done.qkv_ref) | copy-start | bytes 4718596
  54.4 12.6 %collective-permute-start = (bf16[8,2,64,256]{3,2,1,0:T(8,128)(2,1)S(1)}, bf16[8,2,64,256]{3,2,1,0:T(8,128)(2,1)S(1)}, u32[]{:S(2)}, u32[]{:S(2)}) collective-permute-start(bf16[8,2,64,256]{3,2,1,0:T(8,128)(2,1)S(1)} %slice.4), channel_id=1, source_target_pairs={{0,16},{16,32},{32,48},{48,64},{64,80},{80,96},{96,112},{112,128},... | collective-permute-start | bytes 1572872 | tf_op jit(solution)/shard_map/ppermute | solution.py:19
  67.0 0.8 copy-start.1

commit v9 on v8

--- a/solution.py
+++ b/solution.py
@@ -66,10 +66,24 @@
 
 
 def slab_kernel(q_ref, k_ref, v_ref, out_ref):
-    peers, _, _, cols = out_ref.shape
+    group, _, _, cols = out_ref.shape
     for t, ref in enumerate((q_ref, k_ref, v_ref)):
-        for dest in range(peers):
+        for dest in range(group):
             out_ref[dest, t] = ref[:, dest * cols : (dest + 1) * cols]
+
+
+def slabs(queries, keys, values, peers):
+    chunk, width = queries.shape
+    cols = width // peers
+    group = 4 if peers % 4 == 0 else 1
+    tensor = pl.BlockSpec((chunk, group * cols), lambda g: (0, g))
+    return pl.pallas_call(
+        slab_kernel,
+        out_shape=jax.ShapeDtypeStruct((peers, 3, chunk, cols), queries.dtype),
+        grid=(peers // group,),
+        in_specs=[tensor] * 3,
+        out_specs=pl.BlockSpec((group, 3, chunk, cols), lambda g: (g, 0, 0, 0)),
+    )(queries, keys, values)
 
 
 def attend(blocks, flags, qkv, before, prior):
@@ -80,11 +94,11 @@
     operands = [flags, qkv]
     in_specs = [
         pl.BlockSpec(memory_space=pltpu.SMEM),
-        pl.BlockSpec((reads,) + qkv.shape[1:], lambda i: (0, 0, 0, 0)),
+        pl.BlockSpec((reads,) + qkv.shape[1:3] + (HDIM,), lambda h: (0, 0, 0, h)),
     ]
     if before is not None:
         operands.append(before)
-        in_specs.append(pl.BlockSpec(before.shape, lambda i: (0, 0, 0, 0)))
+        in_specs.append(pl.BlockSpec(before.shape[:3] + (HDIM,), lambda h: (0, 0, 0, h)))
     aliases = {}
     if prior is not None:
         aliases = {len(operands): 0}
@@ -93,9 +107,9 @@
     return pl.pallas_call(
         functools.partial(attention_kernel, blocks, before is not None),
         out_shape=jax.ShapeDtypeStruct((peers, chunk, width), qkv.dtype),
-        grid=(1,),
+        grid=(width // HDIM,),
         in_specs=in_specs,
-        out_specs=pl.BlockSpec((rows, chunk, width), lambda i: (blocks[0] * per_block // rows, 0, 0)),
+        out_specs=pl.BlockSpec((rows, chunk, HDIM), lambda h: (blocks[0] * per_block // rows, 0, h)),
         input_output_aliases=aliases,
     )(*operands)
 
@@ -107,12 +121,7 @@
     per_block = BLOCK // chunk
     owned_blocks = peers // per_block
     reach = CYCLE - 1
-    qkv_out = pl.pallas_call(
-        slab_kernel,
-        out_shape=jax.ShapeDtypeStruct((peers, 3, chunk, cols), queries.dtype),
-        in_specs=[pl.BlockSpec(memory_space=pltpu.VMEM)] * 3,
-        out_specs=pl.BlockSpec(memory_space=pltpu.VMEM),
-    )(queries, keys, values)
+    qkv_out = slabs(queries, keys, values, peers)
     qkv = lax.all_to_all(qkv_out, "head", split_axis=0, concat_axis=0, tiled=True)
     before = from_behind(qkv[peers - reach * per_block :, 1:], "blk", 1)
     own = lax.axis_index("blk")

time: 91.6 us -> 92.7 us (1.012)
  Pallas kernels: 10.3 us -> 11.4 us
    pallas_call x1, Pallas kernels: 2.62 us -> 3.63 us  [slabs(): pl.pallas_call(slab_kernel, out_shape=jax.ShapeDtypeStruct((peers, 3, chu...]
where the time goes in v9:
time: 92.7 us; the launch traced here: 92.2 us
  waiting for transfers between devices  47.6 us (51%)
  blocking collectives  18.7 us (20%)
  starting transfers between devices  11.7 us (13%)
  Pallas kernels  11.4 us (12%)
  local copies, waits for them, and re-layouts  1.78 us (2%)
  other arithmetic  0.95 us (1%)
    all_to_all x1, waiting for transfers between devices, body(): lax.all_to_all(qkv_out, 'head', split_axis=0, concat_axis=0, tiled=True)  41.9 us
    all_to_all x1, blocking collectives, body(): lax.all_to_all(joined, 'head', split_axis=0, concat_axis=0, tiled=True)  18.7 us
    all_to_all x1, starting transfers between devices, body(): lax.all_to_all(qkv_out, 'head', split_axis=0, concat_axis=0, tiled=True)  9.8 us
    pallas_call x2, Pallas kernels, attend(): pl.pallas_call(functools.partial(attention_kernel, blocks, before is not...  7.75 us
    ppermute x1, waiting for transfers between devices, from_behind(): lax.ppermute(value, axis, [(source, source + steps) for source in range(i...  5.71 us
    pallas_call x1, Pallas kernels, slabs(): pl.pallas_call(slab_kernel, out_shape=jax.ShapeDtypeStruct((peers, 3, chu...  3.63 us
    ppermute x1, starting transfers between devices, from_behind(): lax.ppermute(value, axis, [(source, source + steps) for source in range(i...  1.92 us
  transfers between devices with their start and end apart: 2, of which 2 were waited for; matrix products, arithmetic and copies ran while one was open for 1% of the time, Pallas kernels for 4%

profile of v9, /device:TPU:256, one launch (start us, length us, event | category | flops | bytes accessed | tf_op | source)
XLA Modules:
  0.0 92.2 jit_solution(4754272217226917871)
XLA Ops:
  0.0 3.6 %shard_map.55 = bf16[16,3,64,256]{3,2,1,0:T(8,128)(2,1)} custom-call(bf16[64,4096]{1,0:T(8,128)(2,1)} %q_ref.1, bf16[64,4096]{1,0:T(8,128)(2,1)} %k_ref.1, bf16[64,4096]{1,0:T(8,128)(2,1)} %v_ref.1), custom_call_target="tpu_custom_call" | custom-call | tf_op jit(solution)/shard_map/pallas_call | solution.py:80
  3.6 0.0 copy-start.3
  3.6 0.0 copy-start.2
  3.6 9.8 %all-to-all-start = ((bf16[16,3,64,256]{3,2,1,0:T(8,128)(2,1)}), bf16[16,3,64,256]{3,2,1,0:T(8,128)(2,1)S(1)}, u32[]{:S(2)}, u32[]{:S(2)}) async-start(bf16[16,3,64,256]{3,2,1,0:T(8,128)(2,1)} %shard_map.55), calls=%async_computation | async-start | bytes 3145728 | tf_op jit(solution)/shard_map/all_to_all | solution.py:125
  13.5 41.9 %all-to-all-done.qkv_ref = bf16[16,3,64,256]{3,2,1,0:T(8,128)(2,1)S(1)} async-done(((bf16[16,3,64,256]{3,2,1,0:T(8,128)(2,1)}), bf16[16,3,64,256]{3,2,1,0:T(8,128)(2,1)S(1)}, u32[]{:S(2)}, u32[]{:S(2)}) %all-to-all-start) | async-done | bytes 1572896 | tf_op jit(solution)/shard_map/all_to_all | solution.py:125
  55.4 0.0 copy-start
  55.4 1.9 %collective-permute-start = (bf16[8,2,64,256]{3,2,1,0:T(8,128)(2,1)S(1)}, bf16[8,2,64,256]{3,2,1,0:T(8,128)(2,1)S(1)}, u32[]{:S(2)}, u32[]{:S(2)}) collective-permute-start(bf16[8,2,64,256]{3,2,1,0:T(8,128)(2,1)S(1)} %slice.4), channel_id=1, source_target_pairs={{0,16},{16,32},{32,48},{48,64},{64,80},{80,96},{96,112},{112,128},... | collective-permute-start | bytes 1572872 | tf_op jit(solution)/shard_map/ppermute | solution.py:19
  57.4 0.0 copy-done.3
  57.4 0.1 iota_compare_fusion
  57.5 0.1 broadcast_subtract_fusion
  57.5 0.0 copy-done.2
  57.5 0.2 and_reduce_fusion
  57.7 0.1 copy.8
  57.9 0.6 convert_element_type.3.flags_ref
  58.4 0.0 copy-done
  58.4 3.9 %shard_map.56.refs_1_ = bf16[16,64,256]{2,1,0:T(8,128)(2,1)} custom-call(s32[4,3]{1,0:T(4,128)} %convert_element_type.3.flags_ref, bf16[16,3,64,256]{3,2,1,0:T(8,128)(2,1)} %copy-done), custom_call_target="tpu_custom_call" | custom-call | tf_op jit(solution)/shard_map/pallas_call | solution.py:107
  62.3 5.7 %collective-permute-done.refs_0_ = bf16[8,2,64,256]{3,2,1,0:T(8,128)(2,1)S(1)} collective-permute-done((bf16[8,2,64,256]{3,2,1,0:T(8,128)(2,1)S(1)}, bf16[8,2,64,256]{3,2,1,0:T(8,128)(2,1)S(1)}, u32[]{:S(2)}, u32[]{:S(2)}) %collective-permute-start) | collective-permute-done | bytes 524320 | tf_op jit(solution)/shard_map/ppermute | solution.py:19
  68.0 0.0 copy-start.1
  68.1 0.8 copy-done.1
  68.8 3.8 %shard_map.57 = bf16[16,64,256]{2,1,0:T(8,128)(2,1)} custom-call(s32[4,3]{1,0:T(4,128)} %convert_element_type.3.flags_ref, bf16[16,3,64,256]{3,2,1,0:T(8,128)(2,1)} %copy-done, bf16[8,2,64,256]{3,2,1,0:T(8,128)(2,1)} %copy-done.1, bf16[16,64,256]{2,1,0:T(8,128)(2,1)} %shard_map.56.refs_1_), custom_call_target="tpu_custom_call", output_to_operand_aliasing={{}: (3, {})} | custom-call | tf_op jit(solution)/shard_map/pallas_call | solution.py:107
  72.7 18.7 %all_to_all.10 = bf16[16,64,256]{2,1,0:T(8,128)(2,1)S(1)} all-to-all(bf16[16,64,256]{2,1,0:T(8,128)(2,1)} %shard_map.57), channel_id=1, replica_groups=mesh['blk'=64,'head'=16] {'head'}, dimensions={0} | all-to-all | bytes 1048576 | tf_op jit(solution)/shard_map/all_to_all | solution.py:137
  91.4 0.8 copy.10
  (3 shorter events, 0.0 us)
Async XLA Ops:
  3.6 53.7 %copy-start.3 = (s32[4]{0:T(128)S(1)}, s32[4]{0:T(128)}, u32[]{:S(2)}) copy-start(s32[4]{0:T(128)} %param.9) | copy-start | bytes 52
  3.6 53.9 %copy-start.2 = (s32[4,3]{1,0:T(4,128)S(1)}, s32[4,3]{1,0:T(4,128)}, u32[]{:S(2)}) copy-start(s32[4,3]{1,0:T(4,128)} %param.8) | copy-start | bytes 148
  3.6 51.8 %all-to-all-start = ((bf16[16,3,64,256]{3,2,1,0:T(8,128)(2,1)}), bf16[16,3,64,256]{3,2,1,0:T(8,128)(2,1)S(1)}, u32[]{:S(2)}, u32[]{:S(2)}) async-start(bf16[16,3,64,256]{3,2,1,0:T(8,128)(2,1)} %shard_map.55), calls=%async_computation | async-start | bytes 3145728 | tf_op jit(solution)/shard_map/all_to_all | solution.py:125
  55.4 3.0 %copy-start = (bf16[16,3,64,256]{3,2,1,0:T(8,128)(2,1)}, bf16[16,3,64,256]{3,2,1,0:T(8,128)(2,1)S(1)}, u32[]{:S(2)}) copy-start(bf16[16,3,64,256]{3,2,1,0:T(8,128)(2,1)S(1)} %all-to-all-done.qkv_ref) | copy-start | bytes 4718596
  55.4 12.6 %collective-permute-start = (bf16[8,2,64,256]{3,2,1,0:T(8,128)(2,1)S(1)}, bf16[8,2,64,256]{3,2,1,0:T(8,128)(2,1)S(1)}, u32[]{:S(2)}, u32[]{:S(2)}) collective-permute-start(bf16[8,2,64,256]{3,2,1,0:T(8,128)(2,1)S(1)} %slice.4), channel_id=1, source_target_pairs={{0,16},{16,32},{32,48},{48,64},{64,80},{80,96},{96,112},{112,128},... | collective-permute-start | bytes 1572872 | tf_op jit(solution)/shard_map/ppermute | solution.py:19
  68.0 0.8 copy-start.1

commit v10 on v8

--- a/solution.py
+++ b/solution.py
@@ -11,6 +11,7 @@
 HDIM = 128
 BLOCK = 256
 CYCLE = 3
+LOG2E = 1.4426950408889634
 
 
 def from_behind(value, axis, steps):
@@ -54,10 +55,10 @@
                 v = jnp.concatenate(
                     (before_ref[halo, 1, :, cols].reshape(-1, HDIM), qkv_ref[own, 2, :, cols].reshape(-1, HDIM)), axis=0
                 )
-            s = lax.dot_general(q, k, (((1,), (1,)), ((), ())), preferred_element_type=jnp.float32) * scale
+            s = lax.dot_general(q, k, (((1,), (1,)), ((), ())), preferred_element_type=jnp.float32)
             s = jnp.where(allowed, s, -1e30)
             top = jnp.max(s, axis=1, keepdims=True)
-            w = jnp.exp(s - top)
+            w = jnp.exp2((s - top) * (scale * LOG2E))
             total = jnp.sum(w, axis=1, keepdims=True)
             summed = jnp.dot(w.astype(jnp.bfloat16), v, preferred_element_type=jnp.float32)
             result = (summed / total).astype(out_ref.dtype)
@@ -65,11 +66,16 @@
             out_ref[out_rows, :, cols] = result.reshape(per_block, chunk, HDIM)
 
 
-def slab_kernel(q_ref, k_ref, v_ref, out_ref):
-    peers, _, _, cols = out_ref.shape
-    for t, ref in enumerate((q_ref, k_ref, v_ref)):
+def slab_kernel(q_hbm, k_hbm, v_hbm, out_hbm, sems):
+    peers, _, _, cols = out_hbm.shape
+    copies = []
+    for t, ref in enumerate((q_hbm, k_hbm, v_hbm)):
         for dest in range(peers):
-            out_ref[dest, t] = ref[:, dest * cols : (dest + 1) * cols]
+            copy = pltpu.make_async_copy(ref.at[:, pl.ds(dest * cols, cols)], out_hbm.at[dest, t], sems.at[t, dest])
+            copy.start()
+            copies.append(copy)
+    for copy in copies:
+        copy.wait()
 
 
 def attend(blocks, flags, qkv, before, prior):
@@ -107,11 +113,13 @@
     per_block = BLOCK // chunk
     owned_blocks = peers // per_block
     reach = CYCLE - 1
+    anywhere = pl.BlockSpec(memory_space=pl.ANY)
     qkv_out = pl.pallas_call(
         slab_kernel,
         out_shape=jax.ShapeDtypeStruct((peers, 3, chunk, cols), queries.dtype),
-        in_specs=[pl.BlockSpec(memory_space=pltpu.VMEM)] * 3,
-        out_specs=pl.BlockSpec(memory_space=pltpu.VMEM),
+        in_specs=[anywhere] * 3,
+        out_specs=anywhere,
+        scratch_shapes=[pltpu.SemaphoreType.DMA((3, peers))],
     )(queries, keys, values)
     qkv = lax.all_to_all(qkv_out, "head", split_axis=0, concat_axis=0, tiled=True)
     before = from_behind(qkv[peers - reach * per_block :, 1:], "blk", 1)

time: 91.6 us -> 138 us (1.51)
  Pallas kernels: 10.3 us -> 56.9 us
    pallas_call x1, Pallas kernels: 2.62 us -> 49.2 us  [body(): pl.pallas_call(slab_kernel, out_shape=jax.ShapeDtypeStruct((peers, 3, chu...]
  transfers between devices with their start and end apart: 2 -> 2, of which waited for: 2 -> 2; matrix products, arithmetic and copies ran while one was open for 1% -> 1% of each run, Pallas kernels for 4% -> 3%
where the time goes in v10:
time: 138 us
  Pallas kernels  56.9 us (41%)
  waiting for transfers between devices  47.6 us (34%)
  blocking collectives  18.7 us (14%)
  starting transfers between devices  11.6 us (8%)
  local copies, waits for them, and re-layouts  1.78 us (1%)
    pallas_call x1, Pallas kernels, body(): pl.pallas_call(slab_kernel, out_shape=jax.ShapeDtypeStruct((peers, 3, chu...  49.2 us
    all_to_all x1, waiting for transfers between devices, body(): lax.all_to_all(qkv_out, 'head', split_axis=0, concat_axis=0, tiled=True)  41.9 us
    all_to_all x1, blocking collectives, body(): lax.all_to_all(joined, 'head', split_axis=0, concat_axis=0, tiled=True)  18.7 us
    all_to_all x1, starting transfers between devices, body(): lax.all_to_all(qkv_out, 'head', split_axis=0, concat_axis=0, tiled=True)  9.68 us
    pallas_call x2, Pallas kernels, attend(): pl.pallas_call(functools.partial(attention_kernel, blocks, before is not...  7.68 us
    ppermute x1, waiting for transfers between devices, from_behind(): lax.ppermute(value, axis, [(source, source + steps) for source in range(i...  5.7 us
  transfers between devices with their start and end apart: 2, of which 2 were waited for; matrix products, arithmetic and copies ran while one was open for 1% of the time, Pallas kernels for 3%

profile of v10, /device:TPU:256, one launch (start us, length us, event | category | flops | bytes accessed | tf_op | source)
XLA Modules:
  0.0 137.6 jit_solution(480250723804167190)
XLA Ops:
  0.0 49.2 %shard_map.55 = bf16[16,3,64,256]{3,2,1,0:T(8,128)(2,1)} custom-call(bf16[64,4096]{1,0:T(8,128)(2,1)} %q_hbm.1, bf16[64,4096]{1,0:T(8,128)(2,1)} %k_hbm.1, bf16[64,4096]{1,0:T(8,128)(2,1)} %v_hbm.1), custom_call_target="tpu_custom_call" | custom-call | tf_op jit(solution)/shard_map/pallas_call | solution.py:117
  49.2 0.0 copy-start.3
  49.2 0.0 copy-start.2
  49.2 9.7 %all-to-all-start = ((bf16[16,3,64,256]{3,2,1,0:T(8,128)(2,1)}), bf16[16,3,64,256]{3,2,1,0:T(8,128)(2,1)S(1)}, u32[]{:S(2)}, u32[]{:S(2)}) async-start(bf16[16,3,64,256]{3,2,1,0:T(8,128)(2,1)} %shard_map.55), calls=%async_computation | async-start | bytes 3145728 | tf_op jit(solution)/shard_map/all_to_all | solution.py:124
  58.9 41.9 %all-to-all-done.qkv_ref = bf16[16,3,64,256]{3,2,1,0:T(8,128)(2,1)S(1)} async-done(((bf16[16,3,64,256]{3,2,1,0:T(8,128)(2,1)}), bf16[16,3,64,256]{3,2,1,0:T(8,128)(2,1)S(1)}, u32[]{:S(2)}, u32[]{:S(2)}) %all-to-all-start) | async-done | bytes 1572896 | tf_op jit(solution)/shard_map/all_to_all | solution.py:124
  100.8 0.0 copy-start
  100.9 1.9 %collective-permute-start = (bf16[8,2,64,256]{3,2,1,0:T(8,128)(2,1)S(1)}, bf16[8,2,64,256]{3,2,1,0:T(8,128)(2,1)S(1)}, u32[]{:S(2)}, u32[]{:S(2)}) collective-permute-start(bf16[8,2,64,256]{3,2,1,0:T(8,128)(2,1)S(1)} %slice.4), channel_id=1, source_target_pairs={{0,16},{16,32},{32,48},{48,64},{64,80},{80,96},{96,112},{112,128},... | collective-permute-start | bytes 1572872 | tf_op jit(solution)/shard_map/ppermute | solution.py:20
  102.8 0.0 copy-done.3
  102.8 0.1 iota_compare_fusion
  102.9 0.1 broadcast_subtract_fusion
  103.0 0.0 copy-done.2
  103.0 0.2 and_reduce_fusion
  103.2 0.1 copy.8
  103.3 0.6 convert_element_type.3.flags_ref
  103.9 0.0 copy-done
  103.9 3.9 %shard_map.56.refs_1_ = bf16[16,64,256]{2,1,0:T(8,128)(2,1)} custom-call(s32[4,3]{1,0:T(4,128)} %convert_element_type.3.flags_ref, bf16[16,3,64,256]{3,2,1,0:T(8,128)(2,1)} %copy-done), custom_call_target="tpu_custom_call" | custom-call | tf_op jit(solution)/shard_map/pallas_call | solution.py:99
  107.8 5.7 %collective-permute-done.refs_0_ = bf16[8,2,64,256]{3,2,1,0:T(8,128)(2,1)S(1)} collective-permute-done((bf16[8,2,64,256]{3,2,1,0:T(8,128)(2,1)S(1)}, bf16[8,2,64,256]{3,2,1,0:T(8,128)(2,1)S(1)}, u32[]{:S(2)}, u32[]{:S(2)}) %collective-permute-start) | collective-permute-done | bytes 524320 | tf_op jit(solution)/shard_map/ppermute | solution.py:20
  113.5 0.0 copy-start.1
  113.5 0.8 copy-done.1
  114.3 3.8 %shard_map.57 = bf16[16,64,256]{2,1,0:T(8,128)(2,1)} custom-call(s32[4,3]{1,0:T(4,128)} %convert_element_type.3.flags_ref, bf16[16,3,64,256]{3,2,1,0:T(8,128)(2,1)} %copy-done, bf16[8,2,64,256]{3,2,1,0:T(8,128)(2,1)} %copy-done.1, bf16[16,64,256]{2,1,0:T(8,128)(2,1)} %shard_map.56.refs_1_), custom_call_target="tpu_custom_call", output_to_operand_aliasing={{}: (3, {})} | custom-call | tf_op jit(solution)/shard_map/pallas_call | solution.py:99
  118.1 18.7 %all_to_all.10 = bf16[16,64,256]{2,1,0:T(8,128)(2,1)S(1)} all-to-all(bf16[16,64,256]{2,1,0:T(8,128)(2,1)} %shard_map.57), channel_id=1, replica_groups=mesh['blk'=64,'head'=16] {'head'}, dimensions={0} | all-to-all | bytes 1048576 | tf_op jit(solution)/shard_map/all_to_all | solution.py:136
  136.8 0.8 copy.10
  (3 shorter events, 0.0 us)
Async XLA Ops:
  49.2 53.6 %copy-start.3 = (s32[4]{0:T(128)S(1)}, s32[4]{0:T(128)}, u32[]{:S(2)}) copy-start(s32[4]{0:T(128)} %param.9) | copy-start | bytes 52
  49.2 53.8 %copy-start.2 = (s32[4,3]{1,0:T(4,128)S(1)}, s32[4,3]{1,0:T(4,128)}, u32[]{:S(2)}) copy-start(s32[4,3]{1,0:T(4,128)} %param.8) | copy-start | bytes 148
  49.2 51.6 %all-to-all-start = ((bf16[16,3,64,256]{3,2,1,0:T(8,128)(2,1)}), bf16[16,3,64,256]{3,2,1,0:T(8,128)(2,1)S(1)}, u32[]{:S(2)}, u32[]{:S(2)}) async-start(bf16[16,3,64,256]{3,2,1,0:T(8,128)(2,1)} %shard_map.55), calls=%async_computation | async-start | bytes 3145728 | tf_op jit(solution)/shard_map/all_to_all | solution.py:124
  100.8 3.0 %copy-start = (bf16[16,3,64,256]{3,2,1,0:T(8,128)(2,1)}, bf16[16,3,64,256]{3,2,1,0:T(8,128)(2,1)S(1)}, u32[]{:S(2)}) copy-start(bf16[16,3,64,256]{3,2,1,0:T(8,128)(2,1)S(1)} %all-to-all-done.qkv_ref) | copy-start | bytes 4718596
  100.9 12.6 %collective-permute-start = (bf16[8,2,64,256]{3,2,1,0:T(8,128)(2,1)S(1)}, bf16[8,2,64,256]{3,2,1,0:T(8,128)(2,1)S(1)}, u32[]{:S(2)}, u32[]{:S(2)}) collective-permute-start(bf16[8,2,64,256]{3,2,1,0:T(8,128)(2,1)S(1)} %slice.4), channel_id=1, source_target_pairs={{0,16},{16,32},{32,48},{48,64},{64,80},{80,96},{96,112},{112,128},... | collective-permute-start | bytes 1572872 | tf_op jit(solution)/shard_map/ppermute | solution.py:20
  113.5 0.8 copy-start.1

commit v11 on v8

--- a/solution.py
+++ b/solution.py
@@ -11,6 +11,7 @@
 HDIM = 128
 BLOCK = 256
 CYCLE = 3
+LOG2E = 1.4426950408889634
 
 
 def from_behind(value, axis, steps):
@@ -54,10 +55,10 @@
                 v = jnp.concatenate(
                     (before_ref[halo, 1, :, cols].reshape(-1, HDIM), qkv_ref[own, 2, :, cols].reshape(-1, HDIM)), axis=0
                 )
-            s = lax.dot_general(q, k, (((1,), (1,)), ((), ())), preferred_element_type=jnp.float32) * scale
+            s = lax.dot_general(q, k, (((1,), (1,)), ((), ())), preferred_element_type=jnp.float32)
             s = jnp.where(allowed, s, -1e30)
             top = jnp.max(s, axis=1, keepdims=True)
-            w = jnp.exp(s - top)
+            w = jnp.exp2((s - top) * (scale * LOG2E))
             total = jnp.sum(w, axis=1, keepdims=True)
             summed = jnp.dot(w.astype(jnp.bfloat16), v, preferred_element_type=jnp.float32)
             result = (summed / total).astype(out_ref.dtype)

time: 91.6 us -> 91.6 us (level)
  no operation moved by 1% of the time
where the time goes in v11:
time: 91.6 us; the launch traced here: 91.2 us
  waiting for transfers between devices  47.6 us (52%)
  blocking collectives  18.7 us (20%)
  starting transfers between devices  11.7 us (13%)
  Pallas kernels  10.3 us (11%)
  local copies, waits for them, and re-layouts  1.78 us (2%)
  other arithmetic  0.95 us (1%)
    all_to_all x1, waiting for transfers between devices, body(): lax.all_to_all(qkv_out, 'head', split_axis=0, concat_axis=0, tiled=True)  41.9 us
    all_to_all x1, blocking collectives, body(): lax.all_to_all(joined, 'head', split_axis=0, concat_axis=0, tiled=True)  18.7 us
    all_to_all x1, starting transfers between devices, body(): lax.all_to_all(qkv_out, 'head', split_axis=0, concat_axis=0, tiled=True)  9.8 us
    pallas_call x2, Pallas kernels, attend(): pl.pallas_call(functools.partial(attention_kernel, blocks, before is not...  7.68 us
    ppermute x1, waiting for transfers between devices, from_behind(): lax.ppermute(value, axis, [(source, source + steps) for source in range(i...  5.7 us
    pallas_call x1, Pallas kernels, body(): pl.pallas_call(slab_kernel, out_shape=jax.ShapeDtypeStruct((peers, 3, chu...  2.62 us
    ppermute x1, starting transfers between devices, from_behind(): lax.ppermute(value, axis, [(source, source + steps) for source in range(i...  1.92 us
  transfers between devices with their start and end apart: 2, of which 2 were waited for; matrix products, arithmetic and copies ran while one was open for 1% of the time, Pallas kernels for 4%

profile of v11, /device:TPU:256, one launch (start us, length us, event | category | flops | bytes accessed | tf_op | source)
XLA Modules:
  0.0 91.2 jit_solution(12867411204963758299)
XLA Ops:
  0.0 2.6 %shard_map.55 = bf16[16,3,64,256]{3,2,1,0:T(8,128)(2,1)} custom-call(bf16[64,4096]{1,0:T(8,128)(2,1)} %q_ref.1, bf16[64,4096]{1,0:T(8,128)(2,1)} %k_ref.1, bf16[64,4096]{1,0:T(8,128)(2,1)} %v_ref.1), custom_call_target="tpu_custom_call" | custom-call | tf_op jit(solution)/shard_map/pallas_call | solution.py:111
  2.6 0.0 copy-start.3
  2.6 0.0 copy-start.2
  2.6 9.8 %all-to-all-start = ((bf16[16,3,64,256]{3,2,1,0:T(8,128)(2,1)}), bf16[16,3,64,256]{3,2,1,0:T(8,128)(2,1)S(1)}, u32[]{:S(2)}, u32[]{:S(2)}) async-start(bf16[16,3,64,256]{3,2,1,0:T(8,128)(2,1)} %shard_map.55), calls=%async_computation | async-start | bytes 3145728 | tf_op jit(solution)/shard_map/all_to_all | solution.py:117
  12.5 41.9 %all-to-all-done.qkv_ref = bf16[16,3,64,256]{3,2,1,0:T(8,128)(2,1)S(1)} async-done(((bf16[16,3,64,256]{3,2,1,0:T(8,128)(2,1)}), bf16[16,3,64,256]{3,2,1,0:T(8,128)(2,1)S(1)}, u32[]{:S(2)}, u32[]{:S(2)}) %all-to-all-start) | async-done | bytes 1572896 | tf_op jit(solution)/shard_map/all_to_all | solution.py:117
  54.4 0.0 copy-start
  54.4 1.9 %collective-permute-start = (bf16[8,2,64,256]{3,2,1,0:T(8,128)(2,1)S(1)}, bf16[8,2,64,256]{3,2,1,0:T(8,128)(2,1)S(1)}, u32[]{:S(2)}, u32[]{:S(2)}) collective-permute-start(bf16[8,2,64,256]{3,2,1,0:T(8,128)(2,1)S(1)} %slice.4), channel_id=1, source_target_pairs={{0,16},{16,32},{32,48},{48,64},{64,80},{80,96},{96,112},{112,128},... | collective-permute-start | bytes 1572872 | tf_op jit(solution)/shard_map/ppermute | solution.py:20
  56.4 0.0 copy-done.3
  56.4 0.1 iota_compare_fusion
  56.4 0.1 broadcast_subtract_fusion
  56.5 0.0 copy-done.2
  56.5 0.2 and_reduce_fusion
  56.7 0.1 copy.8
  56.8 0.6 convert_element_type.3.flags_ref
  57.4 0.0 copy-done
  57.4 3.9 %shard_map.56.refs_1_ = bf16[16,64,256]{2,1,0:T(8,128)(2,1)} custom-call(s32[4,3]{1,0:T(4,128)} %convert_element_type.3.flags_ref, bf16[16,3,64,256]{3,2,1,0:T(8,128)(2,1)} %copy-done), custom_call_target="tpu_custom_call" | custom-call | tf_op jit(solution)/shard_map/pallas_call | solution.py:94
  61.3 5.7 %collective-permute-done.refs_0_ = bf16[8,2,64,256]{3,2,1,0:T(8,128)(2,1)S(1)} collective-permute-done((bf16[8,2,64,256]{3,2,1,0:T(8,128)(2,1)S(1)}, bf16[8,2,64,256]{3,2,1,0:T(8,128)(2,1)S(1)}, u32[]{:S(2)}, u32[]{:S(2)}) %collective-permute-start) | collective-permute-done | bytes 524320 | tf_op jit(solution)/shard_map/ppermute | solution.py:20
  67.0 0.0 copy-start.1
  67.0 0.8 copy-done.1
  67.8 3.8 %shard_map.57 = bf16[16,64,256]{2,1,0:T(8,128)(2,1)} custom-call(s32[4,3]{1,0:T(4,128)} %convert_element_type.3.flags_ref, bf16[16,3,64,256]{3,2,1,0:T(8,128)(2,1)} %copy-done, bf16[8,2,64,256]{3,2,1,0:T(8,128)(2,1)} %copy-done.1, bf16[16,64,256]{2,1,0:T(8,128)(2,1)} %shard_map.56.refs_1_), custom_call_target="tpu_custom_call", output_to_operand_aliasing={{}: (3, {})} | custom-call | tf_op jit(solution)/shard_map/pallas_call | solution.py:94
  71.6 18.7 %all_to_all.10 = bf16[16,64,256]{2,1,0:T(8,128)(2,1)S(1)} all-to-all(bf16[16,64,256]{2,1,0:T(8,128)(2,1)} %shard_map.57), channel_id=1, replica_groups=mesh['blk'=64,'head'=16] {'head'}, dimensions={0} | all-to-all | bytes 1048576 | tf_op jit(solution)/shard_map/all_to_all | solution.py:129
  90.3 0.8 copy.10
  (3 shorter events, 0.0 us)
Async XLA Ops:
  2.6 53.7 %copy-start.3 = (s32[4]{0:T(128)S(1)}, s32[4]{0:T(128)}, u32[]{:S(2)}) copy-start(s32[4]{0:T(128)} %param.9) | copy-start | bytes 52
  2.6 53.9 %copy-start.2 = (s32[4,3]{1,0:T(4,128)S(1)}, s32[4,3]{1,0:T(4,128)}, u32[]{:S(2)}) copy-start(s32[4,3]{1,0:T(4,128)} %param.8) | copy-start | bytes 148
  2.6 51.8 %all-to-all-start = ((bf16[16,3,64,256]{3,2,1,0:T(8,128)(2,1)}), bf16[16,3,64,256]{3,2,1,0:T(8,128)(2,1)S(1)}, u32[]{:S(2)}, u32[]{:S(2)}) async-start(bf16[16,3,64,256]{3,2,1,0:T(8,128)(2,1)} %shard_map.55), calls=%async_computation | async-start | bytes 3145728 | tf_op jit(solution)/shard_map/all_to_all | solution.py:117
  54.4 3.0 %copy-start = (bf16[16,3,64,256]{3,2,1,0:T(8,128)(2,1)}, bf16[16,3,64,256]{3,2,1,0:T(8,128)(2,1)S(1)}, u32[]{:S(2)}) copy-start(bf16[16,3,64,256]{3,2,1,0:T(8,128)(2,1)S(1)} %all-to-all-done.qkv_ref) | copy-start | bytes 4718596
  54.4 12.6 %collective-permute-start = (bf16[8,2,64,256]{3,2,1,0:T(8,128)(2,1)S(1)}, bf16[8,2,64,256]{3,2,1,0:T(8,128)(2,1)S(1)}, u32[]{:S(2)}, u32[]{:S(2)}) collective-permute-start(bf16[8,2,64,256]{3,2,1,0:T(8,128)(2,1)S(1)} %slice.4), channel_id=1, source_target_pairs={{0,16},{16,32},{32,48},{48,64},{64,80},{80,96},{96,112},{112,128},... | collective-permute-start | bytes 1572872 | tf_op jit(solution)/shard_map/ppermute | solution.py:20
  67.0 0.8 copy-start.1

commit v12 on v8

--- a/solution.py
+++ b/solution.py
@@ -121,10 +121,7 @@
     used = jnp.arange(CYCLE, dtype=jnp.int32)[None, :] < block_counts[:, None]
     hits = used[:, None, :] & (block_lists[:, None, :] == (target[:, None] - distance[None, :])[:, :, None])
     flags = jnp.any(hits, axis=2).astype(jnp.int32)
-    late = tuple(range(min(reach, owned_blocks)))
-    early = tuple(range(len(late), owned_blocks))
-    joined = attend(early, flags, qkv, None, None) if early else None
-    joined = attend(late, flags, qkv, before, joined)
+    joined = attend(tuple(range(owned_blocks)), flags, qkv, before, None)
     back = lax.all_to_all(joined, "head", split_axis=0, concat_axis=0, tiled=True)
     return back.transpose(1, 0, 2).reshape(chunk, width)
 

time: 91.6 us -> 93.4 us (1.020)
  waiting for transfers between devices: 47.6 us -> 51.5 us
  Pallas kernels: 10.3 us -> 8.3 us
    ppermute x1, waiting for transfers between devices: 5.68 us -> 9.61 us  [from_behind(): lax.ppermute(value, axis, [(source, source + steps) for source in range(i...]
    pallas_call x2 -> x1, Pallas kernels: 7.73 us -> 5.68 us  [attend(): pl.pallas_call(functools.partial(attention_kernel, blocks, before is not...]
  transfers between devices with their start and end apart: 2 -> 2, of which waited for: 2 -> 2; matrix products, arithmetic and copies ran while one was open for 1% -> 1% of each run, Pallas kernels for 4% -> 0%
where the time goes in v12:
time: 93.4 us; the launch traced here: 93.1 us
  waiting for transfers between devices  51.5 us (55%)
  blocking collectives  18.7 us (20%)
  starting transfers between devices  11.7 us (13%)
  Pallas kernels  8.3 us (9%)
  local copies, waits for them, and re-layouts  1.78 us (2%)
  other arithmetic  0.95 us (1%)
    all_to_all x1, waiting for transfers between devices, body(): lax.all_to_all(qkv_out, 'head', split_axis=0, concat_axis=0, tiled=True)  41.9 us
    all_to_all x1, blocking collectives, body(): lax.all_to_all(joined, 'head', split_axis=0, concat_axis=0, tiled=True)  18.7 us
    all_to_all x1, starting transfers between devices, body(): lax.all_to_all(qkv_out, 'head', split_axis=0, concat_axis=0, tiled=True)  9.8 us
    ppermute x1, waiting for transfers between devices, from_behind(): lax.ppermute(value, axis, [(source, source + steps) for source in range(i...  9.61 us
    pallas_call x1, Pallas kernels, attend(): pl.pallas_call(functools.partial(attention_kernel, blocks, before is not...  5.68 us
    pallas_call x1, Pallas kernels, body(): pl.pallas_call(slab_kernel, out_shape=jax.ShapeDtypeStruct((peers, 3, chu...  2.62 us
    ppermute x1, starting transfers between devices, from_behind(): lax.ppermute(value, axis, [(source, source + steps) for source in range(i...  1.92 us
  transfers between devices with their start and end apart: 2, of which 2 were waited for; matrix products, arithmetic and copies ran while one was open for 1% of the time, Pallas kernels for 0%

profile of v12, /device:TPU:256, one launch (start us, length us, event | category | flops | bytes accessed | tf_op | source)
XLA Modules:
  0.0 93.1 jit_solution(4561255578983188024)
XLA Ops:
  0.0 2.6 %shard_map.55 = bf16[16,3,64,256]{3,2,1,0:T(8,128)(2,1)} custom-call(bf16[64,4096]{1,0:T(8,128)(2,1)} %q_ref.1, bf16[64,4096]{1,0:T(8,128)(2,1)} %k_ref.1, bf16[64,4096]{1,0:T(8,128)(2,1)} %v_ref.1), custom_call_target="tpu_custom_call" | custom-call | tf_op jit(solution)/shard_map/pallas_call | solution.py:110
  2.6 0.0 copy-start.3
  2.6 0.0 copy-start.2
  2.6 9.8 %all-to-all-start = ((bf16[16,3,64,256]{3,2,1,0:T(8,128)(2,1)}), bf16[16,3,64,256]{3,2,1,0:T(8,128)(2,1)S(1)}, u32[]{:S(2)}, u32[]{:S(2)}) async-start(bf16[16,3,64,256]{3,2,1,0:T(8,128)(2,1)} %shard_map.55), calls=%async_computation | async-start | bytes 3145728 | tf_op jit(solution)/shard_map/all_to_all | solution.py:116
  12.5 41.9 %all-to-all-done.qkv_ref = bf16[16,3,64,256]{3,2,1,0:T(8,128)(2,1)S(1)} async-done(((bf16[16,3,64,256]{3,2,1,0:T(8,128)(2,1)}), bf16[16,3,64,256]{3,2,1,0:T(8,128)(2,1)S(1)}, u32[]{:S(2)}, u32[]{:S(2)}) %all-to-all-start) | async-done | bytes 1572896 | tf_op jit(solution)/shard_map/all_to_all | solution.py:116
  54.4 0.0 copy-start
  54.4 1.9 %collective-permute-start = (bf16[8,2,64,256]{3,2,1,0:T(8,128)(2,1)S(1)}, bf16[8,2,64,256]{3,2,1,0:T(8,128)(2,1)S(1)}, u32[]{:S(2)}, u32[]{:S(2)}) collective-permute-start(bf16[8,2,64,256]{3,2,1,0:T(8,128)(2,1)S(1)} %slice.4), channel_id=1, source_target_pairs={{0,16},{16,32},{32,48},{48,64},{64,80},{80,96},{96,112},{112,128},... | collective-permute-start | bytes 1572872 | tf_op jit(solution)/shard_map/ppermute | solution.py:19
  56.4 0.0 copy-done.3
  56.4 0.1 iota_compare_fusion
  56.4 0.1 broadcast_subtract_fusion
  56.5 0.0 copy-done.2
  56.5 0.2 and_reduce_fusion
  56.7 0.1 copy.7
  56.8 0.6 convert_element_type.3.flags_ref
  57.4 9.6 %collective-permute-done.refs_0_ = bf16[8,2,64,256]{3,2,1,0:T(8,128)(2,1)S(1)} collective-permute-done((bf16[8,2,64,256]{3,2,1,0:T(8,128)(2,1)S(1)}, bf16[8,2,64,256]{3,2,1,0:T(8,128)(2,1)S(1)}, u32[]{:S(2)}, u32[]{:S(2)}) %collective-permute-start) | collective-permute-done | bytes 524320 | tf_op jit(solution)/shard_map/ppermute | solution.py:19
  67.0 0.0 copy-done
  67.0 0.0 copy-start.1
  67.0 0.8 copy-done.1
  67.8 5.7 %shard_map.56 = bf16[16,64,256]{2,1,0:T(8,128)(2,1)} custom-call(s32[4,3]{1,0:T(4,128)} %convert_element_type.3.flags_ref, bf16[16,3,64,256]{3,2,1,0:T(8,128)(2,1)} %copy-done, bf16[8,2,64,256]{3,2,1,0:T(8,128)(2,1)} %copy-done.1), custom_call_target="tpu_custom_call" | custom-call | tf_op jit(solution)/shard_map/pallas_call | solution.py:93
  73.5 18.7 %all_to_all.10 = bf16[16,64,256]{2,1,0:T(8,128)(2,1)S(1)} all-to-all(bf16[16,64,256]{2,1,0:T(8,128)(2,1)} %shard_map.56), channel_id=1, replica_groups=mesh['blk'=64,'head'=16] {'head'}, dimensions={0} | all-to-all | bytes 1048576 | tf_op jit(solution)/shard_map/all_to_all | solution.py:125
  92.2 0.8 copy.9
  (3 shorter events, 0.0 us)
Async XLA Ops:
  2.6 53.7 %copy-start.3 = (s32[4]{0:T(128)S(1)}, s32[4]{0:T(128)}, u32[]{:S(2)}) copy-start(s32[4]{0:T(128)} %param.9) | copy-start | bytes 52
  2.6 53.9 %copy-start.2 = (s32[4,3]{1,0:T(4,128)S(1)}, s32[4,3]{1,0:T(4,128)}, u32[]{:S(2)}) copy-start(s32[4,3]{1,0:T(4,128)} %param.8) | copy-start | bytes 148
  2.6 51.8 %all-to-all-start = ((bf16[16,3,64,256]{3,2,1,0:T(8,128)(2,1)}), bf16[16,3,64,256]{3,2,1,0:T(8,128)(2,1)S(1)}, u32[]{:S(2)}, u32[]{:S(2)}) async-start(bf16[16,3,64,256]{3,2,1,0:T(8,128)(2,1)} %shard_map.55), calls=%async_computation | async-start | bytes 3145728 | tf_op jit(solution)/shard_map/all_to_all | solution.py:116
  54.4 12.7 %copy-start = (bf16[16,3,64,256]{3,2,1,0:T(8,128)(2,1)}, bf16[16,3,64,256]{3,2,1,0:T(8,128)(2,1)S(1)}, u32[]{:S(2)}) copy-start(bf16[16,3,64,256]{3,2,1,0:T(8,128)(2,1)S(1)} %all-to-all-done.qkv_ref) | copy-start | bytes 4718596
  54.4 12.6 %collective-permute-start = (bf16[8,2,64,256]{3,2,1,0:T(8,128)(2,1)S(1)}, bf16[8,2,64,256]{3,2,1,0:T(8,128)(2,1)S(1)}, u32[]{:S(2)}, u32[]{:S(2)}) collective-permute-start(bf16[8,2,64,256]{3,2,1,0:T(8,128)(2,1)S(1)} %slice.4), channel_id=1, source_target_pairs={{0,16},{16,32},{32,48},{48,64},{64,80},{80,96},{96,112},{112,128},... | collective-permute-start | bytes 1572872 | tf_op jit(solution)/shard_map/ppermute | solution.py:19
  67.0 0.8 copy-start.1

commit v13 on v8

--- a/solution.py
+++ b/solution.py
@@ -19,7 +19,7 @@
     return lax.ppermute(value, axis, [(source, source + steps) for source in range(initial, last)])
 
 
-def attention_kernel(blocks, has_before, flags_ref, qkv_ref, *refs):
+def attention_kernel(blocks, has_before, lists_ref, counts_ref, qkv_ref, *refs):
     before_ref = refs[0] if has_before else None
     out_ref = refs[-1]
     _, _, chunk, width = qkv_ref.shape
@@ -31,11 +31,17 @@
     row_pos = lax.broadcasted_iota(jnp.int32, (BLOCK, CYCLE * BLOCK), 0)
     col_pos = lax.broadcasted_iota(jnp.int32, (BLOCK, CYCLE * BLOCK), 1)
     causal = (col_pos < reach * BLOCK) | (col_pos - reach * BLOCK <= row_pos)
+    owned_blocks = counts_ref.shape[0]
+    target = lax.axis_index("blk").astype(jnp.int32) * owned_blocks
     for local in blocks:
         allowed = causal
         for place in range(CYCLE):
             inside = (col_pos >= place * BLOCK) & (col_pos < (place + 1) * BLOCK)
-            allowed = allowed & (jnp.logical_not(inside) | (flags_ref[local, place] != 0))
+            wanted = None
+            for entry in range(CYCLE):
+                hit = (counts_ref[local] > entry) & (lists_ref[local, entry] == target + local - (reach - place))
+                wanted = hit if wanted is None else wanted | hit
+            allowed = allowed & (jnp.logical_not(inside) | wanted)
         rows = slice(local * per_block, (local + 1) * per_block)
         first = local - reach
         for head in range(local_heads):
@@ -72,13 +78,14 @@
             out_ref[dest, t] = ref[:, dest * cols : (dest + 1) * cols]
 
 
-def attend(blocks, flags, qkv, before, prior):
+def attend(blocks, block_lists, block_counts, qkv, before, prior):
     peers, _, chunk, width = qkv.shape
     per_block = BLOCK // chunk
     rows = len(blocks) * per_block
     reads = (blocks[-1] + 1) * per_block if blocks[0] == 0 else peers
-    operands = [flags, qkv]
+    operands = [block_lists, block_counts, qkv]
     in_specs = [
+        pl.BlockSpec(memory_space=pltpu.SMEM),
         pl.BlockSpec(memory_space=pltpu.SMEM),
         pl.BlockSpec((reads,) + qkv.shape[1:], lambda i: (0, 0, 0, 0)),
     ]
@@ -115,16 +122,10 @@
     )(queries, keys, values)
     qkv = lax.all_to_all(qkv_out, "head", split_axis=0, concat_axis=0, tiled=True)
     before = from_behind(qkv[peers - reach * per_block :, 1:], "blk", 1)
-    own = lax.axis_index("blk")
-    target = own * owned_blocks + jnp.arange(owned_blocks, dtype=jnp.int32)
-    distance = reach - jnp.arange(CYCLE, dtype=jnp.int32)
-    used = jnp.arange(CYCLE, dtype=jnp.int32)[None, :] < block_counts[:, None]
-    hits = used[:, None, :] & (block_lists[:, None, :] == (target[:, None] - distance[None, :])[:, :, None])
-    flags = jnp.any(hits, axis=2).astype(jnp.int32)
     late = tuple(range(min(reach, owned_blocks)))
     early = tuple(range(len(late), owned_blocks))
-    joined = attend(early, flags, qkv, None, None) if early else None
-    joined = attend(late, flags, qkv, before, joined)
+    joined = attend(early, block_lists, block_counts, qkv, None, None) if early else None
+    joined = attend(late, block_lists, block_counts, qkv, before, joined)
     back = lax.all_to_all(joined, "head", split_axis=0, concat_axis=0, tiled=True)
     return back.transpose(1, 0, 2).reshape(chunk, width)
 

time: 91.6 us -> 90.5 us (0.988)
  blocking collectives: 18.7 us -> 69.4 us
  waiting for transfers between devices: 47.6 us -> 6.75 us
  starting transfers between devices: 11.7 us -> 1.92 us
  other arithmetic: 0.95 us -> 0 us
    all_to_all x0 -> x1, blocking collectives: none -> 49.8 us  [body(): lax.all_to_all(qkv_out, 'head', split_axis=0, concat_axis=0, tiled=True)]
    all_to_all x1 -> x0, waiting for transfers between devices: 41.9 us -> none  [body(): lax.all_to_all(qkv_out, 'head', split_axis=0, concat_axis=0, tiled=True)]
    all_to_all x1 -> x0, starting transfers between devices: 9.8 us -> none  [body(): lax.all_to_all(qkv_out, 'head', split_axis=0, concat_axis=0, tiled=True)]
    ppermute x1, waiting for transfers between devices: 5.68 us -> 6.75 us  [from_behind(): lax.ppermute(value, axis, [(source, source + steps) for source in range(i...]
  transfers between devices with their start and end apart: 2 -> 1, of which waited for: 2 -> 1; matrix products, arithmetic and copies ran while one was open for 1% -> 0% of each run, Pallas kernels for 4% -> 4%
where the time goes in v13:
time: 90.5 us; the launch traced here: 90.1 us
  blocking collectives  69.4 us (77%)
  Pallas kernels  10.3 us (11%)
  waiting for transfers between devices  6.75 us (7%)
  starting transfers between devices  1.92 us (2%)
  local copies, waits for them, and re-layouts  1.66 us (2%)
    all_to_all x1, blocking collectives, body(): lax.all_to_all(qkv_out, 'head', split_axis=0, concat_axis=0, tiled=True)  49.8 us
    all_to_all x1, blocking collectives, body(): lax.all_to_all(joined, 'head', split_axis=0, concat_axis=0, tiled=True)  19.5 us
    pallas_call x2, Pallas kernels, attend(): pl.pallas_call(functools.partial(attention_kernel, blocks, before is not...  7.71 us
    ppermute x1, waiting for transfers between devices, from_behind(): lax.ppermute(value, axis, [(source, source + steps) for source in range(i...  6.75 us
    pallas_call x1, Pallas kernels, body(): pl.pallas_call(slab_kernel, out_shape=jax.ShapeDtypeStruct((peers, 3, chu...  2.63 us
    ppermute x1, starting transfers between devices, from_behind(): lax.ppermute(value, axis, [(source, source + steps) for source in range(i...  1.92 us
  transfers between devices with their start and end apart: 1, of which 1 were waited for; matrix products, arithmetic and copies ran while one was open for 0% of the time, Pallas kernels for 4%

profile of v13, /device:TPU:256, one launch (start us, length us, event | category | flops | bytes accessed | tf_op | source)
XLA Modules:
  0.0 90.1 jit_solution(1945285588912792600)
XLA Ops:
  0.0 2.6 %shard_map.55 = bf16[16,3,64,256]{3,2,1,0:T(8,128)(2,1)} custom-call(bf16[64,4096]{1,0:T(8,128)(2,1)} %q_ref.1, bf16[64,4096]{1,0:T(8,128)(2,1)} %k_ref.1, bf16[64,4096]{1,0:T(8,128)(2,1)} %v_ref.1), custom_call_target="tpu_custom_call" | custom-call | tf_op jit(solution)/shard_map/pallas_call | solution.py:117
  2.6 49.8 %all_to_all.10.qkv_ref = bf16[16,3,64,256]{3,2,1,0:T(8,128)(2,1)S(1)} all-to-all(bf16[16,3,64,256]{3,2,1,0:T(8,128)(2,1)} %shard_map.55), channel_id=1, replica_groups=mesh['blk'=64,'head'=16] {'head'}, dimensions={0} | all-to-all | bytes 3145728 | tf_op jit(solution)/shard_map/all_to_all | solution.py:123
  52.5 0.0 copy-start
  52.5 1.9 %collective-permute-start = (bf16[8,2,64,256]{3,2,1,0:T(8,128)(2,1)S(1)}, bf16[8,2,64,256]{3,2,1,0:T(8,128)(2,1)S(1)}, u32[]{:S(2)}, u32[]{:S(2)}) collective-permute-start(bf16[8,2,64,256]{3,2,1,0:T(8,128)(2,1)S(1)} %slice.4), channel_id=1, source_target_pairs={{0,16},{16,32},{32,48},{48,64},{64,80},{80,96},{96,112},{112,128},... | collective-permute-start | bytes 1572872 | tf_op jit(solution)/shard_map/ppermute | solution.py:19
  54.4 0.0 copy-done
  54.5 3.9 %shard_map.56.refs_1_ = bf16[16,64,256]{2,1,0:T(8,128)(2,1)} custom-call(s32[4,3]{1,0:T(4,128)} %lists_ref.3, s32[4]{0:T(128)} %counts_ref.3, bf16[16,3,64,256]{3,2,1,0:T(8,128)(2,1)} %copy-done), custom_call_target="tpu_custom_call" | custom-call | tf_op jit(solution)/shard_map/pallas_call | solution.py:100
  58.4 6.8 %collective-permute-done.refs_0_ = bf16[8,2,64,256]{3,2,1,0:T(8,128)(2,1)S(1)} collective-permute-done((bf16[8,2,64,256]{3,2,1,0:T(8,128)(2,1)S(1)}, bf16[8,2,64,256]{3,2,1,0:T(8,128)(2,1)S(1)}, u32[]{:S(2)}, u32[]{:S(2)}) %collective-permute-start) | collective-permute-done | bytes 524320 | tf_op jit(solution)/shard_map/ppermute | solution.py:19
  65.1 0.0 copy-start.1
  65.1 0.8 copy-done.1
  65.9 3.8 %shard_map.57 = bf16[16,64,256]{2,1,0:T(8,128)(2,1)} custom-call(s32[4,3]{1,0:T(4,128)} %lists_ref.3, s32[4]{0:T(128)} %counts_ref.3, bf16[16,3,64,256]{3,2,1,0:T(8,128)(2,1)} %copy-done, bf16[8,2,64,256]{3,2,1,0:T(8,128)(2,1)} %copy-done.1, bf16[16,64,256]{2,1,0:T(8,128)(2,1)} %shard_map.56.refs_1_), custom_call_target="tpu_custom_call", output_to_operand_aliasing={{}: (4, {})} | custom-call | tf_op jit(solution)/shard_map/pallas_call | solution.py:100
  69.7 19.5 %all_to_all.11 = bf16[16,64,256]{2,1,0:T(8,128)(2,1)S(1)} all-to-all(bf16[16,64,256]{2,1,0:T(8,128)(2,1)} %shard_map.57), channel_id=1, replica_groups=mesh['blk'=64,'head'=16] {'head'}, dimensions={0} | all-to-all | bytes 1048576 | tf_op jit(solution)/shard_map/all_to_all | solution.py:129
  89.3 0.8 copy.8
  (1 shorter events, 0.0 us)
Async XLA Ops:
  52.5 2.0 %copy-start = (bf16[16,3,64,256]{3,2,1,0:T(8,128)(2,1)}, bf16[16,3,64,256]{3,2,1,0:T(8,128)(2,1)S(1)}, u32[]{:S(2)}) copy-start(bf16[16,3,64,256]{3,2,1,0:T(8,128)(2,1)S(1)} %all_to_all.10.qkv_ref) | copy-start | bytes 4718596
  52.5 12.6 %collective-permute-start = (bf16[8,2,64,256]{3,2,1,0:T(8,128)(2,1)S(1)}, bf16[8,2,64,256]{3,2,1,0:T(8,128)(2,1)S(1)}, u32[]{:S(2)}, u32[]{:S(2)}) collective-permute-start(bf16[8,2,64,256]{3,2,1,0:T(8,128)(2,1)S(1)} %slice.4), channel_id=1, source_target_pairs={{0,16},{16,32},{32,48},{48,64},{64,80},{80,96},{96,112},{112,128},... | collective-permute-start | bytes 1572872 | tf_op jit(solution)/shard_map/ppermute | solution.py:19
  65.1 0.8 copy-start.1

commit v14 on v13

--- a/solution.py
+++ b/solution.py
@@ -11,6 +11,7 @@
 HDIM = 128
 BLOCK = 256
 CYCLE = 3
+LOG2E = 1.4426950408889634
 
 
 def from_behind(value, axis, steps):
@@ -60,10 +61,10 @@
                 v = jnp.concatenate(
                     (before_ref[halo, 1, :, cols].reshape(-1, HDIM), qkv_ref[own, 2, :, cols].reshape(-1, HDIM)), axis=0
                 )
-            s = lax.dot_general(q, k, (((1,), (1,)), ((), ())), preferred_element_type=jnp.float32) * scale
+            s = lax.dot_general(q, k, (((1,), (1,)), ((), ())), preferred_element_type=jnp.float32)
             s = jnp.where(allowed, s, -1e30)
             top = jnp.max(s, axis=1, keepdims=True)
-            w = jnp.exp(s - top)
+            w = jnp.exp2((s - top) * (scale * LOG2E))
             total = jnp.sum(w, axis=1, keepdims=True)
             summed = jnp.dot(w.astype(jnp.bfloat16), v, preferred_element_type=jnp.float32)
             result = (summed / total).astype(out_ref.dtype)

time: 90.5 us -> 90.4 us (level)
  no operation moved by 1% of the time
where the time goes in v14:
time: 90.4 us; the launch traced here: 90.1 us
  blocking collectives  69.4 us (77%)
  Pallas kernels  10.3 us (11%)
  waiting for transfers between devices  6.76 us (7%)
  starting transfers between devices  1.92 us (2%)
  local copies, waits for them, and re-layouts  1.66 us (2%)
    all_to_all x1, blocking collectives, body(): lax.all_to_all(qkv_out, 'head', split_axis=0, concat_axis=0, tiled=True)  49.8 us
    all_to_all x1, blocking collectives, body(): lax.all_to_all(joined, 'head', split_axis=0, concat_axis=0, tiled=True)  19.5 us
    pallas_call x2, Pallas kernels, attend(): pl.pallas_call(functools.partial(attention_kernel, blocks, before is not...  7.69 us
    ppermute x1, waiting for transfers between devices, from_behind(): lax.ppermute(value, axis, [(source, source + steps) for source in range(i...  6.76 us
    pallas_call x1, Pallas kernels, body(): pl.pallas_call(slab_kernel, out_shape=jax.ShapeDtypeStruct((peers, 3, chu...  2.63 us
    ppermute x1, starting transfers between devices, from_behind(): lax.ppermute(value, axis, [(source, source + steps) for source in range(i...  1.92 us
  transfers between devices with their start and end apart: 1, of which 1 were waited for; matrix products, arithmetic and copies ran while one was open for 0% of the time, Pallas kernels for 4%

profile of v14, /device:TPU:256, one launch (start us, length us, event | category | flops | bytes accessed | tf_op | source)
XLA Modules:
  0.0 90.1 jit_solution(5727186136438110326)
XLA Ops:
  0.0 2.6 %shard_map.55 = bf16[16,3,64,256]{3,2,1,0:T(8,128)(2,1)} custom-call(bf16[64,4096]{1,0:T(8,128)(2,1)} %q_ref.1, bf16[64,4096]{1,0:T(8,128)(2,1)} %k_ref.1, bf16[64,4096]{1,0:T(8,128)(2,1)} %v_ref.1), custom_call_target="tpu_custom_call" | custom-call | tf_op jit(solution)/shard_map/pallas_call | solution.py:118
  2.6 49.8 %all_to_all.10.qkv_ref = bf16[16,3,64,256]{3,2,1,0:T(8,128)(2,1)S(1)} all-to-all(bf16[16,3,64,256]{3,2,1,0:T(8,128)(2,1)} %shard_map.55), channel_id=1, replica_groups=mesh['blk'=64,'head'=16] {'head'}, dimensions={0} | all-to-all | bytes 3145728 | tf_op jit(solution)/shard_map/all_to_all | solution.py:124
  52.5 0.0 copy-start
  52.5 1.9 %collective-permute-start = (bf16[8,2,64,256]{3,2,1,0:T(8,128)(2,1)S(1)}, bf16[8,2,64,256]{3,2,1,0:T(8,128)(2,1)S(1)}, u32[]{:S(2)}, u32[]{:S(2)}) collective-permute-start(bf16[8,2,64,256]{3,2,1,0:T(8,128)(2,1)S(1)} %slice.4), channel_id=1, source_target_pairs={{0,16},{16,32},{32,48},{48,64},{64,80},{80,96},{96,112},{112,128},... | collective-permute-start | bytes 1572872 | tf_op jit(solution)/shard_map/ppermute | solution.py:20
  54.4 0.0 copy-done
  54.5 3.9 %shard_map.56.refs_1_ = bf16[16,64,256]{2,1,0:T(8,128)(2,1)} custom-call(s32[4,3]{1,0:T(4,128)} %lists_ref.3, s32[4]{0:T(128)} %counts_ref.3, bf16[16,3,64,256]{3,2,1,0:T(8,128)(2,1)} %copy-done), custom_call_target="tpu_custom_call" | custom-call | tf_op jit(solution)/shard_map/pallas_call | solution.py:101
  58.4 6.8 %collective-permute-done.refs_0_ = bf16[8,2,64,256]{3,2,1,0:T(8,128)(2,1)S(1)} collective-permute-done((bf16[8,2,64,256]{3,2,1,0:T(8,128)(2,1)S(1)}, bf16[8,2,64,256]{3,2,1,0:T(8,128)(2,1)S(1)}, u32[]{:S(2)}, u32[]{:S(2)}) %collective-permute-start) | collective-permute-done | bytes 524320 | tf_op jit(solution)/shard_map/ppermute | solution.py:20
  65.1 0.0 copy-start.1
  65.1 0.8 copy-done.1
  65.9 3.8 %shard_map.57 = bf16[16,64,256]{2,1,0:T(8,128)(2,1)} custom-call(s32[4,3]{1,0:T(4,128)} %lists_ref.3, s32[4]{0:T(128)} %counts_ref.3, bf16[16,3,64,256]{3,2,1,0:T(8,128)(2,1)} %copy-done, bf16[8,2,64,256]{3,2,1,0:T(8,128)(2,1)} %copy-done.1, bf16[16,64,256]{2,1,0:T(8,128)(2,1)} %shard_map.56.refs_1_), custom_call_target="tpu_custom_call", output_to_operand_aliasing={{}: (4, {})} | custom-call | tf_op jit(solution)/shard_map/pallas_call | solution.py:101
  69.7 19.5 %all_to_all.11 = bf16[16,64,256]{2,1,0:T(8,128)(2,1)S(1)} all-to-all(bf16[16,64,256]{2,1,0:T(8,128)(2,1)} %shard_map.57), channel_id=1, replica_groups=mesh['blk'=64,'head'=16] {'head'}, dimensions={0} | all-to-all | bytes 1048576 | tf_op jit(solution)/shard_map/all_to_all | solution.py:130
  89.2 0.8 copy.8
  (1 shorter events, 0.0 us)
Async XLA Ops:
  52.5 2.0 %copy-start = (bf16[16,3,64,256]{3,2,1,0:T(8,128)(2,1)}, bf16[16,3,64,256]{3,2,1,0:T(8,128)(2,1)S(1)}, u32[]{:S(2)}) copy-start(bf16[16,3,64,256]{3,2,1,0:T(8,128)(2,1)S(1)} %all_to_all.10.qkv_ref) | copy-start | bytes 4718596
  52.5 12.6 %collective-permute-start = (bf16[8,2,64,256]{3,2,1,0:T(8,128)(2,1)S(1)}, bf16[8,2,64,256]{3,2,1,0:T(8,128)(2,1)S(1)}, u32[]{:S(2)}, u32[]{:S(2)}) collective-permute-start(bf16[8,2,64,256]{3,2,1,0:T(8,128)(2,1)S(1)} %slice.4), channel_id=1, source_target_pairs={{0,16},{16,32},{32,48},{48,64},{64,80},{80,96},{96,112},{112,128},... | collective-permute-start | bytes 1572872 | tf_op jit(solution)/shard_map/ppermute | solution.py:20
  65.1 0.8 copy-start.1

commit v15 on v14

--- a/solution.py
+++ b/solution.py
@@ -34,15 +34,17 @@
     causal = (col_pos < reach * BLOCK) | (col_pos - reach * BLOCK <= row_pos)
     owned_blocks = counts_ref.shape[0]
     target = lax.axis_index("blk").astype(jnp.int32) * owned_blocks
+    key_place = lax.broadcasted_iota(jnp.int32, (1, CYCLE * BLOCK), 1) // BLOCK
     for local in blocks:
-        allowed = causal
+        column_ok = None
         for place in range(CYCLE):
-            inside = (col_pos >= place * BLOCK) & (col_pos < (place + 1) * BLOCK)
             wanted = None
             for entry in range(CYCLE):
                 hit = (counts_ref[local] > entry) & (lists_ref[local, entry] == target + local - (reach - place))
                 wanted = hit if wanted is None else wanted | hit
-            allowed = allowed & (jnp.logical_not(inside) | wanted)
+            here = (key_place == place) & wanted
+            column_ok = here if column_ok is None else column_ok | here
+        allowed = causal & column_ok
         rows = slice(local * per_block, (local + 1) * per_block)
         first = local - reach
         for head in range(local_heads):

time: 90.4 us -> 90.5 us (level)
  no operation moved by 1% of the time
where the time goes in v15:
time: 90.5 us; the launch traced here: 90.1 us
  blocking collectives  69.4 us (77%)
  Pallas kernels  10.3 us (11%)
  waiting for transfers between devices  6.77 us (7%)
  starting transfers between devices  1.92 us (2%)
  local copies, waits for them, and re-layouts  1.66 us (2%)
    all_to_all x1, blocking collectives, body(): lax.all_to_all(qkv_out, 'head', split_axis=0, concat_axis=0, tiled=True)  49.8 us
    all_to_all x1, blocking collectives, body(): lax.all_to_all(joined, 'head', split_axis=0, concat_axis=0, tiled=True)  19.5 us
    pallas_call x2, Pallas kernels, attend(): pl.pallas_call(functools.partial(attention_kernel, blocks, before is not...  7.68 us
    ppermute x1, waiting for transfers between devices, from_behind(): lax.ppermute(value, axis, [(source, source + steps) for source in range(i...  6.77 us
    pallas_call x1, Pallas kernels, body(): pl.pallas_call(slab_kernel, out_shape=jax.ShapeDtypeStruct((peers, 3, chu...  2.63 us
    ppermute x1, starting transfers between devices, from_behind(): lax.ppermute(value, axis, [(source, source + steps) for source in range(i...  1.92 us
  transfers between devices with their start and end apart: 1, of which 1 were waited for; matrix products, arithmetic and copies ran while one was open for 0% of the time, Pallas kernels for 4%

profile of v15, /device:TPU:256, one launch (start us, length us, event | category | flops | bytes accessed | tf_op | source)
XLA Modules:
  0.0 90.1 jit_solution(12301950514622719196)
XLA Ops:
  0.0 2.6 %shard_map.55 = bf16[16,3,64,256]{3,2,1,0:T(8,128)(2,1)} custom-call(bf16[64,4096]{1,0:T(8,128)(2,1)} %q_ref.1, bf16[64,4096]{1,0:T(8,128)(2,1)} %k_ref.1, bf16[64,4096]{1,0:T(8,128)(2,1)} %v_ref.1), custom_call_target="tpu_custom_call" | custom-call | tf_op jit(solution)/shard_map/pallas_call | solution.py:120
  2.6 49.8 %all_to_all.10.qkv_ref = bf16[16,3,64,256]{3,2,1,0:T(8,128)(2,1)S(1)} all-to-all(bf16[16,3,64,256]{3,2,1,0:T(8,128)(2,1)} %shard_map.55), channel_id=1, replica_groups=mesh['blk'=64,'head'=16] {'head'}, dimensions={0} | all-to-all | bytes 3145728 | tf_op jit(solution)/shard_map/all_to_all | solution.py:126
  52.5 0.0 copy-start
  52.5 1.9 %collective-permute-start = (bf16[8,2,64,256]{3,2,1,0:T(8,128)(2,1)S(1)}, bf16[8,2,64,256]{3,2,1,0:T(8,128)(2,1)S(1)}, u32[]{:S(2)}, u32[]{:S(2)}) collective-permute-start(bf16[8,2,64,256]{3,2,1,0:T(8,128)(2,1)S(1)} %slice.4), channel_id=1, source_target_pairs={{0,16},{16,32},{32,48},{48,64},{64,80},{80,96},{96,112},{112,128},... | collective-permute-start | bytes 1572872 | tf_op jit(solution)/shard_map/ppermute | solution.py:20
  54.4 0.0 copy-done
  54.5 3.9 %shard_map.56.refs_1_ = bf16[16,64,256]{2,1,0:T(8,128)(2,1)} custom-call(s32[4,3]{1,0:T(4,128)} %lists_ref.3, s32[4]{0:T(128)} %counts_ref.3, bf16[16,3,64,256]{3,2,1,0:T(8,128)(2,1)} %copy-done), custom_call_target="tpu_custom_call" | custom-call | tf_op jit(solution)/shard_map/pallas_call | solution.py:103
  58.4 6.8 %collective-permute-done.refs_0_ = bf16[8,2,64,256]{3,2,1,0:T(8,128)(2,1)S(1)} collective-permute-done((bf16[8,2,64,256]{3,2,1,0:T(8,128)(2,1)S(1)}, bf16[8,2,64,256]{3,2,1,0:T(8,128)(2,1)S(1)}, u32[]{:S(2)}, u32[]{:S(2)}) %collective-permute-start) | collective-permute-done | bytes 524320 | tf_op jit(solution)/shard_map/ppermute | solution.py:20
  65.1 0.0 copy-start.1
  65.1 0.8 copy-done.1
  65.9 3.8 %shard_map.57 = bf16[16,64,256]{2,1,0:T(8,128)(2,1)} custom-call(s32[4,3]{1,0:T(4,128)} %lists_ref.3, s32[4]{0:T(128)} %counts_ref.3, bf16[16,3,64,256]{3,2,1,0:T(8,128)(2,1)} %copy-done, bf16[8,2,64,256]{3,2,1,0:T(8,128)(2,1)} %copy-done.1, bf16[16,64,256]{2,1,0:T(8,128)(2,1)} %shard_map.56.refs_1_), custom_call_target="tpu_custom_call", output_to_operand_aliasing={{}: (4, {})} | custom-call | tf_op jit(solution)/shard_map/pallas_call | solution.py:103
  69.7 19.5 %all_to_all.11 = bf16[16,64,256]{2,1,0:T(8,128)(2,1)S(1)} all-to-all(bf16[16,64,256]{2,1,0:T(8,128)(2,1)} %shard_map.57), channel_id=1, replica_groups=mesh['blk'=64,'head'=16] {'head'}, dimensions={0} | all-to-all | bytes 1048576 | tf_op jit(solution)/shard_map/all_to_all | solution.py:132
  89.2 0.8 copy.8
  (1 shorter events, 0.0 us)
Async XLA Ops:
  52.5 2.0 %copy-start = (bf16[16,3,64,256]{3,2,1,0:T(8,128)(2,1)}, bf16[16,3,64,256]{3,2,1,0:T(8,128)(2,1)S(1)}, u32[]{:S(2)}) copy-start(bf16[16,3,64,256]{3,2,1,0:T(8,128)(2,1)S(1)} %all_to_all.10.qkv_ref) | copy-start | bytes 4718596
  52.5 12.6 %collective-permute-start = (bf16[8,2,64,256]{3,2,1,0:T(8,128)(2,1)S(1)}, bf16[8,2,64,256]{3,2,1,0:T(8,128)(2,1)S(1)}, u32[]{:S(2)}, u32[]{:S(2)}) collective-permute-start(bf16[8,2,64,256]{3,2,1,0:T(8,128)(2,1)S(1)} %slice.4), channel_id=1, source_target_pairs={{0,16},{16,32},{32,48},{48,64},{64,80},{80,96},{96,112},{112,128},... | collective-permute-start | bytes 1572872 | tf_op jit(solution)/shard_map/ppermute | solution.py:20
  65.1 0.8 copy-start.1
